TPU v7x, 256 devices: a whole 4x4x8 slice. The times are simulated.
256 devices in a mesh: wide: 64 (over y, z, core), seq: 4 (over x).
Axes of the slice: x: 4, y: 4, z: 8, core: 2. Of those that a mesh axis runs over, the one named last changes fastest.
Arguments:
- power: bfloat16 [160, 2097152], P('seq', 'wide')
- bin_index: int32 [160], P('seq'), may hold values from 0 to 7, as said below
- session: int32 [16384], replicated, may hold values from 0 to 63, as said below
- readin_weight: bfloat16 [64, 128, 2048], P('wide'), may hold values from -0.5 to 0.5
- qkv_weight: bfloat16 [2048, 1536], replicated, may hold values from -0.125 to 0.125
Outputs:
- heads: bfloat16 [16384, 8, 1024], P(('wide', 'seq'))
Inputs may be any that keep to these rules, and one draw needn't show every extreme that they name: `bin_index`: the samples j * 40 to (j + 1) * 40 - 1 name only bins j * 2 to (j + 1) * 2 - 1. In each aligned block of 64 patches (patches k * 64 to (k + 1) * 64 - 1) no session is named by more than 2 patches; one session, the same for every block, is named by exactly 2 patches of every block.
All inputs are finite; a program needn't handle non-finite values.
Results may differ from a plain program's by a relative error of at most 0.008.
Values may be sent and summed in bfloat16 or wider, within the bound.
No kernel may reach another device: no remote copies, remote signals or barrier semaphores. Data moves between devices by JAX's collectives and lax.ppermute only.
A program may use at most 64 MiB of HBM per device.

v0:
```python
import jax
import jax.numpy as jnp
from jax import lax
from jax.sharding import PartitionSpec as P

CH = 128
HD = 128
HEADS = 8
KVH = 2
SPB = 20


def attention_heads(qkv_rows):
    row_count = qkv_rows.shape[0]
    length = qkv_rows.shape[1]
    group_size = HEADS // KVH
    values = qkv_rows.astype(jnp.float32)
    queries = values[:, :, : HEADS * HD].reshape(row_count, length, KVH, group_size, HD)
    key_rows = values[:, :, HEADS * HD : (HEADS + KVH) * HD].reshape(row_count, length, KVH, HD)
    value_rows = values[:, :, (HEADS + KVH) * HD :].reshape(row_count, length, KVH, HD)
    queries = queries / jnp.sqrt(jnp.mean(queries * queries, axis=-1, keepdims=True) + 1e-06)
    key_rows = key_rows / jnp.sqrt(jnp.mean(key_rows * key_rows, axis=-1, keepdims=True) + 1e-06)
    scores = jnp.einsum("pigrd,pjgd->pgrij", queries, key_rows) / HD**0.5
    exponent = jnp.exp(scores)
    weights = (exponent / jnp.sum(exponent, axis=-1, keepdims=True)).astype(jnp.bfloat16)
    mixed = jnp.einsum("pgrij,pjgd->pigrd", weights.astype(jnp.float32), value_rows)
    return mixed.reshape(row_count, length, HEADS * HD).astype(jnp.bfloat16)


def project_rows(tokens, qkv_weight):
    product = jnp.dot(
        tokens.reshape(-1, tokens.shape[-1]), qkv_weight, preferred_element_type=jnp.float32
    )
    return product.astype(jnp.bfloat16).reshape(tokens.shape[:-1] + (qkv_weight.shape[1],))


def readin_rows(slab, weight_block):
    tokens = jnp.einsum(
        "abtc,cd->abtd", slab, weight_block, preferred_element_type=jnp.float32
    ).astype(jnp.bfloat16)
    return tokens


def slot_ranks(owner_ids, wide_count):
    owner_marks = (owner_ids[..., None] == jnp.arange(wide_count, dtype=jnp.int32)).astype(
        jnp.int32
    )
    running = jnp.cumsum(owner_marks, axis=-2)
    return jnp.sum(owner_marks * running, axis=-1) - 1


def body(power, bin_index, session, readin_weight, qkv_weight):
    wide_count = lax.axis_size("wide")
    seq_count = lax.axis_size("seq")
    wide_index = lax.axis_index("wide")
    seq_index = lax.axis_index("seq")
    sample_rows, channels = power.shape
    patch_count = channels // CH
    quarter = patch_count // seq_count
    bin_count = sample_rows // SPB
    capacity = max(2, 2 * quarter // wide_count)
    signal = power.astype(jnp.float32)
    squares = lax.psum(jnp.sum(signal * signal, axis=0), "seq")
    inv_rms = 1.0 / jnp.sqrt(squares / (sample_rows * seq_count) + 1e-06)
    active = jnp.maximum(signal * inv_rms[None, :] - 0.8, 0.0)
    local_bins = bin_index - seq_index * bin_count
    onehot = (local_bins[:, None] == jnp.arange(bin_count, dtype=jnp.int32)[None, :]).astype(
        jnp.float32
    )
    binned = (jnp.dot(onehot.T, active, precision=lax.Precision.HIGHEST) * (1.0 / SPB)).astype(
        jnp.bfloat16
    )
    patches = binned.reshape(bin_count, patch_count, CH).transpose(1, 0, 2)
    owners = lax.dynamic_slice_in_dim(session, wide_index * patch_count, patch_count)
    weight_block = readin_weight[0]
    owner_grid = owners.reshape(seq_count, quarter)
    slot_rank = slot_ranks(owner_grid, wide_count)
    quarter_ids = jnp.arange(seq_count, dtype=jnp.int32)[:, None]
    slot_index = ((owner_grid * seq_count + quarter_ids) * capacity + slot_rank).reshape(
        patch_count
    )
    slot_count = seq_count * capacity
    length = patches.shape[1]
    outgoing = (
        jnp.zeros((wide_count * slot_count, length, CH), jnp.bfloat16).at[slot_index].set(patches)
    )
    outgoing = outgoing.reshape(wide_count, slot_count, length, CH)
    returned_rows = lax.all_to_all(
        readin_rows(
            lax.all_to_all(outgoing, "wide", split_axis=0, concat_axis=0, tiled=True), weight_block
        ),
        "wide",
        split_axis=0,
        concat_axis=0,
        tiled=True,
    )
    arrived = returned_rows.reshape(
        wide_count * slot_count, returned_rows.shape[2], returned_rows.shape[3]
    )[slot_index]
    arrived = lax.all_to_all(arrived, "seq", split_axis=0, concat_axis=1, tiled=True)
    projected = project_rows(arrived, qkv_weight)
    return attention_heads(projected)


def solution(mesh):
    placed = (P("seq", "wide"), P("seq"), P(), P("wide", None, None), P())
    return jax.shard_map(
        body, mesh=mesh, in_specs=placed, out_specs=P(("wide", "seq"), None, None), check_vma=False
    )
```

profile of v0, /device:TPU:1, one launch (start us, length us, event | category | flops | bytes accessed | tf_op | source)
XLA Modules:
  0.0 287.6 jit_solution(8272917020949830205)
XLA Ops:
  6.5 0.0 copy-start
  6.5 0.0 copy-start.1
  6.5 0.0 copy-start.3
  6.5 0.0 all-reduce.2.cloned.1.call-start
  6.5 3.3 %fusion.1 = f32[32768]{0:T(1024)} fusion(bf16[40,32768]{1,0:T(8,128)(2,1)} %param.5), kind=kLoop, calls=%fused_computation.6 | loop fusion | flops 3899392 | bytes 2752512 | tf_op jit(solution)/shard_map/reduce_sum | solution.py:63
  9.8 0.0 all-reduce.2.cloned.1.call-update
  9.8 0.8 dynamic_slice.3
  10.6 0.1 eq.28
  10.7 0.1 add.58
  10.8 0.1 fusion.20
  10.9 0.1 reduce_window_sum.11
  11.0 0.2 select_reduce_fusion
  11.3 0.1 sub.17
  11.3 0.8 compare_select_fusion
  12.1 0.0 copy-done.3
  12.1 46.1 %all-reduce.2.cloned.1.call-done = f32[32768]{0:T(1024)} async-done(((f32[32768]{0:T(1024)}), f32[32768]{0:T(1024)}) %all-reduce.2.cloned.1.call-update) | async-done | bytes 131088 | tf_op jit(solution)/shard_map/psum | solution.py:63
  58.2 0.9 add_rsqrt_fusion
  59.2 0.0 copy-done.1
  59.2 2.5 fusion.11
  61.7 0.1 broadcast_in_dim.4
  61.8 7.3 %scatter_fusion = bf16[512,2,128]{2,1,0:T(2,128)(2,1)S(1)} fusion(bf16[512,2,128]{2,1,0:T(2,128)(2,1)S(1)} %broadcast_in_dim.4, s32[256]{0:T(256)S(1)} %compare_select_fusion, bf16[256,2,128]{2,1,0:T(2,128)(2,1)S(1)} %fusion.11), kind=kCustom, calls=%fused_computation.1 | custom fusion | bytes 394240 | tf_op jit(solution)/shard_map/scatter | solution.py:85
  69.1 24.5 %all_to_all.25 = bf16[64,8,2,128]{3,1,2,0:T(8,128)(2,1)S(1)} all-to-all(bf16[64,8,2,128]{3,1,2,0:T(8,128)(2,1)S(1)} %copy.33), channel_id=1, replica_groups=mesh['wide'=64,'seq'=4] {'wide'}, dimensions={0} | all-to-all | bytes 524288 | tf_op jit(solution)/shard_map/all_to_all | solution.py:90
  93.7 0.0 copy-done
  93.7 3.2 %convolution_convert_fusion = bf16[64,8,2,2048]{3,1,2,0:T(8,128)(2,1)} fusion(bf16[64,8,2,128]{3,1,2,0:T(8,128)(2,1)S(1)} %all_to_all.25, bf16[1,128,2048]{2,1,0:T(8,128)(2,1)S(1)} %copy-done), kind=kOutput, calls=%fused_computation.10 | convolution fusion | flops 538968064 | bytes 4980736 | tf_op jit(solution)/shard_map/abtc,cd->abtd/dot_general | solution.py:38
  96.9 6.2 %all-to-all-start.1 = ((bf16[64,8,2,2048]{3,1,2,0:T(8,128)(2,1)}), bf16[64,8,2,2048]{3,1,2,0:T(8,128)(2,1)}, u32[]{:S(2)}, u32[]{:S(2)}) async-start(bf16[64,8,2,2048]{3,1,2,0:T(8,128)(2,1)} %convolution_convert_fusion), calls=%async_computation.1 | async-start | bytes 8388608 | tf_op jit(solution)/shard_map/all_to_all | solution.py:88
  103.1 95.8 %all-to-all-done.1 = bf16[64,8,2,2048]{3,1,2,0:T(8,128)(2,1)} async-done(((bf16[64,8,2,2048]{3,1,2,0:T(8,128)(2,1)}), bf16[64,8,2,2048]{3,1,2,0:T(8,128)(2,1)}, u32[]{:S(2)}, u32[]{:S(2)}) %all-to-all-start.1) | async-done | bytes 4194336 | tf_op jit(solution)/shard_map/all_to_all | solution.py:88
  198.9 2.5 copy.50
  201.4 6.2 %copy.35 = bf16[512,2,2048]{2,1,0:T(2,128)(2,1)} copy(bf16[512,2,2048]{2,0,1:T(8,128)(2,1)S(1)} %bitcast.54) | data formatting | bytes 8388608 | tf_op jit(solution)/shard_map/reshape | solution.py:97
  207.7 12.7 %gather_fusion = bf16[256,2,2048]{2,1,0:T(2,128)(2,1)S(1)} fusion(bf16[512,2,2048]{2,1,0:T(2,128)(2,1)} %copy.35, s32[1024]{0:T(1024)S(1)} %pad_clamp_fusion), kind=kCustom, calls=%fused_computation | custom fusion | bytes 4195328 | tf_op jit(solution)/shard_map/gather | solution.py:97
  220.4 28.8 %all_to_all.26 = bf16[256,2,2048]{2,1,0:T(2,128)(2,1)S(1)} all-to-all(bf16[256,2,2048]{2,1,0:T(2,128)(2,1)S(1)} %gather_fusion), channel_id=1, replica_groups=mesh['wide'=64,'seq'=4] {'seq'}, dimensions={0} | all-to-all | bytes 4194304 | tf_op jit(solution)/shard_map/all_to_all | solution.py:100
  249.3 2.5 copy.51
  251.8 2.2 reshape.56
  254.0 8.0 %fusion.24 = (f32[64,8,1536]{2,1,0:T(8,128)S(1)}, bf16[64,8,1536]{2,1,0:T(8,128)(2,1)}) fusion(bf16[512,2048]{1,0:T(8,128)(2,1)} %reshape.56, bf16[2048,1536]{1,0:T(8,128)(2,1)} %param.9), kind=kOutput, calls=%fused_computation.48 | convolution fusion | flops 3222798336 | bytes 13107200 | tf_op jit(solution)/shard_map/dot_general | solution.py:31
  262.0 0.0 copy-start.2
  262.0 1.7 copy-done.2
  263.7 0.3 multiply_reduce_fusion.1
  264.0 0.1 copy.37
  264.1 0.1 copy.38
  264.2 1.5 slice.16
  265.6 0.8 multiply_reduce_fusion
  266.5 0.1 copy.39
  266.6 0.2 copy.40
  266.8 7.2 %fusion.9 = f32[64,2,8,8,4]{3,2,4,1,0:T(8,128)} fusion(f32[64,8,2,4,128]{4,1,3,2,0:T(8,128)S(1)} %bitcast.56, f32[64,8,2,4]{1,3,2,0:T(4,128)S(1)} %copy.40, f32[64,8,1536]{2,1,0:T(8,128)} %copy-done.2, f32[64,8,2]{1,2,0:T(2,128)S(1)} %copy.38), kind=kOutput, calls=%fused_computation.17 | convolution fusion | flops 9043968 | bytes 2772992 | tf_op jit(solution)/shard_map/pigrd,pjgd->pgrij/dot_general | solution.py:23
  274.0 2.7 copy.41
  276.7 0.1 bitcast_reduce_fusion
  276.8 0.1 fusion.18
  276.9 1.6 copy.42
  278.4 2.3 convolution_convert_fusion.2
  (7 shorter events, 0.1 us)
Async XLA Ops:
  6.5 87.1 %copy-start = (bf16[1,128,2048]{2,1,0:T(8,128)(2,1)S(1)}, bf16[1,128,2048]{2,1,0:T(8,128)(2,1)}, u32[]{:S(2)}) copy-start(bf16[1,128,2048]{2,1,0:T(8,128)(2,1)} %param.8) | copy-start | bytes 1572868
  6.5 52.6 %copy-start.1 = (bf16[40,32768]{1,0:T(8,128)(2,1)S(1)}, bf16[40,32768]{1,0:T(8,128)(2,1)}, u32[]{:S(2)}) copy-start(bf16[40,32768]{1,0:T(8,128)(2,1)} %param.5) | copy-start | bytes 7864324
  6.5 5.6 %copy-start.3 = (s32[40]{0:T(128)S(1)}, s32[40]{0:T(128)}, u32[]{:S(2)}) copy-start(s32[40]{0:T(128)} %param.6) | copy-start | bytes 484
  6.5 51.7 %all-reduce.2.cloned.1.call-start = ((), (), s32[]{:S(2)}) async-start(), calls=%async_computation.3 | async-start | bytes 262144 | tf_op jit(solution)/shard_map/psum | solution.py:63
  96.9 102.1 %all-to-all-start.1 = ((bf16[64,8,2,2048]{3,1,2,0:T(8,128)(2,1)}), bf16[64,8,2,2048]{3,1,2,0:T(8,128)(2,1)}, u32[]{:S(2)}, u32[]{:S(2)}) async-start(bf16[64,8,2,2048]{3,1,2,0:T(8,128)(2,1)} %convolution_convert_fusion), calls=%async_computation.1 | async-start | bytes 8388608 | tf_op jit(solution)/shard_map/all_to_all | solution.py:88
  262.0 1.7 copy-start.2
Sparse Core Ops, SparseCore 0:
  10.0 48.2 all-reduce.1
where the time goes:
time: 288 us
  waiting for transfers between devices  142 us (49%)
  blocking collectives  53.4 us (19%)
  local copies, waits for them, and re-layouts  42.5 us (15%)
  matrix products  23.3 us (8%)
  between operations  13.6 us (5%)
  other arithmetic  6.75 us (2%)
  starting transfers between devices  6.24 us (2%)
    all_to_all x1, waiting for transfers between devices, body(): lax.all_to_all(readin_rows(lax.all_to_all(outgoing, 'wide', split_axis=0,...  95.8 us
    psum x1, waiting for transfers between devices, body(): squares = lax.psum(jnp.sum(signal * signal, axis=0), 'seq')  46.1 us
    all_to_all x1, blocking collectives, body(): lax.all_to_all(arrived, 'seq', split_axis=0, concat_axis=1, tiled=True)  28.8 us
    all_to_all x1, blocking collectives, body(): lax.all_to_all(outgoing, 'wide', split_axis=0, concat_axis=0, tiled=True)  24.5 us
    gather x1, local copies, waits for them, and re-layouts, body(): returned_rows.reshape(wide_count * slot_count, returned_rows.shape[2], re...  12.7 us
    dot_general x1, matrix products, project_rows(): jnp.dot(tokens.reshape(-1, tokens.shape[-1]), qkv_weight, preferred_eleme...  8.04 us
    scatter x1, local copies, waits for them, and re-layouts, body(): jnp.zeros((wide_count * slot_count, length, CH), jnp.bfloat16)  7.27 us
    dot_general x1, matrix products, attention_heads(): scores = jnp.einsum('pigrd,pjgd->pgrij', queries, key_rows) / HD ** 0.5  7.2 us
  transfers between devices with their start and end apart: 2, of which 2 were waited for; matrix products, arithmetic and copies ran while one was open for 1% of the time, Pallas kernels for 0%

commit v1 on v0

v1 whole, which is shorter than its diff:
```python
import jax
import jax.numpy as jnp
from jax import lax
from jax.sharding import PartitionSpec as P

CH = 128
HD = 128
HEADS = 8
KVH = 2
SPB = 20
CAP = 2


def attention_heads(qkv_rows):
    row_count = qkv_rows.shape[0]
    length = qkv_rows.shape[1]
    group_size = HEADS // KVH
    values = qkv_rows.astype(jnp.float32)
    queries = values[:, :, : HEADS * HD].reshape(row_count, length, KVH, group_size, HD)
    key_rows = values[:, :, HEADS * HD : (HEADS + KVH) * HD].reshape(row_count, length, KVH, HD)
    value_rows = values[:, :, (HEADS + KVH) * HD :].reshape(row_count, length, KVH, HD)
    queries = queries / jnp.sqrt(jnp.mean(queries * queries, axis=-1, keepdims=True) + 1e-06)
    key_rows = key_rows / jnp.sqrt(jnp.mean(key_rows * key_rows, axis=-1, keepdims=True) + 1e-06)
    scores = jnp.einsum("pigrd,pjgd->pgrij", queries, key_rows) / HD**0.5
    exponent = jnp.exp(scores)
    weights = (exponent / jnp.sum(exponent, axis=-1, keepdims=True)).astype(jnp.bfloat16)
    mixed = jnp.einsum("pgrij,pjgd->pigrd", weights.astype(jnp.float32), value_rows)
    return mixed.reshape(row_count, length, HEADS * HD).astype(jnp.bfloat16)


def body(power, bin_index, session, readin_weight, qkv_weight):
    wide_count = lax.axis_size("wide")
    seq_count = lax.axis_size("seq")
    wide_index = lax.axis_index("wide")
    seq_index = lax.axis_index("seq")
    sample_rows, channels = power.shape
    patch_count = channels // CH
    quarter = patch_count // seq_count
    bin_count = sample_rows // SPB
    all_bins = bin_count * seq_count

    signal = power.astype(jnp.float32)
    partial = jnp.sum(signal * signal, axis=0)
    spread = jnp.broadcast_to(partial[None, :], (seq_count, channels))
    gathered = lax.all_to_all(spread, "seq", split_axis=0, concat_axis=0, tiled=True)
    squares = jnp.sum(gathered, axis=0)
    inv_rms = 1.0 / jnp.sqrt(squares / (sample_rows * seq_count) + 1e-06)
    active = jnp.maximum(signal * inv_rms[None, :] - 0.8, 0.0)
    local_bins = bin_index - seq_index * bin_count
    onehot = (local_bins[:, None] == jnp.arange(bin_count, dtype=jnp.int32)[None, :]).astype(
        jnp.float32
    )
    binned = (jnp.dot(onehot.T, active, precision=lax.Precision.HIGHEST) * (1.0 / SPB)).astype(
        jnp.bfloat16
    )
    binned = binned.reshape(bin_count, seq_count, quarter, CH).transpose(1, 0, 2, 3)
    binned = lax.all_to_all(binned, "seq", split_axis=0, concat_axis=0, tiled=True)
    block_rows = binned.reshape(all_bins, quarter, CH).transpose(1, 0, 2).reshape(
        quarter, all_bins * CH
    )

    block = wide_index * seq_count + seq_index
    owners = lax.dynamic_slice_in_dim(session, block * quarter, quarter)
    same = owners[:, None] == owners[None, :]
    earlier = jnp.arange(quarter)[None, :] < jnp.arange(quarter)[:, None]
    rank = jnp.sum((same & earlier).astype(jnp.int32), axis=1)
    slot = owners * CAP + rank
    slot_count = wide_count * CAP
    dispatch = (jnp.arange(slot_count, dtype=jnp.int32)[:, None] == slot[None, :]).astype(
        jnp.bfloat16
    )
    outgoing = jnp.dot(dispatch, block_rows, preferred_element_type=jnp.float32).astype(
        jnp.bfloat16
    )
    arrived = lax.all_to_all(outgoing, "wide", split_axis=0, concat_axis=0, tiled=True)
    weight_block = readin_weight[0]
    tokens = jnp.dot(
        arrived.reshape(slot_count * all_bins, CH), weight_block, preferred_element_type=jnp.float32
    ).astype(jnp.bfloat16)
    tokens = tokens.reshape(slot_count, all_bins * weight_block.shape[1])
    returned = lax.all_to_all(tokens, "wide", split_axis=0, concat_axis=0, tiled=True)
    mine = jnp.dot(dispatch.T, returned, preferred_element_type=jnp.float32).astype(jnp.bfloat16)
    mine = mine.reshape(quarter * all_bins, weight_block.shape[1])
    projected = jnp.dot(mine, qkv_weight, preferred_element_type=jnp.float32).astype(jnp.bfloat16)
    projected = projected.reshape(quarter, all_bins, qkv_weight.shape[1])
    return attention_heads(projected)


def solution(mesh):
    placed = (P("seq", "wide"), P("seq"), P(), P("wide", None, None), P())
    return jax.shard_map(
        body, mesh=mesh, in_specs=placed, out_specs=P(("wide", "seq"), None, None), check_vma=False
    )
```

time: 288 us -> 211 us (0.73)
  waiting for transfers between devices: 142 us -> 10.1 us
  blocking collectives: 53.4 us -> 130 us
  local copies, waits for them, and re-layouts: 42.5 us -> 28 us
  between operations: 13.6 us -> 0.16 us
  matrix products: 23.3 us -> 26.4 us
    all_to_all x1 -> x2, waiting for transfers between devices: 95.8 us -> 10.1 us  [the longest x1 6.1 us: body(): lax.all_to_all(spread, 'seq', split_axis=0, concat_axis=0, tiled=True)]
    all_to_all x1, blocking collectives: 28.8 us -> 102 us  [body(): lax.all_to_all(tokens, 'wide', split_axis=0, concat_axis=0, tiled=True)]
    psum x1 -> x0, waiting for transfers between devices: 46.1 us -> none  [body(): squares = lax.psum(jnp.sum(signal * signal, axis=0), 'seq')]
    gather x1 -> x0, local copies, waits for them, and re-layouts: 12.7 us -> none  [body(): returned_rows.reshape(wide_count * slot_count, returned_rows.shape[2], re...]
    all_to_all x2 -> x3, local copies, waits for them, and re-layouts: 4.95 us -> 15.1 us  [the longest x2 15 us: body(): lax.all_to_all(tokens, 'wide', split_axis=0, concat_axis=0, tiled=True)]
    scatter x1 -> x0, local copies, waits for them, and re-layouts: 7.27 us -> none  [body(): jnp.zeros((wide_count * slot_count, length, CH), jnp.bfloat16)]
    reshape x3, local copies, waits for them, and re-layouts: 8.52 us -> 3.22 us  [the longest x1 2.38 us: body(): mine = mine.reshape(quarter * all_bins, weight_block.shape[1])]
    all_to_all x1, blocking collectives: 24.5 us -> 28.1 us  [body(): lax.all_to_all(outgoing, 'wide', split_axis=0, concat_axis=0, tiled=True)]
where the time goes in v1:
time: 211 us; the launch traced here: 210 us
  blocking collectives  130 us (62%)
  local copies, waits for them, and re-layouts  28 us (13%)
  matrix products  26.4 us (13%)
  waiting for transfers between devices  10.1 us (5%)
  starting transfers between devices  8.16 us (4%)
  other arithmetic  6.43 us (3%)
    all_to_all x1, blocking collectives, body(): lax.all_to_all(tokens, 'wide', split_axis=0, concat_axis=0, tiled=True)  102 us
    all_to_all x1, blocking collectives, body(): lax.all_to_all(outgoing, 'wide', split_axis=0, concat_axis=0, tiled=True)  28.1 us
    all_to_all x2, local copies, waits for them, and re-layouts, body(): lax.all_to_all(tokens, 'wide', split_axis=0, concat_axis=0, tiled=True)  15 us
    dot_general x1, matrix products, body(): jnp.dot(mine, qkv_weight, preferred_element_type=jnp.float32)  8.04 us
    dot_general x1, matrix products, attention_heads(): scores = jnp.einsum('pigrd,pjgd->pgrij', queries, key_rows) / HD ** 0.5  7.2 us
    all_to_all x1, waiting for transfers between devices, body(): lax.all_to_all(spread, 'seq', split_axis=0, concat_axis=0, tiled=True)  6.1 us
    all_to_all x1, starting transfers between devices, body(): lax.all_to_all(spread, 'seq', split_axis=0, concat_axis=0, tiled=True)  4.83 us
  transfers between devices with their start and end apart: 2, of which 2 were waited for; matrix products, arithmetic and copies ran while one was open for 1% of the time, Pallas kernels for 0%

profile of v1, /device:TPU:1, one launch (start us, length us, event | category | flops | bytes accessed | tf_op | source)
XLA Modules:
  0.0 209.7 jit_solution(8894150965925539245)
XLA Ops:
  0.0 0.0 copy-start
  0.0 0.0 copy-start.1
  0.0 0.0 copy-start.3
  0.0 2.6 %fusion.1 = f32[32768]{0:T(1024)S(1)} fusion(bf16[40,32768]{1,0:T(8,128)(2,1)} %param.5), kind=kLoop, calls=%fused_computation.5 | loop fusion | flops 3899392 | bytes 2752512 | tf_op jit(solution)/shard_map/reduce_sum | solution.py:43
  2.6 1.1 broadcast_in_dim.2
  3.7 4.8 %all-to-all-start = ((f32[4,1,32768]{2,1,0:T(1,128)}), f32[4,1,32768]{2,1,0:T(1,128)}, u32[]{:S(2)}, u32[]{:S(2)}) async-start(f32[4,1,32768]{2,1,0:T(1,128)} %broadcast_in_dim.2), calls=%async_computation | async-start | bytes 1048576 | tf_op jit(solution)/shard_map/all_to_all | solution.py:45
  8.5 0.8 dynamic_slice.3
  9.3 0.2 convert_reduce_fusion
  9.5 0.0 copy-done.3
  9.5 6.1 %all-to-all-done = f32[4,1,32768]{2,1,0:T(1,128)} async-done(((f32[4,1,32768]{2,1,0:T(1,128)}), f32[4,1,32768]{2,1,0:T(1,128)}, u32[]{:S(2)}, u32[]{:S(2)}) %all-to-all-start) | async-done | bytes 524320 | tf_op jit(solution)/shard_map/all_to_all | solution.py:45
  15.6 1.5 reduce_sum.56
  17.2 0.0 copy-done.1
  17.2 2.5 %fusion.11 = bf16[1,2,256,128]{3,1,2,0:T(2,128)(2,1)S(1)} fusion(bf16[40,32768]{1,0:T(8,128)(2,1)S(1)} %copy-done.1, f32[32768]{0:T(1024)S(1)} %add_rsqrt_fusion, s32[40]{0:T(128)S(1)} %broadcast_subtract_fusion), kind=kOutput, calls=%fused_computation.19 | convolution fusion | flops 36831312 | bytes 2883744 | tf_op jit(solution)/shard_map/dot_general | solution.py:53
  19.7 0.7 copy.43
  20.3 3.3 %all-to-all-start.1 = ((bf16[4,2,64,128]{3,2,1,0:T(8,128)(2,1)}), bf16[4,2,64,128]{3,2,1,0:T(8,128)(2,1)S(1)}, u32[]{:S(2)}, u32[]{:S(2)}) async-start(bf16[4,2,64,128]{3,2,1,0:T(8,128)(2,1)} %bitcast.51), calls=%async_computation.1 | async-start | bytes 262144 | tf_op jit(solution)/shard_map/all_to_all | solution.py:57
  23.7 0.8 multiply_add_fusion
  24.5 4.0 %all-to-all-done.1 = bf16[4,2,64,128]{3,2,1,0:T(8,128)(2,1)S(1)} async-done(((bf16[4,2,64,128]{3,2,1,0:T(8,128)(2,1)}), bf16[4,2,64,128]{3,2,1,0:T(8,128)(2,1)S(1)}, u32[]{:S(2)}, u32[]{:S(2)}) %all-to-all-start.1) | async-done | bytes 131104 | tf_op jit(solution)/shard_map/all_to_all | solution.py:57
  28.5 0.2 convolution_convert_fusion.4
  28.7 0.1 all_to_all.23
  28.8 28.1 %all_to_all.32 = bf16[64,2,1024]{2,1,0:T(2,128)(2,1)S(1)} all-to-all(bf16[64,2,1024]{2,1,0:T(2,128)(2,1)S(1)} %all_to_all.23), channel_id=1, replica_groups=mesh['wide'=64,'seq'=4] {'wide'}, dimensions={0} | all-to-all | bytes 524288 | tf_op jit(solution)/shard_map/all_to_all | solution.py:75
  56.9 0.2 reshape.71
  57.1 0.0 copy-done
  57.1 3.2 %convolution_convert_fusion.1 = bf16[1024,2048]{1,0:T(8,128)(2,1)} fusion(bf16[1024,128]{1,0:T(8,128)(2,1)S(1)} %reshape.71, bf16[1,128,2048]{2,1,0:T(8,128)(2,1)S(1)} %copy-done), kind=kOutput, calls=%fused_computation.8 | convolution fusion | flops 538968064 | bytes 4980736 | tf_op jit(solution)/shard_map/dot_general | solution.py:77
  60.3 7.8 %all_to_all.25 = bf16[64,2,16384]{2,1,0:T(2,128)(2,1)} reshape(bf16[1024,2048]{1,0:T(8,128)(2,1)} %convolution_convert_fusion.1) | data formatting | bytes 8388608 | tf_op jit(solution)/shard_map/all_to_all | solution.py:81
  68.1 102.3 %all_to_all.33 = bf16[64,2,16384]{2,1,0:T(2,128)(2,1)} all-to-all(bf16[64,2,16384]{2,1,0:T(2,128)(2,1)} %all_to_all.25), channel_id=1, replica_groups=mesh['wide'=64,'seq'=4] {'wide'}, dimensions={0} | all-to-all | bytes 8388608 | tf_op jit(solution)/shard_map/all_to_all | solution.py:81
  170.4 7.2 %all_to_all.27 = bf16[128,16384]{1,0:T(8,128)(2,1)} reshape(bf16[64,2,16384]{2,1,0:T(2,128)(2,1)} %all_to_all.33) | data formatting | bytes 8388608 | tf_op jit(solution)/shard_map/all_to_all | solution.py:81
  177.6 2.9 %convolution_convert_fusion = bf16[64,16384]{1,0:T(8,128)(2,1)S(1)} fusion(bf16[128,16384]{1,0:T(8,128)(2,1)} %all_to_all.27, s32[64]{0:T(128)S(1)} %multiply_add_fusion), kind=kOutput, calls=%fused_computation.2 | convolution fusion | flops 269492224 | bytes 6291712 | tf_op jit(solution)/shard_map/dot_general | solution.py:82
  180.6 2.4 %reshape.72 = bf16[512,2048]{1,0:T(8,128)(2,1)} reshape(bf16[64,16384]{1,0:T(8,128)(2,1)S(1)} %convolution_convert_fusion) | data formatting | bytes 4194304 | tf_op jit(solution)/shard_map/reshape | solution.py:83
  182.9 8.0 %fusion.28 = (f32[64,8,1536]{2,1,0:T(8,128)S(1)}, bf16[64,8,1536]{2,1,0:T(8,128)(2,1)}) fusion(bf16[512,2048]{1,0:T(8,128)(2,1)} %reshape.72, bf16[2048,1536]{1,0:T(8,128)(2,1)} %param.9), kind=kOutput, calls=%fused_computation.50 | convolution fusion | flops 3222798336 | bytes 13107200 | tf_op jit(solution)/shard_map/dot_general | solution.py:84
  191.0 0.0 copy-start.2
  191.0 1.7 copy-done.2
  192.6 0.3 multiply_reduce_fusion.1
  192.9 0.1 copy.27
  193.0 0.1 copy.28
  193.1 1.5 slice.14
  194.6 0.8 multiply_reduce_fusion
  195.4 0.1 copy.29
  195.6 0.2 copy.30
  195.7 7.2 %fusion.9 = f32[64,2,8,8,4]{3,2,4,1,0:T(8,128)} fusion(f32[64,8,2,4,128]{4,1,3,2,0:T(8,128)S(1)} %bitcast.53, f32[64,8,2,4]{1,3,2,0:T(4,128)S(1)} %copy.30, f32[64,8,1536]{2,1,0:T(8,128)} %copy-done.2, f32[64,8,2]{1,2,0:T(2,128)S(1)} %copy.28), kind=kOutput, calls=%fused_computation.14 | convolution fusion | flops 9043968 | bytes 2772992 | tf_op jit(solution)/shard_map/pigrd,pjgd->pgrij/dot_general | solution.py:24
  203.0 2.7 %copy.31 = f32[64,2,8,8,4]{0,2,3,4,1:T(8,128)S(1)} copy(f32[64,2,8,8,4]{3,2,4,1,0:T(8,128)} %fusion.9) | data formatting | bytes 262144 | tf_op jit(solution)/shard_map/pigrd,pjgd->pgrij/dot_general | solution.py:24
  205.6 0.1 bitcast_reduce_fusion
  205.7 0.1 fusion.18
  205.8 1.6 copy.32
  207.4 2.3 %convolution_convert_fusion.3 = bf16[64,2,128,4,8]{2,4,3,1,0:T(8,128)(2,1)} fusion(bf16[64,2,4,8,8]{4,3,2,1,0:T(8,128)(2,1)S(1)} %copy.32, bf16[64,8,1536]{2,1,0:T(8,128)(2,1)} %get-tuple-element.6), kind=kOutput, calls=%fused_computation.17 | convolution fusion | flops 8912896 | bytes 1376256 | tf_op jit(solution)/shard_map/pgrij,pjgd->pigrd/dot_general | solution.py:27
  (5 shorter events, 0.1 us)
Async XLA Ops:
  0.0 57.1 %copy-start = (bf16[1,128,2048]{2,1,0:T(8,128)(2,1)S(1)}, bf16[1,128,2048]{2,1,0:T(8,128)(2,1)}, u32[]{:S(2)}) copy-start(bf16[1,128,2048]{2,1,0:T(8,128)(2,1)} %param.8) | copy-start | bytes 1572868
  0.0 17.2 %copy-start.1 = (bf16[40,32768]{1,0:T(8,128)(2,1)S(1)}, bf16[40,32768]{1,0:T(8,128)(2,1)}, u32[]{:S(2)}) copy-start(bf16[40,32768]{1,0:T(8,128)(2,1)} %param.5) | copy-start | bytes 7864324
  0.0 9.5 %copy-start.3 = (s32[40]{0:T(128)S(1)}, s32[40]{0:T(128)}, u32[]{:S(2)}) copy-start(s32[40]{0:T(128)} %param.6) | copy-start | bytes 484
  3.7 11.9 %all-to-all-start = ((f32[4,1,32768]{2,1,0:T(1,128)}), f32[4,1,32768]{2,1,0:T(1,128)}, u32[]{:S(2)}, u32[]{:S(2)}) async-start(f32[4,1,32768]{2,1,0:T(1,128)} %broadcast_in_dim.2), calls=%async_computation | async-start | bytes 1048576 | tf_op jit(solution)/shard_map/all_to_all | solution.py:45
  20.3 8.1 %all-to-all-start.1 = ((bf16[4,2,64,128]{3,2,1,0:T(8,128)(2,1)}), bf16[4,2,64,128]{3,2,1,0:T(8,128)(2,1)S(1)}, u32[]{:S(2)}, u32[]{:S(2)}) async-start(bf16[4,2,64,128]{3,2,1,0:T(8,128)(2,1)} %bitcast.51), calls=%async_computation.1 | async-start | bytes 262144 | tf_op jit(solution)/shard_map/all_to_all | solution.py:57
  191.0 1.7 copy-start.2

commit v2 on v1

--- a/solution.py
+++ b/solution.py
@@ -77,13 +77,15 @@
     tokens = jnp.dot(
         arrived.reshape(slot_count * all_bins, CH), weight_block, preferred_element_type=jnp.float32
     ).astype(jnp.bfloat16)
-    tokens = tokens.reshape(slot_count, all_bins * weight_block.shape[1])
-    returned = lax.all_to_all(tokens, "wide", split_axis=0, concat_axis=0, tiled=True)
+    projected = jnp.dot(tokens, qkv_weight, preferred_element_type=jnp.float32).astype(jnp.bfloat16)
+    projected = projected.reshape(slot_count, all_bins, qkv_weight.shape[1])
+    heads = attention_heads(projected)
+    width = heads.shape[2]
+    returned = lax.all_to_all(
+        heads.reshape(slot_count, all_bins * width), "wide", split_axis=0, concat_axis=0, tiled=True
+    )
     mine = jnp.dot(dispatch.T, returned, preferred_element_type=jnp.float32).astype(jnp.bfloat16)
-    mine = mine.reshape(quarter * all_bins, weight_block.shape[1])
-    projected = jnp.dot(mine, qkv_weight, preferred_element_type=jnp.float32).astype(jnp.bfloat16)
-    projected = projected.reshape(quarter, all_bins, qkv_weight.shape[1])
-    return attention_heads(projected)
+    return mine.reshape(quarter, all_bins, width)
 
 
 def solution(mesh):

time: 211 us -> 168 us (0.80)
  blocking collectives: 130 us -> 85.5 us
  local copies, waits for them, and re-layouts: 28 us -> 22.1 us
  matrix products: 26.4 us -> 32.2 us
  other arithmetic: 6.43 us -> 8.58 us
    all_to_all x1, blocking collectives: 102 us -> 57.3 us  [body(): lax.all_to_all(heads.reshape(slot_count, all_bins * width), 'wide', split...]
    all_to_all x2 -> x1, local copies, waits for them, and re-layouts: 15 us -> 2.74 us  [body(): lax.all_to_all(heads.reshape(slot_count, all_bins * width), 'wide', split...]
    dot_general x1, matrix products: 7.2 us -> 14 us  [attention_heads(): scores = jnp.einsum('pigrd,pjgd->pgrij', queries, key_rows) / HD ** 0.5]
    convert_element_type x0 -> x2, local copies, waits for them, and re-layouts: none -> 3.28 us  [attention_heads(): return mixed.reshape(row_count, length, HEADS * HD).astype(jnp.bfloat16)]
    dot_general x1, matrix products: 2.94 us -> 0.49 us  [body(): jnp.dot(dispatch.T, returned, preferred_element_type=jnp.float32)]
    reshape x1 -> x0, local copies, waits for them, and re-layouts: 2.38 us -> none  [body(): mine = mine.reshape(quarter * all_bins, weight_block.shape[1])]
    dot_general x2 -> x1, matrix products: 11.2 us -> 13.3 us  [body(): jnp.dot(tokens, qkv_weight, preferred_element_type=jnp.float32)]
where the time goes in v2:
time: 168 us; the launch traced here: 167 us
  blocking collectives  85.5 us (51%)
  matrix products  32.2 us (19%)
  local copies, waits for them, and re-layouts  22.1 us (13%)
  waiting for transfers between devices  10.1 us (6%)
  other arithmetic  8.58 us (5%)
  starting transfers between devices  8.16 us (5%)
    all_to_all x1, blocking collectives, body(): lax.all_to_all(heads.reshape(slot_count, all_bins * width), 'wide', split...  57.3 us
    all_to_all x1, blocking collectives, body(): lax.all_to_all(outgoing, 'wide', split_axis=0, concat_axis=0, tiled=True)  28.1 us
    dot_general x1, matrix products, attention_heads(): scores = jnp.einsum('pigrd,pjgd->pgrij', queries, key_rows) / HD ** 0.5  14 us
    dot_general x1, matrix products, body(): jnp.dot(tokens, qkv_weight, preferred_element_type=jnp.float32)  13.3 us
    all_to_all x1, waiting for transfers between devices, body(): lax.all_to_all(spread, 'seq', split_axis=0, concat_axis=0, tiled=True)  6.1 us
    all_to_all x1, starting transfers between devices, body(): lax.all_to_all(spread, 'seq', split_axis=0, concat_axis=0, tiled=True)  4.83 us
    all_to_all x1, waiting for transfers between devices, body(): lax.all_to_all(binned, 'seq', split_axis=0, concat_axis=0, tiled=True)  4.02 us
    dot_general x1, local copies, waits for them, and re-layouts, attention_heads(): scores = jnp.einsum('pigrd,pjgd->pgrij', queries, key_rows) / HD ** 0.5  3.79 us
  transfers between devices with their start and end apart: 2, of which 2 were waited for; matrix products, arithmetic and copies ran while one was open for 1% of the time, Pallas kernels for 0%

profile of v2, /device:TPU:1, one launch (start us, length us, event | category | flops | bytes accessed | tf_op | source)
XLA Modules:
  0.0 166.8 jit_solution(675307456164153466)
XLA Ops:
  0.0 0.0 copy-start
  0.0 0.0 copy-start.2
  0.0 0.0 copy-start.3
  0.0 2.6 %fusion.1 = f32[32768]{0:T(1024)S(1)} fusion(bf16[40,32768]{1,0:T(8,128)(2,1)} %param.5), kind=kLoop, calls=%fused_computation.5 | loop fusion | flops 3899392 | bytes 2752512 | tf_op jit(solution)/shard_map/reduce_sum | solution.py:43
  2.6 1.1 broadcast_in_dim.2
  3.7 4.8 %all-to-all-start = ((f32[4,1,32768]{2,1,0:T(1,128)}), f32[4,1,32768]{2,1,0:T(1,128)}, u32[]{:S(2)}, u32[]{:S(2)}) async-start(f32[4,1,32768]{2,1,0:T(1,128)} %broadcast_in_dim.2), calls=%async_computation | async-start | bytes 1048576 | tf_op jit(solution)/shard_map/all_to_all | solution.py:45
  8.5 0.8 dynamic_slice.3
  9.3 0.2 convert_reduce_fusion
  9.5 0.0 copy-done.3
  9.5 6.1 %all-to-all-done = f32[4,1,32768]{2,1,0:T(1,128)} async-done(((f32[4,1,32768]{2,1,0:T(1,128)}), f32[4,1,32768]{2,1,0:T(1,128)}, u32[]{:S(2)}, u32[]{:S(2)}) %all-to-all-start) | async-done | bytes 524320 | tf_op jit(solution)/shard_map/all_to_all | solution.py:45
  15.6 1.5 reduce_sum.56
  17.2 0.0 copy-done.2
  17.2 2.5 %fusion.21 = bf16[1,2,256,128]{3,1,2,0:T(2,128)(2,1)S(1)} fusion(bf16[40,32768]{1,0:T(8,128)(2,1)S(1)} %copy-done.2, f32[32768]{0:T(1024)S(1)} %add_rsqrt_fusion, s32[40]{0:T(128)S(1)} %broadcast_subtract_fusion), kind=kOutput, calls=%fused_computation.22 | convolution fusion | flops 36831312 | bytes 2883744 | tf_op jit(solution)/shard_map/dot_general | solution.py:53
  19.7 0.7 copy.49
  20.3 3.3 %all-to-all-start.1 = ((bf16[4,2,64,128]{3,2,1,0:T(8,128)(2,1)}), bf16[4,2,64,128]{3,2,1,0:T(8,128)(2,1)S(1)}, u32[]{:S(2)}, u32[]{:S(2)}) async-start(bf16[4,2,64,128]{3,2,1,0:T(8,128)(2,1)} %bitcast.54), calls=%async_computation.1 | async-start | bytes 262144 | tf_op jit(solution)/shard_map/all_to_all | solution.py:57
  23.7 0.8 multiply_add_fusion
  24.5 4.0 %all-to-all-done.1 = bf16[4,2,64,128]{3,2,1,0:T(8,128)(2,1)S(1)} async-done(((bf16[4,2,64,128]{3,2,1,0:T(8,128)(2,1)}), bf16[4,2,64,128]{3,2,1,0:T(8,128)(2,1)S(1)}, u32[]{:S(2)}, u32[]{:S(2)}) %all-to-all-start.1) | async-done | bytes 131104 | tf_op jit(solution)/shard_map/all_to_all | solution.py:57
  28.5 0.2 convolution_convert_fusion.1
  28.7 0.1 all_to_all.21
  28.8 28.1 %all_to_all.29 = bf16[64,2,1024]{2,1,0:T(2,128)(2,1)S(1)} all-to-all(bf16[64,2,1024]{2,1,0:T(2,128)(2,1)S(1)} %all_to_all.21), channel_id=1, replica_groups=mesh['wide'=64,'seq'=4] {'wide'}, dimensions={0} | all-to-all | bytes 524288 | tf_op jit(solution)/shard_map/all_to_all | solution.py:75
  56.9 0.2 reshape.72
  57.1 0.0 copy-done
  57.1 13.3 %fusion.38 = (f32[128,8,1536]{2,1,0:T(8,128)}, bf16[128,8,1536]{2,1,0:T(8,128)(2,1)}) fusion(bf16[2048,1536]{1,0:T(8,128)(2,1)} %param.9, bf16[1024,128]{1,0:T(8,128)(2,1)S(1)} %reshape.72, bf16[1,128,2048]{2,1,0:T(8,128)(2,1)S(1)} %copy-done), kind=kOutput, calls=%fused_computation.52 | convolution fusion | flops 6984564736 | bytes 16515072 | tf_op jit(solution)/shard_map/dot_general | solution.py:80
  70.4 1.6 multiply_reduce_fusion.1
  72.1 0.1 copy.31
  72.1 0.2 copy.32
  72.3 2.0 %slice.14 = f32[128,8,1024]{2,1,0:T(8,128)S(1)} slice(bf16[128,8,1536]{2,1,0:T(8,128)(2,1)} %get-tuple-element.6), slice={[0:128], [0:8], [0:1024]} | slice | bytes 8388608 | tf_op jit(solution)/shard_map/slice | solution.py:19
  74.4 0.0 copy-start.1
  74.4 2.0 %copy-done.1 = f32[128,8,1024]{2,1,0:T(8,128)} copy-done((f32[128,8,1024]{2,1,0:T(8,128)}, f32[128,8,1024]{2,1,0:T(8,128)S(1)}, u32[]{:S(2)}) %copy-start.1) | copy-done | bytes 4194328
  76.4 1.6 multiply_reduce_fusion
  78.0 0.2 copy.33
  78.3 0.3 copy.34
  78.5 14.0 %fusion.5 = f32[128,2,8,8,4]{3,2,4,1,0:T(8,128)} fusion(f32[128,8,2,4,128]{4,1,3,2,0:T(8,128)} %bitcast.56, f32[128,8,2,4]{1,3,2,0:T(4,128)S(1)} %copy.34, f32[128,8,1536]{2,1,0:T(8,128)} %get-tuple-element.5, f32[128,8,2]{1,2,0:T(2,128)S(1)} %copy.32), kind=kOutput, calls=%fused_computation.8 | convolution fusion | flops 18087936 | bytes 5545984 | tf_op jit(solution)/shard_map/pigrd,pjgd->pgrij/dot_general | solution.py:24
  92.5 3.8 %copy.35 = f32[128,2,8,8,4]{0,2,3,4,1:T(8,128)S(1)} copy(f32[128,2,8,8,4]{3,2,4,1,0:T(8,128)} %fusion.5) | data formatting | bytes 524288 | tf_op jit(solution)/shard_map/pigrd,pjgd->pgrij/dot_general | solution.py:24
  96.3 0.1 bitcast_reduce_fusion
  96.4 0.1 fusion.29
  96.5 3.2 %copy.36 = bf16[128,2,4,8,8]{4,3,2,1,0:T(8,128)(2,1)S(1)} copy(bf16[128,2,4,8,8]{0,4,3,2,1:T(8,128)(2,1)S(1)} %fusion.29) | data formatting | bytes 262144 | tf_op jit(solution)/shard_map/convert_element_type | solution.py:26
  99.7 1.7 %convert_bitcast_fusion = bf16[128,8,2,4,128]{4,1,3,2,0:T(8,128)(2,1)S(1)} fusion(bf16[128,2,4,8,8]{4,3,2,1,0:T(8,128)(2,1)S(1)} %copy.36, bf16[128,8,1536]{2,1,0:T(8,128)(2,1)} %get-tuple-element.6), kind=kOutput, calls=%fused_computation.19 | convolution fusion | flops 17825792 | bytes 2752512 | tf_op jit(solution)/shard_map/pgrij,pjgd->pigrd/dot_general | solution.py:27
  101.4 1.2 copy.37
  102.6 2.1 %convert_element_type.51 = bf16[64,2,8192]{2,1,0:T(2,128)(2,1)} reshape(bf16[128,8,2,4,128]{4,3,2,1,0:T(4,128)(2,1)S(1)} %copy.37) | data formatting | bytes 4194304 | tf_op jit(solution)/shard_map/convert_element_type | solution.py:28
  104.7 57.3 %all_to_all.30 = bf16[64,2,8192]{2,1,0:T(2,128)(2,1)} all-to-all(bf16[64,2,8192]{2,1,0:T(2,128)(2,1)} %convert_element_type.51), channel_id=1, replica_groups=mesh['wide'=64,'seq'=4] {'wide'}, dimensions={0} | all-to-all | bytes 4194304 | tf_op jit(solution)/shard_map/all_to_all | solution.py:84
  162.0 2.7 %all_to_all.24 = bf16[128,8192]{1,0:T(8,128)(2,1)S(1)} reshape(bf16[64,2,8192]{2,1,0:T(2,128)(2,1)} %all_to_all.30) | data formatting | bytes 4194304 | tf_op jit(solution)/shard_map/all_to_all | solution.py:84
  164.8 0.5 convolution_convert_fusion
  165.3 1.6 copy.43
  (5 shorter events, 0.1 us)
Async XLA Ops:
  0.0 57.1 %copy-start = (bf16[1,128,2048]{2,1,0:T(8,128)(2,1)S(1)}, bf16[1,128,2048]{2,1,0:T(8,128)(2,1)}, u32[]{:S(2)}) copy-start(bf16[1,128,2048]{2,1,0:T(8,128)(2,1)} %param.8) | copy-start | bytes 1572868
  0.0 17.2 %copy-start.2 = (bf16[40,32768]{1,0:T(8,128)(2,1)S(1)}, bf16[40,32768]{1,0:T(8,128)(2,1)}, u32[]{:S(2)}) copy-start(bf16[40,32768]{1,0:T(8,128)(2,1)} %param.5) | copy-start | bytes 7864324
  0.0 9.5 %copy-start.3 = (s32[40]{0:T(128)S(1)}, s32[40]{0:T(128)}, u32[]{:S(2)}) copy-start(s32[40]{0:T(128)} %param.6) | copy-start | bytes 484
  3.7 11.9 %all-to-all-start = ((f32[4,1,32768]{2,1,0:T(1,128)}), f32[4,1,32768]{2,1,0:T(1,128)}, u32[]{:S(2)}, u32[]{:S(2)}) async-start(f32[4,1,32768]{2,1,0:T(1,128)} %broadcast_in_dim.2), calls=%async_computation | async-start | bytes 1048576 | tf_op jit(solution)/shard_map/all_to_all | solution.py:45
  20.3 8.1 %all-to-all-start.1 = ((bf16[4,2,64,128]{3,2,1,0:T(8,128)(2,1)}), bf16[4,2,64,128]{3,2,1,0:T(8,128)(2,1)S(1)}, u32[]{:S(2)}, u32[]{:S(2)}) async-start(bf16[4,2,64,128]{3,2,1,0:T(8,128)(2,1)} %bitcast.54), calls=%async_computation.1 | async-start | bytes 262144 | tf_op jit(solution)/shard_map/all_to_all | solution.py:57
  74.4 2.0 %copy-start.1 = (f32[128,8,1024]{2,1,0:T(8,128)}, f32[128,8,1024]{2,1,0:T(8,128)S(1)}, u32[]{:S(2)}) copy-start(f32[128,8,1024]{2,1,0:T(8,128)S(1)} %slice.14) | copy-start | bytes 12582916

commit v3 on v2

--- a/solution.py
+++ b/solution.py
@@ -1,6 +1,7 @@
 import jax
 import jax.numpy as jnp
 from jax import lax
+from jax.experimental import pallas as pl
 from jax.sharding import PartitionSpec as P
 
 CH = 128
@@ -9,6 +10,46 @@
 KVH = 2
 SPB = 20
 CAP = 2
+ROWS = 128
+
+
+def _attention_kernel(x_ref, o_ref):
+    rows = x_ref.shape[0]
+    length = 8
+    row_patch = lax.broadcasted_iota(jnp.int32, (rows, rows), 0) // length
+    col_patch = lax.broadcasted_iota(jnp.int32, (rows, rows), 1) // length
+    same = row_patch == col_patch
+    group_size = HEADS // KVH
+    for g in range(KVH):
+        k = x_ref[:, (HEADS + g) * HD : (HEADS + g + 1) * HD].astype(jnp.float32)
+        k = k / jnp.sqrt(jnp.mean(k * k, axis=-1, keepdims=True) + 1e-06)
+        v = x_ref[:, (HEADS + KVH + g) * HD : (HEADS + KVH + g + 1) * HD]
+        for r in range(group_size):
+            h = g * group_size + r
+            q = x_ref[:, h * HD : (h + 1) * HD].astype(jnp.float32)
+            q = q / jnp.sqrt(jnp.mean(q * q, axis=-1, keepdims=True) + 1e-06)
+            s = lax.dot_general(
+                q, k, (((1,), (1,)), ((), ())), precision=lax.Precision.HIGHEST,
+                preferred_element_type=jnp.float32,
+            ) / HD**0.5
+            e = jnp.where(same, jnp.exp(s), 0.0)
+            w = (e / jnp.sum(e, axis=-1, keepdims=True)).astype(jnp.bfloat16)
+            o = jnp.dot(w, v, preferred_element_type=jnp.float32)
+            o_ref[:, h * HD : (h + 1) * HD] = o.astype(jnp.bfloat16)
+
+
+def attention_kernel(qkv_rows):
+    count, length, width = qkv_rows.shape
+    flat = qkv_rows.reshape(count * length, width)
+    total = count * length
+    out = pl.pallas_call(
+        _attention_kernel,
+        out_shape=jax.ShapeDtypeStruct((total, HEADS * HD), jnp.bfloat16),
+        grid=(total // ROWS,),
+        in_specs=[pl.BlockSpec((ROWS, width), lambda i: (i, 0))],
+        out_specs=pl.BlockSpec((ROWS, HEADS * HD), lambda i: (i, 0)),
+    )(flat)
+    return out.reshape(count, length, HEADS * HD)
 
 
 def attention_heads(qkv_rows):
@@ -74,12 +115,15 @@
     )
     arrived = lax.all_to_all(outgoing, "wide", split_axis=0, concat_axis=0, tiled=True)
     weight_block = readin_weight[0]
-    tokens = jnp.dot(
-        arrived.reshape(slot_count * all_bins, CH), weight_block, preferred_element_type=jnp.float32
-    ).astype(jnp.bfloat16)
-    projected = jnp.dot(tokens, qkv_weight, preferred_element_type=jnp.float32).astype(jnp.bfloat16)
-    projected = projected.reshape(slot_count, all_bins, qkv_weight.shape[1])
-    heads = attention_heads(projected)
+    merged = jnp.dot(weight_block, qkv_weight, preferred_element_type=jnp.float32)
+    merged_hi = merged.astype(jnp.bfloat16)
+    merged_lo = (merged - merged_hi.astype(jnp.float32)).astype(jnp.bfloat16)
+    rows = arrived.reshape(slot_count * all_bins, CH)
+    projected = jnp.dot(rows, merged_hi, preferred_element_type=jnp.float32) + jnp.dot(
+        rows, merged_lo, preferred_element_type=jnp.float32
+    )
+    projected = projected.astype(jnp.bfloat16).reshape(slot_count, all_bins, qkv_weight.shape[1])
+    heads = attention_kernel(projected)
     width = heads.shape[2]
     returned = lax.all_to_all(
         heads.reshape(slot_count, all_bins * width), "wide", split_axis=0, concat_axis=0, tiled=True

time: 168 us -> 158 us (0.940)
  Pallas kernels: 0 us -> 30.2 us
  blocking collectives: 85.5 us -> 57.1 us
  matrix products: 32.2 us -> 10.6 us
  starting transfers between devices: 8.16 us -> 24.5 us
  local copies, waits for them, and re-layouts: 22.1 us -> 11.1 us
  waiting for transfers between devices: 10.1 us -> 17.6 us
  other arithmetic: 8.58 us -> 5.79 us
    pallas_call x0 -> x1, Pallas kernels: none -> 30.2 us  [attention_kernel(): pl.pallas_call(_attention_kernel, out_shape=jax.ShapeDtypeStruct((total,...]
    all_to_all x1 -> x0, blocking collectives: 28.1 us -> none  [body(): lax.all_to_all(outgoing, 'wide', split_axis=0, concat_axis=0, tiled=True)]
    dot_general x3, matrix products: 29 us -> 7.37 us  [the longest x1 3.77 us: body(): jnp.dot(weight_block, qkv_weight, preferred_element_type=jnp.float32)]
    all_to_all x0 -> x1, starting transfers between devices: none -> 16.4 us  [body(): lax.all_to_all(outgoing, 'wide', split_axis=0, concat_axis=0, tiled=True)]
    all_to_all x0 -> x1, waiting for transfers between devices: none -> 8.17 us  [body(): lax.all_to_all(outgoing, 'wide', split_axis=0, concat_axis=0, tiled=True)]
    convert_element_type x3 -> x0, local copies, waits for them, and re-layouts: 6.45 us -> none  [the longest x2 3.28 us: attention_heads(): return mixed.reshape(row_count, length, HEADS * HD).astype(jnp.bfloat16)]
    dot_general x1 -> x0, local copies, waits for them, and re-layouts: 3.79 us -> none  [attention_heads(): scores = jnp.einsum('pigrd,pjgd->pgrij', queries, key_rows) / HD ** 0.5]
    reduce_sum x3 -> x0, other arithmetic: 3.33 us -> none  [the longest x1 1.64 us: attention_heads(): jnp.mean(key_rows * key_rows, axis=-1, keepdims=True) + 1e-06]
  transfers between devices with their start and end apart: 2 -> 3, of which waited for: 2 -> 3; matrix products, arithmetic and copies ran while one was open for 1% -> 4% of each run, Pallas kernels for 0% -> 0%
where the time goes in v3:
time: 158 us; the launch traced here: 157 us
  blocking collectives  57.1 us (36%)
  Pallas kernels  30.2 us (19%)
  starting transfers between devices  24.5 us (16%)
  waiting for transfers between devices  17.6 us (11%)
  local copies, waits for them, and re-layouts  11.1 us (7%)
  matrix products  10.6 us (7%)
  other arithmetic  5.79 us (4%)
    all_to_all x1, blocking collectives, body(): lax.all_to_all(heads.reshape(slot_count, all_bins * width), 'wide', split...  57.1 us
    pallas_call x1, Pallas kernels, attention_kernel(): pl.pallas_call(_attention_kernel, out_shape=jax.ShapeDtypeStruct((total,...  30.2 us
    all_to_all x1, starting transfers between devices, body(): lax.all_to_all(outgoing, 'wide', split_axis=0, concat_axis=0, tiled=True)  16.4 us
    all_to_all x1, waiting for transfers between devices, body(): lax.all_to_all(outgoing, 'wide', split_axis=0, concat_axis=0, tiled=True)  8.17 us
    all_to_all x2, local copies, waits for them, and re-layouts, body(): lax.all_to_all(heads.reshape(slot_count, all_bins * width), 'wide', split...  6.04 us
    all_to_all x1, waiting for transfers between devices, body(): lax.all_to_all(spread, 'seq', split_axis=0, concat_axis=0, tiled=True)  5.45 us
    all_to_all x1, starting transfers between devices, body(): lax.all_to_all(spread, 'seq', split_axis=0, concat_axis=0, tiled=True)  4.83 us
    all_to_all x1, waiting for transfers between devices, body(): lax.all_to_all(binned, 'seq', split_axis=0, concat_axis=0, tiled=True)  4.02 us
  transfers between devices with their start and end apart: 3, of which 3 were waited for; matrix products, arithmetic and copies ran while one was open for 4% of the time, Pallas kernels for 0%

profile of v3, /device:TPU:1, one launch (start us, length us, event | category | flops | bytes accessed | tf_op | source)
XLA Modules:
  0.0 157.0 jit_solution(7162280598718381982)
XLA Ops:
  0.0 0.0 copy-start
  0.0 0.0 copy-start.1
  0.0 2.6 %fusion.1 = f32[32768]{0:T(1024)S(1)} fusion(bf16[40,32768]{1,0:T(8,128)(2,1)} %param.5), kind=kLoop, calls=%fused_computation.6 | loop fusion | flops 3899392 | bytes 2752512 | tf_op jit(solution)/shard_map/reduce_sum | solution.py:84
  2.6 1.1 broadcast_in_dim.2
  3.7 4.8 %all-to-all-start = ((f32[4,1,32768]{2,1,0:T(1,128)}), f32[4,1,32768]{2,1,0:T(1,128)}, u32[]{:S(2)}, u32[]{:S(2)}) async-start(f32[4,1,32768]{2,1,0:T(1,128)} %broadcast_in_dim.2), calls=%async_computation | async-start | bytes 1048576 | tf_op jit(solution)/shard_map/all_to_all | solution.py:86
  8.5 0.8 dynamic_slice.3
  9.3 0.2 convert_reduce_fusion
  9.5 0.7 broadcast_subtract_fusion
  10.1 5.5 %all-to-all-done = f32[4,1,32768]{2,1,0:T(1,128)} async-done(((f32[4,1,32768]{2,1,0:T(1,128)}), f32[4,1,32768]{2,1,0:T(1,128)}, u32[]{:S(2)}, u32[]{:S(2)}) %all-to-all-start) | async-done | bytes 524320 | tf_op jit(solution)/shard_map/all_to_all | solution.py:86
  15.6 1.5 reduce_sum.29
  17.1 0.0 copy-done.1
  17.2 2.5 %fusion.8 = bf16[1,2,256,128]{3,1,2,0:T(2,128)(2,1)S(1)} fusion(bf16[40,32768]{1,0:T(8,128)(2,1)S(1)} %copy-done.1, f32[32768]{0:T(1024)S(1)} %add_rsqrt_fusion, s32[40]{0:T(128)S(1)} %broadcast_subtract_fusion), kind=kOutput, calls=%fused_computation.13 | convolution fusion | flops 36831312 | bytes 2883744 | tf_op jit(solution)/shard_map/dot_general | solution.py:94
  19.7 0.7 copy.22
  20.3 3.3 %all-to-all-start.1 = ((bf16[4,2,64,128]{3,2,1,0:T(8,128)(2,1)}), bf16[4,2,64,128]{3,2,1,0:T(8,128)(2,1)S(1)}, u32[]{:S(2)}, u32[]{:S(2)}) async-start(bf16[4,2,64,128]{3,2,1,0:T(8,128)(2,1)} %bitcast.22), calls=%async_computation.1 | async-start | bytes 262144 | tf_op jit(solution)/shard_map/all_to_all | solution.py:98
  23.7 0.8 multiply_add_fusion
  24.4 4.0 %all-to-all-done.1 = bf16[4,2,64,128]{3,2,1,0:T(8,128)(2,1)S(1)} async-done(((bf16[4,2,64,128]{3,2,1,0:T(8,128)(2,1)}), bf16[4,2,64,128]{3,2,1,0:T(8,128)(2,1)S(1)}, u32[]{:S(2)}, u32[]{:S(2)}) %all-to-all-start.1) | async-done | bytes 131104 | tf_op jit(solution)/shard_map/all_to_all | solution.py:98
  28.5 0.2 convolution_convert_fusion.1
  28.7 0.8 all_to_all.23
  29.5 16.4 %all-to-all-start.2 = ((bf16[64,2,1024]{2,1,0:T(2,128)(2,1)}), bf16[64,2,1024]{2,1,0:T(2,128)(2,1)S(1)}, u32[]{:S(2)}, u32[]{:S(2)}) async-start(bf16[64,2,1024]{2,1,0:T(2,128)(2,1)} %all_to_all.23), calls=%async_computation.2 | async-start | bytes 524288 | tf_op jit(solution)/shard_map/all_to_all | solution.py:116
  45.8 0.0 copy-done
  45.9 3.8 %fusion.11 = f32[128,1536]{1,0:T(8,128)S(1)} fusion(bf16[2048,1536]{1,0:T(8,128)(2,1)} %param.9, bf16[1,128,2048]{2,1,0:T(8,128)(2,1)S(1)} %copy-done), kind=kOutput, calls=%fused_computation.15 | convolution fusion | flops 805306368 | bytes 7602176 | tf_op jit(solution)/shard_map/dot_general | solution.py:118
  49.6 8.2 %all-to-all-done.2 = bf16[64,2,1024]{2,1,0:T(2,128)(2,1)S(1)} async-done(((bf16[64,2,1024]{2,1,0:T(2,128)(2,1)}), bf16[64,2,1024]{2,1,0:T(2,128)(2,1)S(1)}, u32[]{:S(2)}, u32[]{:S(2)}) %all-to-all-start.2) | async-done | bytes 262176 | tf_op jit(solution)/shard_map/all_to_all | solution.py:116
  57.8 0.2 reshape.39
  58.0 1.0 fusion.14
  59.0 2.6 %add_convert_fusion.x_ref = bf16[1024,1536]{1,0:T(8,128)(2,1)} fusion(f32[1024,1536]{1,0:T(8,128)S(1)} %fusion.14, bf16[1024,128]{1,0:T(8,128)(2,1)S(1)} %reshape.39, f32[128,1536]{1,0:T(8,128)S(1)} %fusion.11), kind=kOutput, calls=%fused_computation.5 | convolution fusion | flops 406585344 | bytes 10485760 | tf_op jit(solution)/shard_map/dot_general | solution.py:122
  61.6 30.2 %shard_map.55 = bf16[1024,1024]{1,0:T(8,128)(2,1)} custom-call(bf16[1024,1536]{1,0:T(8,128)(2,1)} %add_convert_fusion.x_ref), custom_call_target="tpu_custom_call" | custom-call | tf_op jit(solution)/shard_map/pallas_call | solution.py:45
  91.8 3.3 %all_to_all.25 = bf16[64,2,8192]{2,1,0:T(2,128)(2,1)S(1)} reshape(bf16[1024,1024]{1,0:T(8,128)(2,1)} %shard_map.55) | data formatting | bytes 4194304 | tf_op jit(solution)/shard_map/all_to_all | solution.py:128
  95.1 57.1 %all_to_all.32 = bf16[64,2,8192]{2,1,0:T(2,128)(2,1)} all-to-all(bf16[64,2,8192]{2,1,0:T(2,128)(2,1)S(1)} %all_to_all.25), channel_id=1, replica_groups=mesh['wide'=64,'seq'=4] {'wide'}, dimensions={0} | all-to-all | bytes 4194304 | tf_op jit(solution)/shard_map/all_to_all | solution.py:128
  152.2 2.7 %all_to_all.27 = bf16[128,8192]{1,0:T(8,128)(2,1)S(1)} reshape(bf16[64,2,8192]{2,1,0:T(2,128)(2,1)} %all_to_all.32) | data formatting | bytes 4194304 | tf_op jit(solution)/shard_map/all_to_all | solution.py:128
  155.0 0.5 convolution_convert_fusion
  155.5 1.6 copy.16
  (2 shorter events, 0.0 us)
Async XLA Ops:
  0.0 45.8 %copy-start = (bf16[1,128,2048]{2,1,0:T(8,128)(2,1)S(1)}, bf16[1,128,2048]{2,1,0:T(8,128)(2,1)}, u32[]{:S(2)}) copy-start(bf16[1,128,2048]{2,1,0:T(8,128)(2,1)} %param.8) | copy-start | bytes 1572868
  0.0 17.1 %copy-start.1 = (bf16[40,32768]{1,0:T(8,128)(2,1)S(1)}, bf16[40,32768]{1,0:T(8,128)(2,1)}, u32[]{:S(2)}) copy-start(bf16[40,32768]{1,0:T(8,128)(2,1)} %param.5) | copy-start | bytes 7864324
  3.7 11.9 %all-to-all-start = ((f32[4,1,32768]{2,1,0:T(1,128)}), f32[4,1,32768]{2,1,0:T(1,128)}, u32[]{:S(2)}, u32[]{:S(2)}) async-start(f32[4,1,32768]{2,1,0:T(1,128)} %broadcast_in_dim.2), calls=%async_computation | async-start | bytes 1048576 | tf_op jit(solution)/shard_map/all_to_all | solution.py:86
  20.3 8.1 %all-to-all-start.1 = ((bf16[4,2,64,128]{3,2,1,0:T(8,128)(2,1)}), bf16[4,2,64,128]{3,2,1,0:T(8,128)(2,1)S(1)}, u32[]{:S(2)}, u32[]{:S(2)}) async-start(bf16[4,2,64,128]{3,2,1,0:T(8,128)(2,1)} %bitcast.22), calls=%async_computation.1 | async-start | bytes 262144 | tf_op jit(solution)/shard_map/all_to_all | solution.py:98
  29.5 28.3 %all-to-all-start.2 = ((bf16[64,2,1024]{2,1,0:T(2,128)(2,1)}), bf16[64,2,1024]{2,1,0:T(2,128)(2,1)S(1)}, u32[]{:S(2)}, u32[]{:S(2)}) async-start(bf16[64,2,1024]{2,1,0:T(2,128)(2,1)} %all_to_all.23), calls=%async_computation.2 | async-start | bytes 524288 | tf_op jit(solution)/shard_map/all_to_all | solution.py:116

commit v4 on v2

--- a/solution.py
+++ b/solution.py
@@ -1,6 +1,7 @@
 import jax
 import jax.numpy as jnp
 from jax import lax
+from jax.experimental import pallas as pl
 from jax.sharding import PartitionSpec as P
 
 CH = 128
@@ -9,23 +10,65 @@
 KVH = 2
 SPB = 20
 CAP = 2
+BINS = 8
+ROWS = 128
+SUB = 4
 
 
-def attention_heads(qkv_rows):
-    row_count = qkv_rows.shape[0]
-    length = qkv_rows.shape[1]
+def _weights_kernel(x_ref, o_ref):
     group_size = HEADS // KVH
-    values = qkv_rows.astype(jnp.float32)
-    queries = values[:, :, : HEADS * HD].reshape(row_count, length, KVH, group_size, HD)
-    key_rows = values[:, :, HEADS * HD : (HEADS + KVH) * HD].reshape(row_count, length, KVH, HD)
-    value_rows = values[:, :, (HEADS + KVH) * HD :].reshape(row_count, length, KVH, HD)
-    queries = queries / jnp.sqrt(jnp.mean(queries * queries, axis=-1, keepdims=True) + 1e-06)
-    key_rows = key_rows / jnp.sqrt(jnp.mean(key_rows * key_rows, axis=-1, keepdims=True) + 1e-06)
-    scores = jnp.einsum("pigrd,pjgd->pgrij", queries, key_rows) / HD**0.5
-    exponent = jnp.exp(scores)
-    weights = (exponent / jnp.sum(exponent, axis=-1, keepdims=True)).astype(jnp.bfloat16)
-    mixed = jnp.einsum("pgrij,pjgd->pigrd", weights.astype(jnp.float32), value_rows)
-    return mixed.reshape(row_count, length, HEADS * HD).astype(jnp.bfloat16)
+    sub_rows = SUB * BINS
+    cols = SUB * group_size * BINS
+    row_patch = lax.broadcasted_iota(jnp.int32, (sub_rows, cols), 0) // BINS
+    col_patch = lax.broadcasted_iota(jnp.int32, (sub_rows, cols), 1) // (group_size * BINS)
+    same = row_patch == col_patch
+    for sg in range(x_ref.shape[0] // sub_rows):
+        base = sg * sub_rows
+        xs = x_ref[base : base + sub_rows, :].astype(jnp.float32)
+        for g in range(KVH):
+            k = xs[:, (HEADS + g) * HD : (HEADS + g + 1) * HD]
+            k = k / jnp.sqrt(jnp.mean(k * k, axis=-1, keepdims=True) + 1e-06)
+            pieces = []
+            for p in range(SUB):
+                for r in range(group_size):
+                    h = g * group_size + r
+                    pieces.append(xs[p * BINS : (p + 1) * BINS, h * HD : (h + 1) * HD])
+            q = jnp.concatenate(pieces, axis=0)
+            q = q / jnp.sqrt(jnp.mean(q * q, axis=-1, keepdims=True) + 1e-06)
+            s = lax.dot_general(
+                k, q, (((1,), (1,)), ((), ())), precision=lax.Precision.HIGHEST,
+                preferred_element_type=jnp.float32,
+            ) / HD**0.5
+            e = jnp.where(same, jnp.exp(s), 0.0)
+            w = (e / jnp.sum(e, axis=0, keepdims=True)).astype(jnp.bfloat16).astype(jnp.float32)
+            width = group_size * BINS
+            for p in range(SUB):
+                tile = w[p * BINS : (p + 1) * BINS, :]
+                compact = tile[:, 0:width]
+                for c in range(1, SUB):
+                    compact = compact + tile[:, c * width : (c + 1) * width]
+                row0 = base + p * BINS
+                o_ref[row0 : row0 + BINS, g * width : (g + 1) * width] = compact
+
+
+def attention_weights(qkv_flat):
+    total, width = qkv_flat.shape
+    return pl.pallas_call(
+        _weights_kernel,
+        out_shape=jax.ShapeDtypeStruct((total, HEADS * BINS), jnp.float32),
+        grid=(total // ROWS,),
+        in_specs=[pl.BlockSpec((ROWS, width), lambda i: (i, 0))],
+        out_specs=pl.BlockSpec((ROWS, HEADS * BINS), lambda i: (i, 0)),
+    )(qkv_flat)
+
+
+def heads_from(weights, values):
+    n = weights.shape[0]
+    group_size = HEADS // KVH
+    w = weights.reshape(n, BINS, KVH, group_size, BINS)
+    v = values.reshape(n, BINS, KVH, HD)
+    mixed = jnp.einsum("pjgri,pjge->pigre", w, v, preferred_element_type=jnp.float32)
+    return mixed.reshape(n, BINS, HEADS * HD).astype(jnp.bfloat16)
 
 
 def body(power, bin_index, session, readin_weight, qkv_weight):
@@ -74,18 +117,25 @@
     )
     arrived = lax.all_to_all(outgoing, "wide", split_axis=0, concat_axis=0, tiled=True)
     weight_block = readin_weight[0]
-    tokens = jnp.dot(
-        arrived.reshape(slot_count * all_bins, CH), weight_block, preferred_element_type=jnp.float32
-    ).astype(jnp.bfloat16)
-    projected = jnp.dot(tokens, qkv_weight, preferred_element_type=jnp.float32).astype(jnp.bfloat16)
-    projected = projected.reshape(slot_count, all_bins, qkv_weight.shape[1])
-    heads = attention_heads(projected)
-    width = heads.shape[2]
-    returned = lax.all_to_all(
-        heads.reshape(slot_count, all_bins * width), "wide", split_axis=0, concat_axis=0, tiled=True
+    merged = jnp.dot(weight_block, qkv_weight, preferred_element_type=jnp.float32)
+    merged_hi = merged.astype(jnp.bfloat16)
+    merged_lo = (merged - merged_hi.astype(jnp.float32)).astype(jnp.bfloat16)
+    rows = arrived.reshape(slot_count * all_bins, CH)
+    projected = jnp.dot(rows, merged_hi, preferred_element_type=jnp.float32) + jnp.dot(
+        rows, merged_lo, preferred_element_type=jnp.float32
     )
+    projected = projected.astype(jnp.bfloat16).reshape(slot_count, all_bins, qkv_weight.shape[1])
+    weights = attention_weights(projected.reshape(slot_count * all_bins, qkv_weight.shape[1]))
+    weights = weights.astype(jnp.bfloat16).reshape(slot_count, all_bins * HEADS * BINS)
+    values = projected[:, :, (HEADS + KVH) * HD :].reshape(slot_count, all_bins * KVH * HD)
+    payload = jnp.concatenate([values, weights], axis=1)
+    returned = lax.all_to_all(payload, "wide", split_axis=0, concat_axis=0, tiled=True)
     mine = jnp.dot(dispatch.T, returned, preferred_element_type=jnp.float32).astype(jnp.bfloat16)
-    return mine.reshape(quarter, all_bins, width)
+    split = all_bins * KVH * HD
+    return heads_from(
+        mine[:, split:].reshape(quarter, all_bins, HEADS * BINS),
+        mine[:, :split].reshape(quarter, all_bins, KVH * HD),
+    )
 
 
 def solution(mesh):

time: 168 us -> 107 us (0.64)
  blocking collectives: 85.5 us -> 25.9 us
  matrix products: 32.2 us -> 11.7 us
  starting transfers between devices: 8.16 us -> 24.5 us
  local copies, waits for them, and re-layouts: 22.1 us -> 7.03 us
  Pallas kernels: 0 us -> 11.6 us
  waiting for transfers between devices: 10.1 us -> 17.7 us
    all_to_all x2 -> x1, blocking collectives: 85.5 us -> 25.9 us  [body(): lax.all_to_all(payload, 'wide', split_axis=0, concat_axis=0, tiled=True)]
    dot_general x3, matrix products: 29 us -> 7.37 us  [the longest x1 3.77 us: body(): jnp.dot(weight_block, qkv_weight, preferred_element_type=jnp.float32)]
    all_to_all x0 -> x1, starting transfers between devices: none -> 16.4 us  [body(): lax.all_to_all(outgoing, 'wide', split_axis=0, concat_axis=0, tiled=True)]
    pallas_call x0 -> x1, Pallas kernels: none -> 11.6 us  [attention_weights(): pl.pallas_call(_weights_kernel, out_shape=jax.ShapeDtypeStruct((total, HE...]
    all_to_all x0 -> x1, waiting for transfers between devices: none -> 8.18 us  [body(): lax.all_to_all(outgoing, 'wide', split_axis=0, concat_axis=0, tiled=True)]
    convert_element_type x3 -> x0, local copies, waits for them, and re-layouts: 6.45 us -> none  [the longest x2 3.28 us: attention_heads(): return mixed.reshape(row_count, length, HEADS * HD).astype(jnp.bfloat16)]
    dot_general x1 -> x0, local copies, waits for them, and re-layouts: 3.79 us -> none  [attention_heads(): scores = jnp.einsum('pigrd,pjgd->pgrij', queries, key_rows) / HD ** 0.5]
    unnamed x10 -> x5, local copies, waits for them, and re-layouts: 3.64 us -> 0.03 us
  transfers between devices with their start and end apart: 2 -> 3, of which waited for: 2 -> 3; matrix products, arithmetic and copies ran while one was open for 1% -> 6% of each run, Pallas kernels for 0% -> 0%
where the time goes in v4:
time: 107 us; the launch traced here: 106 us
  blocking collectives  25.9 us (24%)
  starting transfers between devices  24.5 us (23%)
  waiting for transfers between devices  17.7 us (17%)
  matrix products  11.7 us (11%)
  Pallas kernels  11.6 us (11%)
  other arithmetic  7.44 us (7%)
  local copies, waits for them, and re-layouts  7.03 us (7%)
    all_to_all x1, blocking collectives, body(): lax.all_to_all(payload, 'wide', split_axis=0, concat_axis=0, tiled=True)  25.9 us
    all_to_all x1, starting transfers between devices, body(): lax.all_to_all(outgoing, 'wide', split_axis=0, concat_axis=0, tiled=True)  16.4 us
    pallas_call x1, Pallas kernels, attention_weights(): pl.pallas_call(_weights_kernel, out_shape=jax.ShapeDtypeStruct((total, HE...  11.6 us
    all_to_all x1, waiting for transfers between devices, body(): lax.all_to_all(outgoing, 'wide', split_axis=0, concat_axis=0, tiled=True)  8.18 us
    all_to_all x1, waiting for transfers between devices, body(): lax.all_to_all(spread, 'seq', split_axis=0, concat_axis=0, tiled=True)  5.45 us
    all_to_all x1, starting transfers between devices, body(): lax.all_to_all(spread, 'seq', split_axis=0, concat_axis=0, tiled=True)  4.83 us
    all_to_all x1, waiting for transfers between devices, body(): lax.all_to_all(binned, 'seq', split_axis=0, concat_axis=0, tiled=True)  4.02 us
    dot_general x1, matrix products, body(): jnp.dot(weight_block, qkv_weight, preferred_element_type=jnp.float32)  3.77 us
  transfers between devices with their start and end apart: 3, of which 3 were waited for; matrix products, arithmetic and copies ran while one was open for 6% of the time, Pallas kernels for 0%

profile of v4, /device:TPU:1, one launch (start us, length us, event | category | flops | bytes accessed | tf_op | source)
XLA Modules:
  0.0 106.0 jit_solution(8175409660769463300)
XLA Ops:
  0.0 0.0 copy-start
  0.0 0.0 copy-start.1
  0.0 2.6 %fusion.1 = f32[32768]{0:T(1024)S(1)} fusion(bf16[40,32768]{1,0:T(8,128)(2,1)} %param.5), kind=kLoop, calls=%fused_computation.5 | loop fusion | flops 3899392 | bytes 2752512 | tf_op jit(solution)/shard_map/reduce_sum | solution.py:86
  2.6 1.1 %broadcast_in_dim.2 = f32[4,1,32768]{2,1,0:T(1,128)} broadcast(f32[32768]{0:T(1024)S(1)} %fusion.1), dimensions={2} | broadcast | bytes 655360 | tf_op jit(solution)/shard_map/broadcast_in_dim | solution.py:87
  3.7 4.8 %all-to-all-start = ((f32[4,1,32768]{2,1,0:T(1,128)}), f32[4,1,32768]{2,1,0:T(1,128)}, u32[]{:S(2)}, u32[]{:S(2)}) async-start(f32[4,1,32768]{2,1,0:T(1,128)} %broadcast_in_dim.2), calls=%async_computation | async-start | bytes 1048576 | tf_op jit(solution)/shard_map/all_to_all | solution.py:88
  8.5 0.8 dynamic_slice.3
  9.3 0.2 convert_reduce_fusion
  9.5 0.7 broadcast_subtract_fusion
  10.1 5.5 %all-to-all-done = f32[4,1,32768]{2,1,0:T(1,128)} async-done(((f32[4,1,32768]{2,1,0:T(1,128)}), f32[4,1,32768]{2,1,0:T(1,128)}, u32[]{:S(2)}, u32[]{:S(2)}) %all-to-all-start) | async-done | bytes 524320 | tf_op jit(solution)/shard_map/all_to_all | solution.py:88
  15.6 1.5 %reduce_sum.29 = f32[32768]{0:T(1024)S(1)} reduce(f32[4,1,32768]{2,1,0:T(1,128)} %all-to-all-done, f32[]{:T(128)} %constant.10.clone.1), dimensions={0,1}, to_apply=%region_2.0 | reduce | flops 98304 | bytes 655364 | tf_op jit(solution)/shard_map/reduce_sum | solution.py:89
  17.1 0.0 copy-done.1
  17.2 2.5 %fusion.8 = bf16[1,2,256,128]{3,1,2,0:T(2,128)(2,1)S(1)} fusion(bf16[40,32768]{1,0:T(8,128)(2,1)S(1)} %copy-done.1, f32[32768]{0:T(1024)S(1)} %add_rsqrt_fusion, s32[40]{0:T(128)S(1)} %broadcast_subtract_fusion), kind=kOutput, calls=%fused_computation.14 | convolution fusion | flops 36831312 | bytes 2883744 | tf_op jit(solution)/shard_map/dot_general | solution.py:96
  19.7 0.7 copy.34
  20.3 3.3 %all-to-all-start.1 = ((bf16[4,2,64,128]{3,2,1,0:T(8,128)(2,1)}), bf16[4,2,64,128]{3,2,1,0:T(8,128)(2,1)S(1)}, u32[]{:S(2)}, u32[]{:S(2)}) async-start(bf16[4,2,64,128]{3,2,1,0:T(8,128)(2,1)} %bitcast.32), calls=%async_computation.1 | async-start | bytes 262144 | tf_op jit(solution)/shard_map/all_to_all | solution.py:100
  23.7 0.8 multiply_add_fusion
  24.4 4.0 %all-to-all-done.1 = bf16[4,2,64,128]{3,2,1,0:T(8,128)(2,1)S(1)} async-done(((bf16[4,2,64,128]{3,2,1,0:T(8,128)(2,1)}), bf16[4,2,64,128]{3,2,1,0:T(8,128)(2,1)S(1)}, u32[]{:S(2)}, u32[]{:S(2)}) %all-to-all-start.1) | async-done | bytes 131104 | tf_op jit(solution)/shard_map/all_to_all | solution.py:100
  28.5 0.2 convolution_convert_fusion.1
  28.7 0.8 all_to_all.21
  29.5 16.4 %all-to-all-start.2 = ((bf16[64,2,1024]{2,1,0:T(2,128)(2,1)}), bf16[64,2,1024]{2,1,0:T(2,128)(2,1)S(1)}, u32[]{:S(2)}, u32[]{:S(2)}) async-start(bf16[64,2,1024]{2,1,0:T(2,128)(2,1)} %all_to_all.21), calls=%async_computation.2 | async-start | bytes 524288 | tf_op jit(solution)/shard_map/all_to_all | solution.py:118
  45.8 0.0 copy-done
  45.9 3.8 %fusion.12 = f32[128,1536]{1,0:T(8,128)S(1)} fusion(bf16[2048,1536]{1,0:T(8,128)(2,1)} %param.9, bf16[1,128,2048]{2,1,0:T(8,128)(2,1)S(1)} %copy-done), kind=kOutput, calls=%fused_computation.18 | convolution fusion | flops 805306368 | bytes 7602176 | tf_op jit(solution)/shard_map/dot_general | solution.py:120
  49.6 8.2 %all-to-all-done.2 = bf16[64,2,1024]{2,1,0:T(2,128)(2,1)S(1)} async-done(((bf16[64,2,1024]{2,1,0:T(2,128)(2,1)}), bf16[64,2,1024]{2,1,0:T(2,128)(2,1)S(1)}, u32[]{:S(2)}, u32[]{:S(2)}) %all-to-all-start.2) | async-done | bytes 262176 | tf_op jit(solution)/shard_map/all_to_all | solution.py:118
  57.8 0.2 reshape.46
  58.0 1.0 fusion.16
  59.0 2.6 %add_convert_fusion.x_ref = bf16[1024,1536]{1,0:T(8,128)(2,1)} fusion(f32[1024,1536]{1,0:T(8,128)S(1)} %fusion.16, bf16[1024,128]{1,0:T(8,128)(2,1)S(1)} %reshape.46, f32[128,1536]{1,0:T(8,128)S(1)} %fusion.12), kind=kOutput, calls=%fused_computation.4 | convolution fusion | flops 406585344 | bytes 10485760 | tf_op jit(solution)/shard_map/dot_general | solution.py:124
  61.6 11.6 %shard_map.55 = f32[1024,64]{1,0:T(8,128)} custom-call(bf16[1024,1536]{1,0:T(8,128)(2,1)} %add_convert_fusion.x_ref), custom_call_target="tpu_custom_call" | custom-call | tf_op jit(solution)/shard_map/pallas_call | solution.py:56
  73.2 1.1 %slice.12 = bf16[128,8,256]{2,1,0:T(8,128)(2,1)S(1)} slice(bf16[128,8,1536]{2,1,0:T(8,128)(2,1)} %bitcast.33), slice={[0:128], [0:8], [1280:1536]} | slice | bytes 1048576 | tf_op jit(solution)/shard_map/slice | solution.py:130
  74.2 0.1 concatenate.8
  74.4 1.1 %convert_element_type.49 = bf16[1024,64]{1,0:T(8,128)(2,1)S(1)} convert(f32[1024,64]{1,0:T(8,128)} %shard_map.55) | non-fusion elementwise | flops 65536 | bytes 393216 | tf_op jit(solution)/shard_map/convert_element_type | solution.py:129
  75.4 0.2 concatenate.9
  75.6 0.6 pad_maximum_fusion
  76.2 25.9 %all_to_all.29 = bf16[64,2,2560]{2,1,0:T(2,128)(2,1)S(1)} all-to-all(bf16[64,2,2560]{2,1,0:T(2,128)(2,1)S(1)} %pad_maximum_fusion), channel_id=1, replica_groups=mesh['wide'=64,'seq'=4] {'wide'}, dimensions={0} | all-to-all | bytes 1310720 | tf_op jit(solution)/shard_map/all_to_all | solution.py:132
  102.2 0.2 all_to_all.24
  102.4 0.3 convolution_convert_fusion
  102.7 0.2 reshape_reshape.6
  102.9 0.1 copy.21
  103.0 1.6 %copy.23 = bf16[64,8,2,4,8]{1,4,3,2,0:T(8,128)(2,1)S(1)} copy(bf16[64,8,2,4,8]{0,4,3,2,1:T(8,128)(2,1)S(1)} %bitcast.34) | data formatting | bytes 131072 | tf_op jit(solution)/shard_map/reshape;reshape | solution.py:68
  104.6 1.4 %bitcast_convert_fusion = bf16[64,2,128,4,8]{2,4,3,1,0:T(8,128)(2,1)} fusion(bf16[64,8,2,4,8]{1,4,3,2,0:T(8,128)(2,1)S(1)} %copy.23, bf16[64,8,2,128]{3,2,1,0:T(2,128)(2,1)S(1)} %reshape_reshape.6), kind=kOutput, calls=%fused_computation.12 | convolution fusion | flops 8912896 | bytes 1376256
  (4 shorter events, 0.1 us)
Async XLA Ops:
  0.0 45.8 %copy-start = (bf16[1,128,2048]{2,1,0:T(8,128)(2,1)S(1)}, bf16[1,128,2048]{2,1,0:T(8,128)(2,1)}, u32[]{:S(2)}) copy-start(bf16[1,128,2048]{2,1,0:T(8,128)(2,1)} %param.8) | copy-start | bytes 1572868
  0.0 17.1 %copy-start.1 = (bf16[40,32768]{1,0:T(8,128)(2,1)S(1)}, bf16[40,32768]{1,0:T(8,128)(2,1)}, u32[]{:S(2)}) copy-start(bf16[40,32768]{1,0:T(8,128)(2,1)} %param.5) | copy-start | bytes 7864324
  3.7 11.9 %all-to-all-start = ((f32[4,1,32768]{2,1,0:T(1,128)}), f32[4,1,32768]{2,1,0:T(1,128)}, u32[]{:S(2)}, u32[]{:S(2)}) async-start(f32[4,1,32768]{2,1,0:T(1,128)} %broadcast_in_dim.2), calls=%async_computation | async-start | bytes 1048576 | tf_op jit(solution)/shard_map/all_to_all | solution.py:88
  20.3 8.1 %all-to-all-start.1 = ((bf16[4,2,64,128]{3,2,1,0:T(8,128)(2,1)}), bf16[4,2,64,128]{3,2,1,0:T(8,128)(2,1)S(1)}, u32[]{:S(2)}, u32[]{:S(2)}) async-start(bf16[4,2,64,128]{3,2,1,0:T(8,128)(2,1)} %bitcast.32), calls=%async_computation.1 | async-start | bytes 262144 | tf_op jit(solution)/shard_map/all_to_all | solution.py:100
  29.5 28.3 %all-to-all-start.2 = ((bf16[64,2,1024]{2,1,0:T(2,128)(2,1)}), bf16[64,2,1024]{2,1,0:T(2,128)(2,1)S(1)}, u32[]{:S(2)}, u32[]{:S(2)}) async-start(bf16[64,2,1024]{2,1,0:T(2,128)(2,1)} %all_to_all.21), calls=%async_computation.2 | async-start | bytes 524288 | tf_op jit(solution)/shard_map/all_to_all | solution.py:118

commit v5 on v4

--- a/solution.py
+++ b/solution.py
@@ -2,6 +2,7 @@
 import jax.numpy as jnp
 from jax import lax
 from jax.experimental import pallas as pl
+from jax.experimental.pallas import tpu as pltpu
 from jax.sharding import PartitionSpec as P
 
 CH = 128
@@ -15,16 +16,24 @@
 SUB = 4
 
 
-def _weights_kernel(x_ref, o_ref):
+def _owner_kernel(rows_ref, hi_ref, lo_ref, o_ref, w_ref):
     group_size = HEADS // KVH
     sub_rows = SUB * BINS
     cols = SUB * group_size * BINS
+    value_width = KVH * HD
+    rows = rows_ref[...]
+    projected = jnp.dot(rows, hi_ref[...], preferred_element_type=jnp.float32) + jnp.dot(
+        rows, lo_ref[...], preferred_element_type=jnp.float32
+    )
+    projected = projected.astype(jnp.bfloat16)
+    o_ref[:, :value_width] = projected[:, (HEADS + KVH) * HD :]
+    projected = projected.astype(jnp.float32)
     row_patch = lax.broadcasted_iota(jnp.int32, (sub_rows, cols), 0) // BINS
     col_patch = lax.broadcasted_iota(jnp.int32, (sub_rows, cols), 1) // (group_size * BINS)
     same = row_patch == col_patch
-    for sg in range(x_ref.shape[0] // sub_rows):
+    for sg in range(rows_ref.shape[0] // sub_rows):
         base = sg * sub_rows
-        xs = x_ref[base : base + sub_rows, :].astype(jnp.float32)
+        xs = projected[base : base + sub_rows, :]
         for g in range(KVH):
             k = xs[:, (HEADS + g) * HD : (HEADS + g + 1) * HD]
             k = k / jnp.sqrt(jnp.mean(k * k, axis=-1, keepdims=True) + 1e-06)
@@ -48,25 +57,32 @@
                 for c in range(1, SUB):
                     compact = compact + tile[:, c * width : (c + 1) * width]
                 row0 = base + p * BINS
-                o_ref[row0 : row0 + BINS, g * width : (g + 1) * width] = compact
+                w_ref[row0 : row0 + BINS, g * width : (g + 1) * width] = compact
+    o_ref[:, value_width:] = w_ref[...].astype(jnp.bfloat16)
 
 
-def attention_weights(qkv_flat):
-    total, width = qkv_flat.shape
+def owner_payload(rows, merged_hi, merged_lo):
+    total, depth = rows.shape
+    width = merged_hi.shape[1]
     return pl.pallas_call(
-        _weights_kernel,
-        out_shape=jax.ShapeDtypeStruct((total, HEADS * BINS), jnp.float32),
+        _owner_kernel,
+        out_shape=jax.ShapeDtypeStruct((total, KVH * HD + HEADS * BINS), jnp.bfloat16),
         grid=(total // ROWS,),
-        in_specs=[pl.BlockSpec((ROWS, width), lambda i: (i, 0))],
-        out_specs=pl.BlockSpec((ROWS, HEADS * BINS), lambda i: (i, 0)),
-    )(qkv_flat)
+        in_specs=[
+            pl.BlockSpec((ROWS, depth), lambda i: (i, 0)),
+            pl.BlockSpec((depth, width), lambda i: (0, 0)),
+            pl.BlockSpec((depth, width), lambda i: (0, 0)),
+        ],
+        out_specs=pl.BlockSpec((ROWS, KVH * HD + HEADS * BINS), lambda i: (i, 0)),
+        scratch_shapes=[pltpu.VMEM((ROWS, HEADS * BINS), jnp.float32)],
+    )(rows, merged_hi, merged_lo)
 
 
-def heads_from(weights, values):
-    n = weights.shape[0]
+def heads_from(payload):
+    n = payload.shape[0]
     group_size = HEADS // KVH
-    w = weights.reshape(n, BINS, KVH, group_size, BINS)
-    v = values.reshape(n, BINS, KVH, HD)
+    v = payload[:, :, : KVH * HD].reshape(n, BINS, KVH, HD)
+    w = payload[:, :, KVH * HD :].reshape(n, BINS, KVH, group_size, BINS)
     mixed = jnp.einsum("pjgri,pjge->pigre", w, v, preferred_element_type=jnp.float32)
     return mixed.reshape(n, BINS, HEADS * HD).astype(jnp.bfloat16)
 
@@ -121,21 +137,10 @@
     merged_hi = merged.astype(jnp.bfloat16)
     merged_lo = (merged - merged_hi.astype(jnp.float32)).astype(jnp.bfloat16)
     rows = arrived.reshape(slot_count * all_bins, CH)
-    projected = jnp.dot(rows, merged_hi, preferred_element_type=jnp.float32) + jnp.dot(
-        rows, merged_lo, preferred_element_type=jnp.float32
-    )
-    projected = projected.astype(jnp.bfloat16).reshape(slot_count, all_bins, qkv_weight.shape[1])
-    weights = attention_weights(projected.reshape(slot_count * all_bins, qkv_weight.shape[1]))
-    weights = weights.astype(jnp.bfloat16).reshape(slot_count, all_bins * HEADS * BINS)
-    values = projected[:, :, (HEADS + KVH) * HD :].reshape(slot_count, all_bins * KVH * HD)
-    payload = jnp.concatenate([values, weights], axis=1)
+    payload = owner_payload(rows, merged_hi, merged_lo).reshape(slot_count, -1)
     returned = lax.all_to_all(payload, "wide", split_axis=0, concat_axis=0, tiled=True)
     mine = jnp.dot(dispatch.T, returned, preferred_element_type=jnp.float32).astype(jnp.bfloat16)
-    split = all_bins * KVH * HD
-    return heads_from(
-        mine[:, split:].reshape(quarter, all_bins, HEADS * BINS),
-        mine[:, :split].reshape(quarter, all_bins, KVH * HD),
-    )
+    return heads_from(mine.reshape(quarter, all_bins, -1))
 
 
 def solution(mesh):

time: 107 us -> 105 us (0.981)
  Pallas kernels: 11.6 us -> 14.6 us
  matrix products: 11.7 us -> 9.04 us
  other arithmetic: 7.44 us -> 5.79 us
    dot_general x2 -> x0, matrix products: 3.6 us -> none  [the longest x1 2.63 us: body(): jnp.dot(rows, merged_lo, preferred_element_type=jnp.float32)]
    pallas_call x1, Pallas kernels: 11.6 us -> 14.6 us  [owner_payload(): pl.pallas_call(_owner_kernel, out_shape=jax.ShapeDtypeStruct((total, KVH...]
    all_to_all x1 -> x2, local copies, waits for them, and re-layouts: 0.25 us -> 2.67 us  [body(): lax.all_to_all(payload, 'wide', split_axis=0, concat_axis=0, tiled=True)]
    another operation x2 -> x0, local copies, waits for them, and re-layouts: 1.76 us -> none  [the longest x1 1.59 us: heads_from(): w = weights.reshape(n, BINS, KVH, group_size, BINS)]
    convert_element_type x1 -> x0, other arithmetic: 1.07 us -> none  [body(): weights.astype(jnp.bfloat16).reshape(slot_count, all_bins * HEADS * BINS)]
  transfers between devices with their start and end apart: 3 -> 3, of which waited for: 3 -> 3; matrix products, arithmetic and copies ran while one was open for 6% -> 7% of each run, Pallas kernels for 0% -> 0%
where the time goes in v5:
time: 105 us; the launch traced here: 104 us
  blocking collectives  25.9 us (25%)
  starting transfers between devices  24.5 us (23%)
  waiting for transfers between devices  16.8 us (16%)
  Pallas kernels  14.6 us (14%)
  matrix products  9.04 us (9%)
  local copies, waits for them, and re-layouts  7.63 us (7%)
  other arithmetic  5.79 us (6%)
    all_to_all x1, blocking collectives, body(): lax.all_to_all(payload, 'wide', split_axis=0, concat_axis=0, tiled=True)  25.9 us
    all_to_all x1, starting transfers between devices, body(): lax.all_to_all(outgoing, 'wide', split_axis=0, concat_axis=0, tiled=True)  16.4 us
    pallas_call x1, Pallas kernels, owner_payload(): pl.pallas_call(_owner_kernel, out_shape=jax.ShapeDtypeStruct((total, KVH...  14.6 us
    all_to_all x1, waiting for transfers between devices, body(): lax.all_to_all(outgoing, 'wide', split_axis=0, concat_axis=0, tiled=True)  7.3 us
    all_to_all x1, waiting for transfers between devices, body(): lax.all_to_all(spread, 'seq', split_axis=0, concat_axis=0, tiled=True)  5.45 us
    all_to_all x1, starting transfers between devices, body(): lax.all_to_all(spread, 'seq', split_axis=0, concat_axis=0, tiled=True)  4.83 us
    dot_general x1, matrix products, body(): jnp.dot(weight_block, qkv_weight, preferred_element_type=jnp.float32)  4.66 us
    all_to_all x1, waiting for transfers between devices, body(): lax.all_to_all(binned, 'seq', split_axis=0, concat_axis=0, tiled=True)  4.02 us
  transfers between devices with their start and end apart: 3, of which 3 were waited for; matrix products, arithmetic and copies ran while one was open for 7% of the time, Pallas kernels for 0%

profile of v5, /device:TPU:1, one launch (start us, length us, event | category | flops | bytes accessed | tf_op | source)
XLA Modules:
  0.0 104.4 jit_solution(17637468173990257809)
XLA Ops:
  0.0 0.0 copy-start
  0.0 0.0 copy-start.1
  0.0 2.6 %fusion.1 = f32[32768]{0:T(1024)S(1)} fusion(bf16[40,32768]{1,0:T(8,128)(2,1)} %param.5), kind=kLoop, calls=%fused_computation.4 | loop fusion | flops 3899392 | bytes 2752512 | tf_op jit(solution)/shard_map/reduce_sum | solution.py:102
  2.6 1.1 %broadcast_in_dim.2 = f32[4,1,32768]{2,1,0:T(1,128)} broadcast(f32[32768]{0:T(1024)S(1)} %fusion.1), dimensions={2} | broadcast | bytes 655360 | tf_op jit(solution)/shard_map/broadcast_in_dim | solution.py:103
  3.7 4.8 %all-to-all-start = ((f32[4,1,32768]{2,1,0:T(1,128)}), f32[4,1,32768]{2,1,0:T(1,128)}, u32[]{:S(2)}, u32[]{:S(2)}) async-start(f32[4,1,32768]{2,1,0:T(1,128)} %broadcast_in_dim.2), calls=%async_computation | async-start | bytes 1048576 | tf_op jit(solution)/shard_map/all_to_all | solution.py:104
  8.5 0.8 dynamic_slice.3
  9.3 0.2 convert_reduce_fusion
  9.5 0.7 broadcast_subtract_fusion
  10.1 5.5 %all-to-all-done = f32[4,1,32768]{2,1,0:T(1,128)} async-done(((f32[4,1,32768]{2,1,0:T(1,128)}), f32[4,1,32768]{2,1,0:T(1,128)}, u32[]{:S(2)}, u32[]{:S(2)}) %all-to-all-start) | async-done | bytes 524320 | tf_op jit(solution)/shard_map/all_to_all | solution.py:104
  15.6 1.5 %reduce_sum.29 = f32[32768]{0:T(1024)S(1)} reduce(f32[4,1,32768]{2,1,0:T(1,128)} %all-to-all-done, f32[]{:T(128)} %constant.10.clone.1), dimensions={0,1}, to_apply=%region_2.0 | reduce | flops 98304 | bytes 655364 | tf_op jit(solution)/shard_map/reduce_sum | solution.py:105
  17.1 0.0 copy-done.1
  17.2 2.5 %fusion.8 = bf16[1,2,256,128]{3,1,2,0:T(2,128)(2,1)S(1)} fusion(bf16[40,32768]{1,0:T(8,128)(2,1)S(1)} %copy-done.1, f32[32768]{0:T(1024)S(1)} %add_rsqrt_fusion, s32[40]{0:T(128)S(1)} %broadcast_subtract_fusion), kind=kOutput, calls=%fused_computation.13 | convolution fusion | flops 36831312 | bytes 2883744 | tf_op jit(solution)/shard_map/dot_general | solution.py:112
  19.7 0.7 copy.25
  20.3 3.3 %all-to-all-start.1 = ((bf16[4,2,64,128]{3,2,1,0:T(8,128)(2,1)}), bf16[4,2,64,128]{3,2,1,0:T(8,128)(2,1)S(1)}, u32[]{:S(2)}, u32[]{:S(2)}) async-start(bf16[4,2,64,128]{3,2,1,0:T(8,128)(2,1)} %bitcast.34), calls=%async_computation.1 | async-start | bytes 262144 | tf_op jit(solution)/shard_map/all_to_all | solution.py:116
  23.7 0.8 multiply_add_fusion
  24.4 4.0 %all-to-all-done.1 = bf16[4,2,64,128]{3,2,1,0:T(8,128)(2,1)S(1)} async-done(((bf16[4,2,64,128]{3,2,1,0:T(8,128)(2,1)}), bf16[4,2,64,128]{3,2,1,0:T(8,128)(2,1)S(1)}, u32[]{:S(2)}, u32[]{:S(2)}) %all-to-all-start.1) | async-done | bytes 131104 | tf_op jit(solution)/shard_map/all_to_all | solution.py:116
  28.5 0.2 convolution_convert_fusion.1
  28.7 0.8 all_to_all.23
  29.5 16.4 %all-to-all-start.2 = ((bf16[64,2,1024]{2,1,0:T(2,128)(2,1)}), bf16[64,2,1024]{2,1,0:T(2,128)(2,1)S(1)}, u32[]{:S(2)}, u32[]{:S(2)}) async-start(bf16[64,2,1024]{2,1,0:T(2,128)(2,1)} %all_to_all.23), calls=%async_computation.2 | async-start | bytes 524288 | tf_op jit(solution)/shard_map/all_to_all | solution.py:134
  45.9 0.0 copy-done
  45.9 4.7 %subtract_convert_fusion = (bf16[128,1536]{1,0:T(8,128)(2,1)}, bf16[128,1536]{1,0:T(8,128)(2,1)}) fusion(bf16[2048,1536]{1,0:T(8,128)(2,1)} %param.9, bf16[1,128,2048]{2,1,0:T(8,128)(2,1)S(1)} %copy-done), kind=kOutput, calls=%fused_computation.14 | convolution fusion | flops 806092800 | bytes 7602176 | tf_op jit(solution)/shard_map/dot_general | solution.py:136
  50.5 7.3 %all-to-all-done.2 = bf16[64,2,1024]{2,1,0:T(2,128)(2,1)S(1)} async-done(((bf16[64,2,1024]{2,1,0:T(2,128)(2,1)}), bf16[64,2,1024]{2,1,0:T(2,128)(2,1)S(1)}, u32[]{:S(2)}, u32[]{:S(2)}) %all-to-all-start.2) | async-done | bytes 262176 | tf_op jit(solution)/shard_map/all_to_all | solution.py:134
  57.8 0.9 reshape.48.rows_ref
  58.7 14.6 %shard_map.55 = bf16[1024,320]{1,0:T(8,128)(2,1)} custom-call(bf16[1024,128]{1,0:T(8,128)(2,1)} %reshape.48.rows_ref, bf16[128,1536]{1,0:T(8,128)(2,1)} %get-tuple-element.6.hi_ref, bf16[128,1536]{1,0:T(8,128)(2,1)} %get-tuple-element.5.lo_ref), custom_call_target="tpu_custom_call" | custom-call | tf_op jit(solution)/shard_map/pallas_call | solution.py:67
  73.3 2.4 %all_to_all.25 = bf16[64,2,2560]{2,1,0:T(2,128)(2,1)S(1)} reshape(bf16[1024,320]{1,0:T(8,128)(2,1)} %shard_map.55) | data formatting | bytes 1310720 | tf_op jit(solution)/shard_map/all_to_all | solution.py:141
  75.7 25.9 %all_to_all.32 = bf16[64,2,2560]{2,1,0:T(2,128)(2,1)S(1)} all-to-all(bf16[64,2,2560]{2,1,0:T(2,128)(2,1)S(1)} %all_to_all.25), channel_id=1, replica_groups=mesh['wide'=64,'seq'=4] {'wide'}, dimensions={0} | all-to-all | bytes 1310720 | tf_op jit(solution)/shard_map/all_to_all | solution.py:141
  101.7 0.2 all_to_all.27
  101.9 0.3 convolution_convert_fusion
  102.2 0.3 reshape.49
  102.5 0.5 copy.16
  103.0 1.4 %bitcast_convert_fusion = bf16[64,2,128,4,8]{2,4,3,1,0:T(8,128)(2,1)} fusion(bf16[64,2,8,32]{2,3,1,0:T(8,128)(2,1)S(1)} %bitcast.35, bf16[64,8,320]{2,1,0:T(8,128)(2,1)S(1)} %reshape.49), kind=kOutput, calls=%fused_computation.11 | convolution fusion | flops 8912896 | bytes 2359296
  (3 shorter events, 0.1 us)
Async XLA Ops:
  0.0 45.9 %copy-start = (bf16[1,128,2048]{2,1,0:T(8,128)(2,1)S(1)}, bf16[1,128,2048]{2,1,0:T(8,128)(2,1)}, u32[]{:S(2)}) copy-start(bf16[1,128,2048]{2,1,0:T(8,128)(2,1)} %param.8) | copy-start | bytes 1572868
  0.0 17.1 %copy-start.1 = (bf16[40,32768]{1,0:T(8,128)(2,1)S(1)}, bf16[40,32768]{1,0:T(8,128)(2,1)}, u32[]{:S(2)}) copy-start(bf16[40,32768]{1,0:T(8,128)(2,1)} %param.5) | copy-start | bytes 7864324
  3.7 11.9 %all-to-all-start = ((f32[4,1,32768]{2,1,0:T(1,128)}), f32[4,1,32768]{2,1,0:T(1,128)}, u32[]{:S(2)}, u32[]{:S(2)}) async-start(f32[4,1,32768]{2,1,0:T(1,128)} %broadcast_in_dim.2), calls=%async_computation | async-start | bytes 1048576 | tf_op jit(solution)/shard_map/all_to_all | solution.py:104
  20.3 8.1 %all-to-all-start.1 = ((bf16[4,2,64,128]{3,2,1,0:T(8,128)(2,1)}), bf16[4,2,64,128]{3,2,1,0:T(8,128)(2,1)S(1)}, u32[]{:S(2)}, u32[]{:S(2)}) async-start(bf16[4,2,64,128]{3,2,1,0:T(8,128)(2,1)} %bitcast.34), calls=%async_computation.1 | async-start | bytes 262144 | tf_op jit(solution)/shard_map/all_to_all | solution.py:116
  29.5 28.4 %all-to-all-start.2 = ((bf16[64,2,1024]{2,1,0:T(2,128)(2,1)}), bf16[64,2,1024]{2,1,0:T(2,128)(2,1)S(1)}, u32[]{:S(2)}, u32[]{:S(2)}) async-start(bf16[64,2,1024]{2,1,0:T(2,128)(2,1)} %all_to_all.23), calls=%async_computation.2 | async-start | bytes 524288 | tf_op jit(solution)/shard_map/all_to_all | solution.py:134

commit v6 on v5

--- a/solution.py
+++ b/solution.py
@@ -100,9 +100,12 @@
 
     signal = power.astype(jnp.float32)
     partial = jnp.sum(signal * signal, axis=0)
-    spread = jnp.broadcast_to(partial[None, :], (seq_count, channels))
-    gathered = lax.all_to_all(spread, "seq", split_axis=0, concat_axis=0, tiled=True)
-    squares = jnp.sum(gathered, axis=0)
+    squares = partial
+    step = 1
+    while step < seq_count:
+        pairs = [(i, i ^ step) for i in range(seq_count)]
+        squares = squares + lax.ppermute(squares, "seq", pairs)
+        step *= 2
     inv_rms = 1.0 / jnp.sqrt(squares / (sample_rows * seq_count) + 1e-06)
     active = jnp.maximum(signal * inv_rms[None, :] - 0.8, 0.0)
     local_bins = bin_index - seq_index * bin_count
@@ -113,7 +116,13 @@
         jnp.bfloat16
     )
     binned = binned.reshape(bin_count, seq_count, quarter, CH).transpose(1, 0, 2, 3)
-    binned = lax.all_to_all(binned, "seq", split_axis=0, concat_axis=0, tiled=True)
+    received = [lax.dynamic_index_in_dim(binned, seq_index, 0, keepdims=False)]
+    for shift in range(1, seq_count):
+        pairs = [(i, (i + shift) % seq_count) for i in range(seq_count)]
+        piece = lax.dynamic_index_in_dim(binned, (seq_index + shift) % seq_count, 0, keepdims=False)
+        received.append(lax.ppermute(piece, "seq", pairs))
+    order = (seq_index - jnp.arange(seq_count, dtype=jnp.int32)) % seq_count
+    binned = jnp.take(jnp.stack(received), order, axis=0)
     block_rows = binned.reshape(all_bins, quarter, CH).transpose(1, 0, 2).reshape(
         quarter, all_bins * CH
     )

time: 105 us -> 101 us (0.962)
  waiting for transfers between devices: 16.8 us -> 12.9 us
  matrix products: 9.04 us -> 10.8 us
  other arithmetic: 5.79 us -> 4.3 us
  starting transfers between devices: 24.5 us -> 25.6 us
    ppermute x0 -> x5, starting transfers between devices: none -> 9.65 us  [the longest x2 5.75 us: body(): squares = squares + lax.ppermute(squares, 'seq', pairs)]
    all_to_all x2 -> x0, waiting for transfers between devices: 9.47 us -> none  [the longest x1 5.45 us: body(): lax.all_to_all(spread, 'seq', split_axis=0, concat_axis=0, tiled=True)]
    all_to_all x2 -> x0, starting transfers between devices: 8.16 us -> none  [the longest x1 4.83 us: body(): lax.all_to_all(spread, 'seq', split_axis=0, concat_axis=0, tiled=True)]
    ppermute x0 -> x5, waiting for transfers between devices: none -> 5.6 us  [the longest x3 3.31 us: body(): received.append(lax.ppermute(piece, 'seq', pairs))]
    dot_general x1, matrix products: 2.49 us -> 4.22 us  [body(): jnp.dot(onehot.T, active, precision=lax.Precision.HIGHEST) * (1.0 / SPB)]
    reduce_sum x1 -> x0, other arithmetic: 1.53 us -> none  [body(): squares = jnp.sum(gathered, axis=0)]
  transfers between devices with their start and end apart: 3 -> 6, of which waited for: 3 -> 4; matrix products, arithmetic and copies ran while one was open for 7% -> 7% of each run, Pallas kernels for 0% -> 0%
where the time goes in v6:
time: 101 us
  blocking collectives  26 us (26%)
  starting transfers between devices  25.6 us (25%)
  Pallas kernels  14.6 us (14%)
  waiting for transfers between devices  12.9 us (13%)
  matrix products  10.8 us (11%)
  local copies, waits for them, and re-layouts  6.66 us (7%)
  other arithmetic  4.3 us (4%)
    all_to_all x1, blocking collectives, body(): lax.all_to_all(payload, 'wide', split_axis=0, concat_axis=0, tiled=True)  26 us
    all_to_all x1, starting transfers between devices, body(): lax.all_to_all(outgoing, 'wide', split_axis=0, concat_axis=0, tiled=True)  15.9 us
    pallas_call x1, Pallas kernels, owner_payload(): pl.pallas_call(_owner_kernel, out_shape=jax.ShapeDtypeStruct((total, KVH...  14.6 us
    all_to_all x1, waiting for transfers between devices, body(): lax.all_to_all(outgoing, 'wide', split_axis=0, concat_axis=0, tiled=True)  7.27 us
    ppermute x2, starting transfers between devices, body(): squares = squares + lax.ppermute(squares, 'seq', pairs)  5.75 us
    dot_general x1, matrix products, body(): jnp.dot(weight_block, qkv_weight, preferred_element_type=jnp.float32)  4.68 us
    dot_general x1, matrix products, body(): jnp.dot(onehot.T, active, precision=lax.Precision.HIGHEST) * (1.0 / SPB)  4.22 us
    ppermute x3, starting transfers between devices, body(): received.append(lax.ppermute(piece, 'seq', pairs))  3.9 us
  transfers between devices with their start and end apart: 6, of which 4 were waited for; matrix products, arithmetic and copies ran while one was open for 7% of the time, Pallas kernels for 0%

profile of v6, /device:TPU:1, one launch (start us, length us, event | category | flops | bytes accessed | tf_op | source)
XLA Modules:
  0.0 100.9 jit_solution(12364578889569701717)
XLA Ops:
  0.0 0.0 copy-start
  0.0 2.5 %fusion.1 = f32[32768]{0:T(1024)S(1)} fusion(bf16[40,32768]{1,0:T(8,128)(2,1)} %param.5), kind=kLoop, calls=%fused_computation.5 | loop fusion | flops 3899392 | bytes 2752512 | tf_op jit(solution)/shard_map/reduce_sum | solution.py:102
  2.5 2.1 %collective-permute-start = (f32[32768]{0:T(1024)S(1)}, f32[32768]{0:T(1024)S(1)}, u32[]{:S(2)}, u32[]{:S(2)}) collective-permute-start(f32[32768]{0:T(1024)S(1)} %fusion.1), channel_id=1, source_target_pairs={{0,1},{1,0},{2,3},{3,2},{4,5},{5,4},{6,7},{7,6},{8,9},{9,8},{10,11... | collective-permute-start | bytes 393224 | tf_op jit(solution)/shard_map/ppermute | solution.py:107
  4.6 0.8 dynamic_slice.10
  5.4 0.2 convert_reduce_fusion
  5.6 0.8 multiply_add_fusion
  6.3 0.7 broadcast_subtract_fusion
  7.0 0.0 collective-permute-done
  7.0 3.6 %collective-permute-start.1 = (f32[32768]{0:T(1024)S(1)}, f32[32768]{0:T(1024)S(1)}, u32[]{:S(2)}, u32[]{:S(2)}) collective-permute-start(f32[32768]{0:T(1024)S(1)} %add.91), channel_id=1, source_target_pairs={{0,2},{1,3},{2,0},{3,1},{4,6},{5,7},{6,4},{7,5},{8,10},{9,11},{10,... | collective-permute-start | bytes 393224 | tf_op jit(solution)/shard_map/ppermute | solution.py:107
  10.7 2.3 %collective-permute-done.1 = f32[32768]{0:T(1024)S(1)} collective-permute-done((f32[32768]{0:T(1024)S(1)}, f32[32768]{0:T(1024)S(1)}, u32[]{:S(2)}, u32[]{:S(2)}) %collective-permute-start.1) | collective-permute-done | bytes 131104 | tf_op jit(solution)/shard_map/ppermute | solution.py:107
  13.0 4.2 %fusion.8 = bf16[1,2,256,128]{3,1,2,0:T(2,128)(2,1)S(1)} fusion(bf16[40,32768]{1,0:T(8,128)(2,1)} %param.5, f32[32768]{0:T(1024)S(1)} %add_rsqrt_fusion, s32[40]{0:T(128)S(1)} %broadcast_subtract_fusion), kind=kOutput, calls=%fused_computation.14 | convolution fusion | flops 36831312 | bytes 2883744 | tf_op jit(solution)/shard_map/dot_general | solution.py:115
  17.3 2.8 %collective-permute-start.4 = (bf16[2,64,128]{2,1,0:T(8,128)(2,1)S(1)}, bf16[2,64,128]{2,1,0:T(8,128)(2,1)S(1)}, u32[]{:S(2)}, u32[]{:S(2)}) collective-permute-start(bf16[2,64,128]{2,1,0:T(8,128)(2,1)S(1)} %get-tuple-element.8), channel_id=1, source_target_pairs={{0,3},{1,0},{2,1},{3,2},{4,7},{5,4},{6,5},{7,6},{8,11},{9,8},{10,9... | collective-permute-start | bytes 98312 | tf_op jit(solution)/shard_map/ppermute | solution.py:123
  20.1 0.4 collective-permute-start.3
  20.5 0.8 collective-permute-start.2
  21.2 0.1 broadcast_in_dim.14
  21.3 0.1 broadcast_in_dim.24
  21.4 0.0 collective-permute-done.4
  21.4 3.0 %collective-permute-done.3 = bf16[2,64,128]{2,1,0:T(8,128)(2,1)S(1)} collective-permute-done((bf16[2,64,128]{2,1,0:T(8,128)(2,1)S(1)}, bf16[2,64,128]{2,1,0:T(8,128)(2,1)S(1)}, u32[]{:S(2)}, u32[]{:S(2)}) %collective-permute-start.3) | collective-permute-done | bytes 32800 | tf_op jit(solution)/shard_map/ppermute | solution.py:123
  24.4 0.3 collective-permute-done.2
  24.8 0.6 gather_fusion
  25.3 0.1 copy_select_fusion
  25.4 0.2 convolution_convert_fusion.1
  25.6 0.8 all_to_all.14
  26.4 15.9 %all-to-all-start = ((bf16[64,2,1024]{2,1,0:T(2,128)(2,1)}), bf16[64,2,1024]{2,1,0:T(2,128)(2,1)S(1)}, u32[]{:S(2)}, u32[]{:S(2)}) async-start(bf16[64,2,1024]{2,1,0:T(2,128)(2,1)} %all_to_all.14), calls=%async_computation | async-start | bytes 524288 | tf_op jit(solution)/shard_map/all_to_all | solution.py:143
  42.4 0.0 copy-done
  42.4 4.7 %subtract_convert_fusion = (bf16[128,1536]{1,0:T(8,128)(2,1)}, bf16[128,1536]{1,0:T(8,128)(2,1)}) fusion(bf16[2048,1536]{1,0:T(8,128)(2,1)} %param.9, bf16[1,128,2048]{2,1,0:T(8,128)(2,1)S(1)} %copy-done), kind=kOutput, calls=%fused_computation.15 | convolution fusion | flops 806092800 | bytes 7602176 | tf_op jit(solution)/shard_map/dot_general | solution.py:145
  47.1 7.3 %all-to-all-done = bf16[64,2,1024]{2,1,0:T(2,128)(2,1)S(1)} async-done(((bf16[64,2,1024]{2,1,0:T(2,128)(2,1)}), bf16[64,2,1024]{2,1,0:T(2,128)(2,1)S(1)}, u32[]{:S(2)}, u32[]{:S(2)}) %all-to-all-start) | async-done | bytes 262176 | tf_op jit(solution)/shard_map/all_to_all | solution.py:143
  54.3 0.9 reshape.98.rows_ref
  55.2 14.6 %shard_map.55 = bf16[1024,320]{1,0:T(8,128)(2,1)} custom-call(bf16[1024,128]{1,0:T(8,128)(2,1)} %reshape.98.rows_ref, bf16[128,1536]{1,0:T(8,128)(2,1)} %get-tuple-element.6.hi_ref, bf16[128,1536]{1,0:T(8,128)(2,1)} %get-tuple-element.5.lo_ref), custom_call_target="tpu_custom_call" | custom-call | tf_op jit(solution)/shard_map/pallas_call | solution.py:67
  69.8 2.4 %all_to_all.16 = bf16[64,2,2560]{2,1,0:T(2,128)(2,1)S(1)} reshape(bf16[1024,320]{1,0:T(8,128)(2,1)} %shard_map.55) | data formatting | bytes 1310720 | tf_op jit(solution)/shard_map/all_to_all | solution.py:150
  72.2 26.0 %all_to_all.21 = bf16[64,2,2560]{2,1,0:T(2,128)(2,1)S(1)} all-to-all(bf16[64,2,2560]{2,1,0:T(2,128)(2,1)S(1)} %all_to_all.16), channel_id=1, replica_groups=mesh['wide'=64,'seq'=4] {'wide'}, dimensions={0} | all-to-all | bytes 1310720 | tf_op jit(solution)/shard_map/all_to_all | solution.py:150
  98.2 0.2 all_to_all.18
  98.4 0.3 convolution_convert_fusion
  98.7 0.3 reshape.99
  99.0 0.5 copy.11
  99.5 1.4 %bitcast_convert_fusion = bf16[64,2,128,4,8]{2,4,3,1,0:T(8,128)(2,1)} fusion(bf16[64,2,8,32]{2,3,1,0:T(8,128)(2,1)S(1)} %bitcast.44, bf16[64,8,320]{2,1,0:T(8,128)(2,1)S(1)} %reshape.99), kind=kOutput, calls=%fused_computation.12 | convolution fusion | flops 8912896 | bytes 2359296
  (9 shorter events, 0.1 us)
Async XLA Ops:
  0.0 42.4 %copy-start = (bf16[1,128,2048]{2,1,0:T(8,128)(2,1)S(1)}, bf16[1,128,2048]{2,1,0:T(8,128)(2,1)}, u32[]{:S(2)}) copy-start(bf16[1,128,2048]{2,1,0:T(8,128)(2,1)} %param.8) | copy-start | bytes 1572868
  2.5 4.5 %collective-permute-start = (f32[32768]{0:T(1024)S(1)}, f32[32768]{0:T(1024)S(1)}, u32[]{:S(2)}, u32[]{:S(2)}) collective-permute-start(f32[32768]{0:T(1024)S(1)} %fusion.1), channel_id=1, source_target_pairs={{0,1},{1,0},{2,3},{3,2},{4,5},{5,4},{6,7},{7,6},{8,9},{9,8},{10,11... | collective-permute-start | bytes 393224 | tf_op jit(solution)/shard_map/ppermute | solution.py:107
  7.0 6.0 %collective-permute-start.1 = (f32[32768]{0:T(1024)S(1)}, f32[32768]{0:T(1024)S(1)}, u32[]{:S(2)}, u32[]{:S(2)}) collective-permute-start(f32[32768]{0:T(1024)S(1)} %add.91), channel_id=1, source_target_pairs={{0,2},{1,3},{2,0},{3,1},{4,6},{5,7},{6,4},{7,5},{8,10},{9,11},{10,... | collective-permute-start | bytes 393224 | tf_op jit(solution)/shard_map/ppermute | solution.py:107
  17.3 4.1 %collective-permute-start.4 = (bf16[2,64,128]{2,1,0:T(8,128)(2,1)S(1)}, bf16[2,64,128]{2,1,0:T(8,128)(2,1)S(1)}, u32[]{:S(2)}, u32[]{:S(2)}) collective-permute-start(bf16[2,64,128]{2,1,0:T(8,128)(2,1)S(1)} %get-tuple-element.8), channel_id=1, source_target_pairs={{0,3},{1,0},{2,1},{3,2},{4,7},{5,4},{6,5},{7,6},{8,11},{9,8},{10,9... | collective-permute-start | bytes 98312 | tf_op jit(solution)/shard_map/ppermute | solution.py:123
  20.1 4.3 %collective-permute-start.3 = (bf16[2,64,128]{2,1,0:T(8,128)(2,1)S(1)}, bf16[2,64,128]{2,1,0:T(8,128)(2,1)S(1)}, u32[]{:S(2)}, u32[]{:S(2)}) collective-permute-start(bf16[2,64,128]{2,1,0:T(8,128)(2,1)S(1)} %get-tuple-element.9), channel_id=1, source_target_pairs={{0,2},{1,3},{2,0},{3,1},{4,6},{5,7},{6,4},{7,5},{8,10},{9,11},{10,... | collective-permute-start | bytes 98312 | tf_op jit(solution)/shard_map/ppermute | solution.py:123
  20.5 4.3 %collective-permute-start.2 = (bf16[2,64,128]{2,1,0:T(8,128)(2,1)S(1)}, bf16[2,64,128]{2,1,0:T(8,128)(2,1)S(1)}, u32[]{:S(2)}, u32[]{:S(2)}) collective-permute-start(bf16[2,64,128]{2,1,0:T(8,128)(2,1)S(1)} %get-tuple-element.10), channel_id=1, source_target_pairs={{0,1},{1,2},{2,3},{3,0},{4,5},{5,6},{6,7},{7,4},{8,9},{9,10},{10,1... | collective-permute-start | bytes 98312 | tf_op jit(solution)/shard_map/ppermute | solution.py:123
  26.4 27.9 %all-to-all-start = ((bf16[64,2,1024]{2,1,0:T(2,128)(2,1)}), bf16[64,2,1024]{2,1,0:T(2,128)(2,1)S(1)}, u32[]{:S(2)}, u32[]{:S(2)}) async-start(bf16[64,2,1024]{2,1,0:T(2,128)(2,1)} %all_to_all.14), calls=%async_computation | async-start | bytes 524288 | tf_op jit(solution)/shard_map/all_to_all | solution.py:143

commit v7 on v6

--- a/solution.py
+++ b/solution.py
@@ -87,10 +87,28 @@
     return mixed.reshape(n, BINS, HEADS * HD).astype(jnp.bfloat16)
 
 
+WIDE_AXES = ("y", "z", "core")
+
+
+def wide_all_to_all(x, sizes):
+    ny, nz, nc = sizes
+    total = x.shape[0]
+    rest = (total // (ny * nz * nc),) + x.shape[1:]
+    x = x.reshape(ny, nz, nc, *rest)
+    x = lax.all_to_all(x, "z", split_axis=1, concat_axis=1, tiled=True)
+    x = jnp.moveaxis(x, 2, 1).reshape(ny * nc, nz, *rest)
+    x = lax.all_to_all(x, ("y", "core"), split_axis=0, concat_axis=0, tiled=True)
+    x = jnp.moveaxis(x.reshape(ny, nc, nz, *rest), 1, 2)
+    return x.reshape(total, *x.shape[4:])
+
+
 def body(power, bin_index, session, readin_weight, qkv_weight):
-    wide_count = lax.axis_size("wide")
+    sizes = tuple(lax.axis_size(name) for name in WIDE_AXES)
+    wide_count = sizes[0] * sizes[1] * sizes[2]
     seq_count = lax.axis_size("seq")
-    wide_index = lax.axis_index("wide")
+    wide_index = (lax.axis_index("y") * sizes[1] + lax.axis_index("z")) * sizes[2] + lax.axis_index(
+        "core"
+    )
     seq_index = lax.axis_index("seq")
     sample_rows, channels = power.shape
     patch_count = channels // CH
@@ -140,20 +158,25 @@
     outgoing = jnp.dot(dispatch, block_rows, preferred_element_type=jnp.float32).astype(
         jnp.bfloat16
     )
-    arrived = lax.all_to_all(outgoing, "wide", split_axis=0, concat_axis=0, tiled=True)
+    arrived = wide_all_to_all(outgoing, sizes)
     weight_block = readin_weight[0]
     merged = jnp.dot(weight_block, qkv_weight, preferred_element_type=jnp.float32)
     merged_hi = merged.astype(jnp.bfloat16)
     merged_lo = (merged - merged_hi.astype(jnp.float32)).astype(jnp.bfloat16)
     rows = arrived.reshape(slot_count * all_bins, CH)
     payload = owner_payload(rows, merged_hi, merged_lo).reshape(slot_count, -1)
-    returned = lax.all_to_all(payload, "wide", split_axis=0, concat_axis=0, tiled=True)
+    returned = wide_all_to_all(payload, sizes)
     mine = jnp.dot(dispatch.T, returned, preferred_element_type=jnp.float32).astype(jnp.bfloat16)
     return heads_from(mine.reshape(quarter, all_bins, -1))
 
 
 def solution(mesh):
-    placed = (P("seq", "wide"), P("seq"), P(), P("wide", None, None), P())
+    sizes = (4, 8, 2)
+    wide_total, seq_total = mesh.devices.shape
+    assert sizes[0] * sizes[1] * sizes[2] == wide_total
+    split = jax.sharding.Mesh(mesh.devices.reshape(*sizes, seq_total), WIDE_AXES + ("seq",))
+    placed = (P("seq", WIDE_AXES), P("seq"), P(), P(WIDE_AXES, None, None), P())
     return jax.shard_map(
-        body, mesh=mesh, in_specs=placed, out_specs=P(("wide", "seq"), None, None), check_vma=False
+        body, mesh=split, in_specs=placed, out_specs=P(WIDE_AXES + ("seq",), None, None),
+        check_vma=False,
     )

time: 101 us -> 120 us (1.19)
  blocking collectives: 26 us -> 54.4 us
  starting transfers between devices: 25.6 us -> 19.7 us
  waiting for transfers between devices: 12.9 us -> 7.38 us
  local copies, waits for them, and re-layouts: 6.66 us -> 8.59 us
    all_to_all x1 -> x3, blocking collectives: 26 us -> 54.4 us  [the longest x2 39 us: wide_all_to_all(): x = lax.all_to_all(x, 'z', split_axis=1, concat_axis=1, tiled=True)]
    all_to_all x1, starting transfers between devices: 15.9 us -> 10.1 us  [wide_all_to_all(): lax.all_to_all(x, ('y', 'core'), split_axis=0, concat_axis=0, tiled=True)]
    all_to_all x1, waiting for transfers between devices: 7.27 us -> 1.78 us  [wide_all_to_all(): lax.all_to_all(x, ('y', 'core'), split_axis=0, concat_axis=0, tiled=True)]
    another operation x0 -> x3, local copies, waits for them, and re-layouts: none -> 3.75 us  [the longest x2 2.88 us: wide_all_to_all(): x = x.reshape(ny, nz, nc, *rest)]
    all_to_all x3 -> x2, local copies, waits for them, and re-layouts: 3.48 us -> 1.22 us  [wide_all_to_all(): x = lax.all_to_all(x, 'z', split_axis=1, concat_axis=1, tiled=True)]
  transfers between devices with their start and end apart: 6 -> 6, of which waited for: 4 -> 4; matrix products, arithmetic and copies ran while one was open for 7% -> 6% of each run, Pallas kernels for 0% -> 0%
where the time goes in v7:
time: 120 us
  blocking collectives  54.4 us (45%)
  starting transfers between devices  19.7 us (16%)
  Pallas kernels  14.6 us (12%)
  matrix products  10.8 us (9%)
  local copies, waits for them, and re-layouts  8.59 us (7%)
  waiting for transfers between devices  7.38 us (6%)
  other arithmetic  4.3 us (4%)
    all_to_all x2, blocking collectives, wide_all_to_all(): x = lax.all_to_all(x, 'z', split_axis=1, concat_axis=1, tiled=True)  39 us
    all_to_all x1, blocking collectives, wide_all_to_all(): lax.all_to_all(x, ('y', 'core'), split_axis=0, concat_axis=0, tiled=True)  15.4 us
    pallas_call x1, Pallas kernels, owner_payload(): pl.pallas_call(_owner_kernel, out_shape=jax.ShapeDtypeStruct((total, KVH...  14.6 us
    all_to_all x1, starting transfers between devices, wide_all_to_all(): lax.all_to_all(x, ('y', 'core'), split_axis=0, concat_axis=0, tiled=True)  10.1 us
    ppermute x2, starting transfers between devices, body(): squares = squares + lax.ppermute(squares, 'seq', pairs)  5.75 us
    dot_general x1, matrix products, body(): jnp.dot(weight_block, qkv_weight, preferred_element_type=jnp.float32)  4.68 us
    dot_general x1, matrix products, body(): jnp.dot(onehot.T, active, precision=lax.Precision.HIGHEST) * (1.0 / SPB)  4.22 us
    ppermute x3, starting transfers between devices, body(): received.append(lax.ppermute(piece, 'seq', pairs))  3.9 us
  transfers between devices with their start and end apart: 6, of which 4 were waited for; matrix products, arithmetic and copies ran while one was open for 6% of the time, Pallas kernels for 0%

profile of v7, /device:TPU:1, one launch (start us, length us, event | category | flops | bytes accessed | tf_op | source)
XLA Modules:
  0.0 120.0 jit_solution(9768495078486273776)
XLA Ops:
  0.0 0.0 copy-start
  0.0 2.5 %fusion.1 = f32[32768]{0:T(1024)S(1)} fusion(bf16[40,32768]{1,0:T(8,128)(2,1)} %param.5), kind=kLoop, calls=%fused_computation.5 | loop fusion | flops 3899392 | bytes 2752512 | tf_op jit(solution)/shard_map/reduce_sum | solution.py:120
  2.5 2.1 %collective-permute-start = (f32[32768]{0:T(1024)S(1)}, f32[32768]{0:T(1024)S(1)}, u32[]{:S(2)}, u32[]{:S(2)}) collective-permute-start(f32[32768]{0:T(1024)S(1)} %fusion.1), channel_id=1, source_target_pairs={{0,1},{1,0},{2,3},{3,2},{4,5},{5,4},{6,7},{7,6},{8,9},{9,8},{10,11... | collective-permute-start | bytes 393224 | tf_op jit(solution)/shard_map/ppermute | solution.py:125
  4.6 0.8 dynamic_slice.10
  5.4 0.2 convert_reduce_fusion
  5.6 0.8 multiply_add_fusion
  6.3 0.7 broadcast_subtract_fusion
  7.0 0.0 collective-permute-done
  7.0 3.6 %collective-permute-start.1 = (f32[32768]{0:T(1024)S(1)}, f32[32768]{0:T(1024)S(1)}, u32[]{:S(2)}, u32[]{:S(2)}) collective-permute-start(f32[32768]{0:T(1024)S(1)} %add.99), channel_id=1, source_target_pairs={{0,2},{1,3},{2,0},{3,1},{4,6},{5,7},{6,4},{7,5},{8,10},{9,11},{10,... | collective-permute-start | bytes 393224 | tf_op jit(solution)/shard_map/ppermute | solution.py:125
  10.7 2.3 %collective-permute-done.1 = f32[32768]{0:T(1024)S(1)} collective-permute-done((f32[32768]{0:T(1024)S(1)}, f32[32768]{0:T(1024)S(1)}, u32[]{:S(2)}, u32[]{:S(2)}) %collective-permute-start.1) | collective-permute-done | bytes 131104 | tf_op jit(solution)/shard_map/ppermute | solution.py:125
  13.0 4.2 %fusion.8 = bf16[1,2,256,128]{3,1,2,0:T(2,128)(2,1)S(1)} fusion(bf16[40,32768]{1,0:T(8,128)(2,1)} %param.5, f32[32768]{0:T(1024)S(1)} %add_rsqrt_fusion, s32[40]{0:T(128)S(1)} %broadcast_subtract_fusion), kind=kOutput, calls=%fused_computation.14 | convolution fusion | flops 36831312 | bytes 2883744 | tf_op jit(solution)/shard_map/dot_general | solution.py:133
  17.3 2.8 %collective-permute-start.4 = (bf16[2,64,128]{2,1,0:T(8,128)(2,1)S(1)}, bf16[2,64,128]{2,1,0:T(8,128)(2,1)S(1)}, u32[]{:S(2)}, u32[]{:S(2)}) collective-permute-start(bf16[2,64,128]{2,1,0:T(8,128)(2,1)S(1)} %get-tuple-element.8), channel_id=1, source_target_pairs={{0,3},{1,0},{2,1},{3,2},{4,7},{5,4},{6,5},{7,6},{8,11},{9,8},{10,9... | collective-permute-start | bytes 98312 | tf_op jit(solution)/shard_map/ppermute | solution.py:141
  20.1 0.4 collective-permute-start.3
  20.5 0.8 collective-permute-start.2
  21.2 0.1 broadcast_in_dim.14
  21.3 0.1 broadcast_in_dim.24
  21.4 0.0 collective-permute-done.4
  21.4 3.0 %collective-permute-done.3 = bf16[2,64,128]{2,1,0:T(8,128)(2,1)S(1)} collective-permute-done((bf16[2,64,128]{2,1,0:T(8,128)(2,1)S(1)}, bf16[2,64,128]{2,1,0:T(8,128)(2,1)S(1)}, u32[]{:S(2)}, u32[]{:S(2)}) %collective-permute-start.3) | collective-permute-done | bytes 32800 | tf_op jit(solution)/shard_map/ppermute | solution.py:141
  24.4 0.3 collective-permute-done.2
  24.8 0.6 gather_fusion
  25.3 0.1 copy_select_fusion
  25.4 0.2 convolution_convert_fusion.1
  25.6 0.1 reshape.106
  25.7 0.2 copy.27
  25.9 17.4 %all_to_all.20 = bf16[4,8,2,2,1024]{4,3,2,0,1:T(2,128)(2,1)S(1)} all-to-all(bf16[4,8,2,2,1024]{4,3,2,0,1:T(2,128)(2,1)S(1)} %copy.27), channel_id=1, replica_groups=mesh['y'=4,'z'=8,'core'=2,'seq'=4] {'z'}, dimensions={1} | all-to-all | bytes 524288 | tf_op jit(solution)/shard_map/all_to_all | solution.py:98
  43.4 0.9 copy.28
  44.2 10.1 %all-to-all-start.1 = ((bf16[8,8,2,1024]{3,1,2,0:T(8,128)(2,1)}), bf16[8,8,2,1024]{3,1,2,0:T(8,128)(2,1)S(1)}, u32[]{:S(2)}, u32[]{:S(2)}) async-start(bf16[8,8,2,1024]{3,1,2,0:T(8,128)(2,1)} %bitcast.11), calls=%async_computation.1 | async-start | bytes 524288 | tf_op jit(solution)/shard_map/all_to_all | solution.py:100
  54.3 0.0 copy-done
  54.3 4.7 %subtract_convert_fusion = (bf16[128,1536]{1,0:T(8,128)(2,1)}, bf16[128,1536]{1,0:T(8,128)(2,1)}) fusion(bf16[2048,1536]{1,0:T(8,128)(2,1)} %param.9, bf16[1,128,2048]{2,1,0:T(8,128)(2,1)S(1)} %copy-done), kind=kOutput, calls=%fused_computation.15 | convolution fusion | flops 806092800 | bytes 7602176 | tf_op jit(solution)/shard_map/dot_general | solution.py:163
  59.0 1.8 %all-to-all-done.1 = bf16[8,8,2,1024]{3,1,2,0:T(8,128)(2,1)S(1)} async-done(((bf16[8,8,2,1024]{3,1,2,0:T(8,128)(2,1)}), bf16[8,8,2,1024]{3,1,2,0:T(8,128)(2,1)S(1)}, u32[]{:S(2)}, u32[]{:S(2)}) %all-to-all-start.1) | async-done | bytes 262176 | tf_op jit(solution)/shard_map/all_to_all | solution.py:100
  60.7 0.3 copy.29
  61.0 0.9 reshape_reshape.6.rows_ref
  61.9 14.6 %shard_map.55 = bf16[1024,320]{1,0:T(8,128)(2,1)} custom-call(bf16[1024,128]{1,0:T(8,128)(2,1)} %reshape_reshape.6.rows_ref, bf16[128,1536]{1,0:T(8,128)(2,1)} %get-tuple-element.6.hi_ref, bf16[128,1536]{1,0:T(8,128)(2,1)} %get-tuple-element.5.lo_ref), custom_call_target="tpu_custom_call" | custom-call | tf_op jit(solution)/shard_map/pallas_call | solution.py:67
  76.5 2.4 %reshape_reshape.7 = bf16[4,8,2,2,2560]{4,3,2,1,0:T(2,128)(2,1)S(1)} reshape(bf16[1024,320]{1,0:T(8,128)(2,1)} %shard_map.55) | data formatting | bytes 1310720 | tf_op jit(solution)/shard_map/reshape;reshape | solution.py:97
  78.9 0.5 copy.30
  79.4 21.5 %all_to_all.21 = bf16[4,8,2,2,2560]{4,3,2,0,1:T(2,128)(2,1)S(1)} all-to-all(bf16[4,8,2,2,2560]{4,3,2,0,1:T(2,128)(2,1)S(1)} %copy.30), channel_id=1, replica_groups=mesh['y'=4,'z'=8,'core'=2,'seq'=4] {'z'}, dimensions={1} | all-to-all | bytes 1310720 | tf_op jit(solution)/shard_map/all_to_all | solution.py:98
  100.9 0.4 copy.31
  101.3 15.4 %all_to_all.22 = bf16[8,8,2,2560]{3,1,2,0:T(8,128)(2,1)S(1)} all-to-all(bf16[8,8,2,2560]{3,1,2,0:T(8,128)(2,1)S(1)} %bitcast.58), channel_id=1, replica_groups=mesh['y'=4,'z'=8,'core'=2,'seq'=4] {'y','core'}, dimensions={0} | all-to-all | bytes 1310720 | tf_op jit(solution)/shard_map/all_to_all | solution.py:100
  116.7 0.5 copy.42
  117.2 0.2 reshape.111
  117.5 0.3 convolution_convert_fusion
  117.8 0.3 reshape.112
  118.1 0.5 copy.33
  118.6 1.4 %bitcast_convert_fusion = bf16[64,2,128,4,8]{2,4,3,1,0:T(8,128)(2,1)} fusion(bf16[64,2,8,32]{2,3,1,0:T(8,128)(2,1)S(1)} %bitcast.57, bf16[64,8,320]{2,1,0:T(8,128)(2,1)S(1)} %reshape.112), kind=kOutput, calls=%fused_computation.12 | convolution fusion | flops 8912896 | bytes 2359296
  (9 shorter events, 0.1 us)
Async XLA Ops:
  0.0 54.3 %copy-start = (bf16[1,128,2048]{2,1,0:T(8,128)(2,1)S(1)}, bf16[1,128,2048]{2,1,0:T(8,128)(2,1)}, u32[]{:S(2)}) copy-start(bf16[1,128,2048]{2,1,0:T(8,128)(2,1)} %param.8) | copy-start | bytes 1572868
  2.5 4.5 %collective-permute-start = (f32[32768]{0:T(1024)S(1)}, f32[32768]{0:T(1024)S(1)}, u32[]{:S(2)}, u32[]{:S(2)}) collective-permute-start(f32[32768]{0:T(1024)S(1)} %fusion.1), channel_id=1, source_target_pairs={{0,1},{1,0},{2,3},{3,2},{4,5},{5,4},{6,7},{7,6},{8,9},{9,8},{10,11... | collective-permute-start | bytes 393224 | tf_op jit(solution)/shard_map/ppermute | solution.py:125
  7.0 6.0 %collective-permute-start.1 = (f32[32768]{0:T(1024)S(1)}, f32[32768]{0:T(1024)S(1)}, u32[]{:S(2)}, u32[]{:S(2)}) collective-permute-start(f32[32768]{0:T(1024)S(1)} %add.99), channel_id=1, source_target_pairs={{0,2},{1,3},{2,0},{3,1},{4,6},{5,7},{6,4},{7,5},{8,10},{9,11},{10,... | collective-permute-start | bytes 393224 | tf_op jit(solution)/shard_map/ppermute | solution.py:125
  17.3 4.1 %collective-permute-start.4 = (bf16[2,64,128]{2,1,0:T(8,128)(2,1)S(1)}, bf16[2,64,128]{2,1,0:T(8,128)(2,1)S(1)}, u32[]{:S(2)}, u32[]{:S(2)}) collective-permute-start(bf16[2,64,128]{2,1,0:T(8,128)(2,1)S(1)} %get-tuple-element.8), channel_id=1, source_target_pairs={{0,3},{1,0},{2,1},{3,2},{4,7},{5,4},{6,5},{7,6},{8,11},{9,8},{10,9... | collective-permute-start | bytes 98312 | tf_op jit(solution)/shard_map/ppermute | solution.py:141
  20.1 4.3 %collective-permute-start.3 = (bf16[2,64,128]{2,1,0:T(8,128)(2,1)S(1)}, bf16[2,64,128]{2,1,0:T(8,128)(2,1)S(1)}, u32[]{:S(2)}, u32[]{:S(2)}) collective-permute-start(bf16[2,64,128]{2,1,0:T(8,128)(2,1)S(1)} %get-tuple-element.9), channel_id=1, source_target_pairs={{0,2},{1,3},{2,0},{3,1},{4,6},{5,7},{6,4},{7,5},{8,10},{9,11},{10,... | collective-permute-start | bytes 98312 | tf_op jit(solution)/shard_map/ppermute | solution.py:141
  20.5 4.3 %collective-permute-start.2 = (bf16[2,64,128]{2,1,0:T(8,128)(2,1)S(1)}, bf16[2,64,128]{2,1,0:T(8,128)(2,1)S(1)}, u32[]{:S(2)}, u32[]{:S(2)}) collective-permute-start(bf16[2,64,128]{2,1,0:T(8,128)(2,1)S(1)} %get-tuple-element.10), channel_id=1, source_target_pairs={{0,1},{1,2},{2,3},{3,0},{4,5},{5,6},{6,7},{7,4},{8,9},{9,10},{10,1... | collective-permute-start | bytes 98312 | tf_op jit(solution)/shard_map/ppermute | solution.py:141
  44.2 16.5 %all-to-all-start.1 = ((bf16[8,8,2,1024]{3,1,2,0:T(8,128)(2,1)}), bf16[8,8,2,1024]{3,1,2,0:T(8,128)(2,1)S(1)}, u32[]{:S(2)}, u32[]{:S(2)}) async-start(bf16[8,8,2,1024]{3,1,2,0:T(8,128)(2,1)} %bitcast.11), calls=%async_computation.1 | async-start | bytes 524288 | tf_op jit(solution)/shard_map/all_to_all | solution.py:100

commit v8 on v6

--- a/solution.py
+++ b/solution.py
@@ -100,12 +100,12 @@
 
     signal = power.astype(jnp.float32)
     partial = jnp.sum(signal * signal, axis=0)
-    squares = partial
-    step = 1
-    while step < seq_count:
-        pairs = [(i, i ^ step) for i in range(seq_count)]
-        squares = squares + lax.ppermute(squares, "seq", pairs)
-        step *= 2
+    received = [partial]
+    for shift in range(1, seq_count):
+        pairs = [(i, (i + shift) % seq_count) for i in range(seq_count)]
+        received.append(lax.ppermute(partial, "seq", pairs))
+    order = (seq_index - jnp.arange(seq_count, dtype=jnp.int32)) % seq_count
+    squares = jnp.sum(jnp.take(jnp.stack(received), order, axis=0), axis=0)
     inv_rms = 1.0 / jnp.sqrt(squares / (sample_rows * seq_count) + 1e-06)
     active = jnp.maximum(signal * inv_rms[None, :] - 0.8, 0.0)
     local_bins = bin_index - seq_index * bin_count

time: 101 us -> 101 us (level)
  starting transfers between devices: 25.6 us -> 19.8 us
  waiting for transfers between devices: 12.9 us -> 16.8 us
    ppermute x2 -> x3, waiting for transfers between devices: 2.29 us -> 6.74 us  [body(): received.append(lax.ppermute(partial, 'seq', pairs))]
    ppermute x3, starting transfers between devices: 3.9 us -> 1.54 us  [body(): received.append(lax.ppermute(piece, 'seq', pairs))]
    all_to_all x1, starting transfers between devices: 15.9 us -> 13.7 us  [body(): lax.all_to_all(outgoing, 'wide', split_axis=0, concat_axis=0, tiled=True)]
    ppermute x2 -> x3, starting transfers between devices: 5.75 us -> 4.5 us  [body(): received.append(lax.ppermute(partial, 'seq', pairs))]
  transfers between devices with their start and end apart: 6 -> 7, of which waited for: 4 -> 7; matrix products, arithmetic and copies ran while one was open for 7% -> 7% of each run, Pallas kernels for 0% -> 0%
where the time goes in v8:
time: 101 us
  blocking collectives  25.9 us (26%)
  starting transfers between devices  19.8 us (20%)
  waiting for transfers between devices  16.8 us (17%)
  Pallas kernels  14.6 us (14%)
  matrix products  10.8 us (11%)
  local copies, waits for them, and re-layouts  7.46 us (7%)
  other arithmetic  5.2 us (5%)
    all_to_all x1, blocking collectives, body(): lax.all_to_all(payload, 'wide', split_axis=0, concat_axis=0, tiled=True)  25.9 us
    pallas_call x1, Pallas kernels, owner_payload(): pl.pallas_call(_owner_kernel, out_shape=jax.ShapeDtypeStruct((total, KVH...  14.6 us
    all_to_all x1, starting transfers between devices, body(): lax.all_to_all(outgoing, 'wide', split_axis=0, concat_axis=0, tiled=True)  13.7 us
    all_to_all x1, waiting for transfers between devices, body(): lax.all_to_all(outgoing, 'wide', split_axis=0, concat_axis=0, tiled=True)  7.29 us
    ppermute x3, waiting for transfers between devices, body(): received.append(lax.ppermute(partial, 'seq', pairs))  6.74 us
    dot_general x1, matrix products, body(): jnp.dot(weight_block, qkv_weight, preferred_element_type=jnp.float32)  4.66 us
    ppermute x3, starting transfers between devices, body(): received.append(lax.ppermute(partial, 'seq', pairs))  4.5 us
    dot_general x1, matrix products, body(): jnp.dot(onehot.T, active, precision=lax.Precision.HIGHEST) * (1.0 / SPB)  4.22 us
  transfers between devices with their start and end apart: 7, of which 7 were waited for; matrix products, arithmetic and copies ran while one was open for 7% of the time, Pallas kernels for 0%

profile of v8, /device:TPU:1, one launch (start us, length us, event | category | flops | bytes accessed | tf_op | source)
XLA Modules:
  0.0 100.7 jit_solution(4989710701653008849)
XLA Ops:
  0.0 0.0 copy-start
  0.0 2.5 %fusion.1 = f32[32768]{0:T(1024)S(1)} fusion(bf16[40,32768]{1,0:T(8,128)(2,1)} %param.5), kind=kLoop, calls=%fused_computation.6 | loop fusion | flops 3899392 | bytes 2752512 | tf_op jit(solution)/shard_map/reduce_sum | solution.py:102
  2.5 3.4 %collective-permute-start.2 = (f32[32768]{0:T(1024)S(1)}, f32[32768]{0:T(1024)S(1)}, u32[]{:S(2)}, u32[]{:S(2)}) collective-permute-start(f32[32768]{0:T(1024)S(1)} %fusion.1), channel_id=1, source_target_pairs={{0,3},{1,0},{2,1},{3,2},{4,7},{5,4},{6,5},{7,6},{8,11},{9,8},{10,9... | collective-permute-start | bytes 393224 | tf_op jit(solution)/shard_map/ppermute | solution.py:106
  5.9 0.5 collective-permute-start.1
  6.4 0.6 collective-permute-start
  7.0 0.7 broadcast_subtract_fusion
  7.8 0.8 dynamic_slice.10
  8.5 0.2 convert_reduce_fusion
  8.7 0.8 collective-permute-done.2
  9.5 1.8 %collective-permute-done.1 = f32[32768]{0:T(1024)S(1)} collective-permute-done((f32[32768]{0:T(1024)S(1)}, f32[32768]{0:T(1024)S(1)}, u32[]{:S(2)}, u32[]{:S(2)}) %collective-permute-start.1) | collective-permute-done | bytes 131104 | tf_op jit(solution)/shard_map/ppermute | solution.py:106
  11.3 4.1 %collective-permute-done = f32[32768]{0:T(1024)S(1)} collective-permute-done((f32[32768]{0:T(1024)S(1)}, f32[32768]{0:T(1024)S(1)}, u32[]{:S(2)}, u32[]{:S(2)}) %collective-permute-start) | collective-permute-done | bytes 131104 | tf_op jit(solution)/shard_map/ppermute | solution.py:106
  15.5 0.5 pad_maximum_fusion
  16.0 0.8 gather_fusion
  16.8 0.4 select_reduce_fusion
  17.2 4.2 %fusion.8 = bf16[1,2,256,128]{3,1,2,0:T(2,128)(2,1)S(1)} fusion(bf16[40,32768]{1,0:T(8,128)(2,1)} %param.5, f32[32768]{0:T(1024)S(1)} %add_rsqrt_fusion, s32[40]{0:T(128)S(1)} %broadcast_subtract_fusion), kind=kOutput, calls=%fused_computation.15 | convolution fusion | flops 36831312 | bytes 2883744 | tf_op jit(solution)/shard_map/dot_general | solution.py:115
  21.5 0.1 collective-permute-start.5
  21.6 0.2 collective-permute-start.4
  21.9 1.2 %collective-permute-start.3 = (bf16[2,64,128]{2,1,0:T(8,128)(2,1)S(1)}, bf16[2,64,128]{2,1,0:T(8,128)(2,1)S(1)}, u32[]{:S(2)}, u32[]{:S(2)}) collective-permute-start(bf16[2,64,128]{2,1,0:T(8,128)(2,1)S(1)} %get-tuple-element.10), channel_id=1, source_target_pairs={{0,1},{1,2},{2,3},{3,0},{4,5},{5,6},{6,7},{7,4},{8,9},{9,10},{10,1... | collective-permute-start | bytes 98312 | tf_op jit(solution)/shard_map/ppermute | solution.py:123
  23.1 0.8 multiply_add_fusion
  23.8 0.1 broadcast_in_dim.33
  23.9 0.1 broadcast_in_dim.34
  24.0 0.4 collective-permute-done.5
  24.4 1.6 %collective-permute-done.4 = bf16[2,64,128]{2,1,0:T(8,128)(2,1)S(1)} collective-permute-done((bf16[2,64,128]{2,1,0:T(8,128)(2,1)S(1)}, bf16[2,64,128]{2,1,0:T(8,128)(2,1)S(1)}, u32[]{:S(2)}, u32[]{:S(2)}) %collective-permute-start.4) | collective-permute-done | bytes 32800 | tf_op jit(solution)/shard_map/ppermute | solution.py:123
  26.0 0.8 collective-permute-done.3
  26.8 0.6 gather_fusion.1
  27.4 0.1 copy_select_fusion
  27.4 0.2 convolution_convert_fusion.1
  27.7 0.8 all_to_all.14
  28.5 13.7 %all-to-all-start = ((bf16[64,2,1024]{2,1,0:T(2,128)(2,1)}), bf16[64,2,1024]{2,1,0:T(2,128)(2,1)S(1)}, u32[]{:S(2)}, u32[]{:S(2)}) async-start(bf16[64,2,1024]{2,1,0:T(2,128)(2,1)} %all_to_all.14), calls=%async_computation | async-start | bytes 524288 | tf_op jit(solution)/shard_map/all_to_all | solution.py:143
  42.2 0.0 copy-done
  42.2 4.7 %subtract_convert_fusion = (bf16[128,1536]{1,0:T(8,128)(2,1)}, bf16[128,1536]{1,0:T(8,128)(2,1)}) fusion(bf16[2048,1536]{1,0:T(8,128)(2,1)} %param.9, bf16[1,128,2048]{2,1,0:T(8,128)(2,1)S(1)} %copy-done), kind=kOutput, calls=%fused_computation.16 | convolution fusion | flops 806092800 | bytes 7602176 | tf_op jit(solution)/shard_map/dot_general | solution.py:145
  46.9 7.3 %all-to-all-done = bf16[64,2,1024]{2,1,0:T(2,128)(2,1)S(1)} async-done(((bf16[64,2,1024]{2,1,0:T(2,128)(2,1)}), bf16[64,2,1024]{2,1,0:T(2,128)(2,1)S(1)}, u32[]{:S(2)}, u32[]{:S(2)}) %all-to-all-start) | async-done | bytes 262176 | tf_op jit(solution)/shard_map/all_to_all | solution.py:143
  54.2 0.9 reshape.102.rows_ref
  55.0 14.6 %shard_map.55 = bf16[1024,320]{1,0:T(8,128)(2,1)} custom-call(bf16[1024,128]{1,0:T(8,128)(2,1)} %reshape.102.rows_ref, bf16[128,1536]{1,0:T(8,128)(2,1)} %get-tuple-element.6.hi_ref, bf16[128,1536]{1,0:T(8,128)(2,1)} %get-tuple-element.5.lo_ref), custom_call_target="tpu_custom_call" | custom-call | tf_op jit(solution)/shard_map/pallas_call | solution.py:67
  69.6 2.4 %all_to_all.16 = bf16[64,2,2560]{2,1,0:T(2,128)(2,1)S(1)} reshape(bf16[1024,320]{1,0:T(8,128)(2,1)} %shard_map.55) | data formatting | bytes 1310720 | tf_op jit(solution)/shard_map/all_to_all | solution.py:150
  72.1 25.9 %all_to_all.21 = bf16[64,2,2560]{2,1,0:T(2,128)(2,1)S(1)} all-to-all(bf16[64,2,2560]{2,1,0:T(2,128)(2,1)S(1)} %all_to_all.16), channel_id=1, replica_groups=mesh['wide'=64,'seq'=4] {'wide'}, dimensions={0} | all-to-all | bytes 1310720 | tf_op jit(solution)/shard_map/all_to_all | solution.py:150
  98.0 0.2 all_to_all.18
  98.2 0.3 convolution_convert_fusion
  98.5 0.3 reshape.103
  98.9 0.5 copy.11
  99.3 1.4 %bitcast_convert_fusion = bf16[64,2,128,4,8]{2,4,3,1,0:T(8,128)(2,1)} fusion(bf16[64,2,8,32]{2,3,1,0:T(8,128)(2,1)S(1)} %bitcast.48, bf16[64,8,320]{2,1,0:T(8,128)(2,1)S(1)} %reshape.103), kind=kOutput, calls=%fused_computation.13 | convolution fusion | flops 8912896 | bytes 2359296
  (8 shorter events, 0.1 us)
Async XLA Ops:
  0.0 42.2 %copy-start = (bf16[1,128,2048]{2,1,0:T(8,128)(2,1)S(1)}, bf16[1,128,2048]{2,1,0:T(8,128)(2,1)}, u32[]{:S(2)}) copy-start(bf16[1,128,2048]{2,1,0:T(8,128)(2,1)} %param.8) | copy-start | bytes 1572868
  2.5 7.0 %collective-permute-start.2 = (f32[32768]{0:T(1024)S(1)}, f32[32768]{0:T(1024)S(1)}, u32[]{:S(2)}, u32[]{:S(2)}) collective-permute-start(f32[32768]{0:T(1024)S(1)} %fusion.1), channel_id=1, source_target_pairs={{0,3},{1,0},{2,1},{3,2},{4,7},{5,4},{6,5},{7,6},{8,11},{9,8},{10,9... | collective-permute-start | bytes 393224 | tf_op jit(solution)/shard_map/ppermute | solution.py:106
  5.9 5.4 %collective-permute-start.1 = (f32[32768]{0:T(1024)S(1)}, f32[32768]{0:T(1024)S(1)}, u32[]{:S(2)}, u32[]{:S(2)}) collective-permute-start(f32[32768]{0:T(1024)S(1)} %fusion.1), channel_id=1, source_target_pairs={{0,2},{1,3},{2,0},{3,1},{4,6},{5,7},{6,4},{7,5},{8,10},{9,11},{10,... | collective-permute-start | bytes 393224 | tf_op jit(solution)/shard_map/ppermute | solution.py:106
  6.4 9.0 %collective-permute-start = (f32[32768]{0:T(1024)S(1)}, f32[32768]{0:T(1024)S(1)}, u32[]{:S(2)}, u32[]{:S(2)}) collective-permute-start(f32[32768]{0:T(1024)S(1)} %fusion.1), channel_id=1, source_target_pairs={{0,1},{1,2},{2,3},{3,0},{4,5},{5,6},{6,7},{7,4},{8,9},{9,10},{10,1... | collective-permute-start | bytes 393224 | tf_op jit(solution)/shard_map/ppermute | solution.py:106
  21.5 2.8 %collective-permute-start.5 = (bf16[2,64,128]{2,1,0:T(8,128)(2,1)S(1)}, bf16[2,64,128]{2,1,0:T(8,128)(2,1)S(1)}, u32[]{:S(2)}, u32[]{:S(2)}) collective-permute-start(bf16[2,64,128]{2,1,0:T(8,128)(2,1)S(1)} %get-tuple-element.8), channel_id=1, source_target_pairs={{0,3},{1,0},{2,1},{3,2},{4,7},{5,4},{6,5},{7,6},{8,11},{9,8},{10,9... | collective-permute-start | bytes 98312 | tf_op jit(solution)/shard_map/ppermute | solution.py:123
  21.6 4.4 %collective-permute-start.4 = (bf16[2,64,128]{2,1,0:T(8,128)(2,1)S(1)}, bf16[2,64,128]{2,1,0:T(8,128)(2,1)S(1)}, u32[]{:S(2)}, u32[]{:S(2)}) collective-permute-start(bf16[2,64,128]{2,1,0:T(8,128)(2,1)S(1)} %get-tuple-element.9), channel_id=1, source_target_pairs={{0,2},{1,3},{2,0},{3,1},{4,6},{5,7},{6,4},{7,5},{8,10},{9,11},{10,... | collective-permute-start | bytes 98312 | tf_op jit(solution)/shard_map/ppermute | solution.py:123
  21.9 4.9 %collective-permute-start.3 = (bf16[2,64,128]{2,1,0:T(8,128)(2,1)S(1)}, bf16[2,64,128]{2,1,0:T(8,128)(2,1)S(1)}, u32[]{:S(2)}, u32[]{:S(2)}) collective-permute-start(bf16[2,64,128]{2,1,0:T(8,128)(2,1)S(1)} %get-tuple-element.10), channel_id=1, source_target_pairs={{0,1},{1,2},{2,3},{3,0},{4,5},{5,6},{6,7},{7,4},{8,9},{9,10},{10,1... | collective-permute-start | bytes 98312 | tf_op jit(solution)/shard_map/ppermute | solution.py:123
  28.5 25.7 %all-to-all-start = ((bf16[64,2,1024]{2,1,0:T(2,128)(2,1)}), bf16[64,2,1024]{2,1,0:T(2,128)(2,1)S(1)}, u32[]{:S(2)}, u32[]{:S(2)}) async-start(bf16[64,2,1024]{2,1,0:T(2,128)(2,1)} %all_to_all.14), calls=%async_computation | async-start | bytes 524288 | tf_op jit(solution)/shard_map/all_to_all | solution.py:143

commit v9 on v8

--- a/solution.py
+++ b/solution.py
@@ -27,29 +27,36 @@
     )
     projected = projected.astype(jnp.bfloat16)
     o_ref[:, :value_width] = projected[:, (HEADS + KVH) * HD :]
-    projected = projected.astype(jnp.float32)
     row_patch = lax.broadcasted_iota(jnp.int32, (sub_rows, cols), 0) // BINS
     col_patch = lax.broadcasted_iota(jnp.int32, (sub_rows, cols), 1) // (group_size * BINS)
     same = row_patch == col_patch
+    ones = jnp.ones((8, HD), jnp.float32)
     for sg in range(rows_ref.shape[0] // sub_rows):
         base = sg * sub_rows
         xs = projected[base : base + sub_rows, :]
         for g in range(KVH):
             k = xs[:, (HEADS + g) * HD : (HEADS + g + 1) * HD]
-            k = k / jnp.sqrt(jnp.mean(k * k, axis=-1, keepdims=True) + 1e-06)
+            kf = k.astype(jnp.float32)
+            k_scale = 1.0 / jnp.sqrt(jnp.mean(kf * kf, axis=-1, keepdims=True) + 1e-06)
             pieces = []
             for p in range(SUB):
                 for r in range(group_size):
                     h = g * group_size + r
                     pieces.append(xs[p * BINS : (p + 1) * BINS, h * HD : (h + 1) * HD])
             q = jnp.concatenate(pieces, axis=0)
-            q = q / jnp.sqrt(jnp.mean(q * q, axis=-1, keepdims=True) + 1e-06)
-            s = lax.dot_general(
-                k, q, (((1,), (1,)), ((), ())), precision=lax.Precision.HIGHEST,
+            qf = q.astype(jnp.float32)
+            q_sums = lax.dot_general(
+                ones, qf * qf, (((1,), (1,)), ((), ())), precision=lax.Precision.HIGHEST,
                 preferred_element_type=jnp.float32,
-            ) / HD**0.5
+            )[0:1, :]
+            q_scale = 1.0 / jnp.sqrt(q_sums / HD + 1e-06)
+            raw = lax.dot_general(
+                k, q, (((1,), (1,)), ((), ())), preferred_element_type=jnp.float32
+            )
+            s = raw * k_scale * q_scale / HD**0.5
             e = jnp.where(same, jnp.exp(s), 0.0)
-            w = (e / jnp.sum(e, axis=0, keepdims=True)).astype(jnp.bfloat16).astype(jnp.float32)
+            total = jnp.sum(e, axis=0, keepdims=True)
+            w = (e * (1.0 / total)).astype(jnp.bfloat16).astype(jnp.float32)
             width = group_size * BINS
             for p in range(SUB):
                 tile = w[p * BINS : (p + 1) * BINS, :]
@@ -109,12 +116,10 @@
     inv_rms = 1.0 / jnp.sqrt(squares / (sample_rows * seq_count) + 1e-06)
     active = jnp.maximum(signal * inv_rms[None, :] - 0.8, 0.0)
     local_bins = bin_index - seq_index * bin_count
-    onehot = (local_bins[:, None] == jnp.arange(bin_count, dtype=jnp.int32)[None, :]).astype(
-        jnp.float32
-    )
-    binned = (jnp.dot(onehot.T, active, precision=lax.Precision.HIGHEST) * (1.0 / SPB)).astype(
-        jnp.bfloat16
-    )
+    sums = [
+        jnp.sum(jnp.where((local_bins == b)[:, None], active, 0.0), axis=0) for b in range(bin_count)
+    ]
+    binned = (jnp.stack(sums) * (1.0 / SPB)).astype(jnp.bfloat16)
     binned = binned.reshape(bin_count, seq_count, quarter, CH).transpose(1, 0, 2, 3)
     received = [lax.dynamic_index_in_dim(binned, seq_index, 0, keepdims=False)]
     for shift in range(1, seq_count):

time: 101 us -> 100 us (0.990)
  matrix products: 10.8 us -> 6.55 us
  other arithmetic: 5.2 us -> 8.82 us
    dot_general x1 -> x0, matrix products: 4.22 us -> none  [body(): jnp.dot(onehot.T, active, precision=lax.Precision.HIGHEST) * (1.0 / SPB)]
    reduce_sum x0 -> x1, other arithmetic: none -> 3.59 us  [body(): jnp.sum(jnp.where((local_bins == b)[:, None], active, 0.0), axis=0)]
where the time goes in v9:
time: 100 us; the launch traced here: 99.8 us
  blocking collectives  25.9 us (26%)
  starting transfers between devices  19.8 us (20%)
  waiting for transfers between devices  16.8 us (17%)
  Pallas kernels  14.3 us (14%)
  other arithmetic  8.82 us (9%)
  local copies, waits for them, and re-layouts  7.46 us (7%)
  matrix products  6.55 us (7%)
    all_to_all x1, blocking collectives, body(): lax.all_to_all(payload, 'wide', split_axis=0, concat_axis=0, tiled=True)  25.9 us
    pallas_call x1, Pallas kernels, owner_payload(): pl.pallas_call(_owner_kernel, out_shape=jax.ShapeDtypeStruct((total, KVH...  14.3 us
    all_to_all x1, starting transfers between devices, body(): lax.all_to_all(outgoing, 'wide', split_axis=0, concat_axis=0, tiled=True)  13.7 us
    all_to_all x1, waiting for transfers between devices, body(): lax.all_to_all(outgoing, 'wide', split_axis=0, concat_axis=0, tiled=True)  7.29 us
    ppermute x3, waiting for transfers between devices, body(): received.append(lax.ppermute(partial, 'seq', pairs))  6.74 us
    dot_general x1, matrix products, body(): jnp.dot(weight_block, qkv_weight, preferred_element_type=jnp.float32)  4.66 us
    ppermute x3, starting transfers between devices, body(): received.append(lax.ppermute(partial, 'seq', pairs))  4.5 us
    reduce_sum x1, other arithmetic, body(): jnp.sum(jnp.where((local_bins == b)[:, None], active, 0.0), axis=0)  3.59 us
  transfers between devices with their start and end apart: 7, of which 7 were waited for; matrix products, arithmetic and copies ran while one was open for 7% of the time, Pallas kernels for 0%

profile of v9, /device:TPU:1, one launch (start us, length us, event | category | flops | bytes accessed | tf_op | source)
XLA Modules:
  0.0 99.8 jit_solution(1998475377465511008)
XLA Ops:
  0.0 0.0 copy-start
  0.0 2.5 %fusion = f32[32768]{0:T(1024)S(1)} fusion(bf16[40,32768]{1,0:T(8,128)(2,1)} %param.5), kind=kLoop, calls=%fused_computation.4 | loop fusion | flops 3899392 | bytes 2752512 | tf_op jit(solution)/shard_map/reduce_sum | solution.py:109
  2.5 3.4 %collective-permute-start.2 = (f32[32768]{0:T(1024)S(1)}, f32[32768]{0:T(1024)S(1)}, u32[]{:S(2)}, u32[]{:S(2)}) collective-permute-start(f32[32768]{0:T(1024)S(1)} %fusion), channel_id=1, source_target_pairs={{0,3},{1,0},{2,1},{3,2},{4,7},{5,4},{6,5},{7,6},{8,11},{9,8},{10,9... | collective-permute-start | bytes 393224 | tf_op jit(solution)/shard_map/ppermute | solution.py:113
  5.9 0.5 collective-permute-start.1
  6.4 0.6 collective-permute-start
  7.0 0.7 subtract_compare_fusion
  7.8 0.8 dynamic_slice.10
  8.5 0.2 convert_reduce_fusion
  8.7 0.8 collective-permute-done.2
  9.5 1.8 %collective-permute-done.1 = f32[32768]{0:T(1024)S(1)} collective-permute-done((f32[32768]{0:T(1024)S(1)}, f32[32768]{0:T(1024)S(1)}, u32[]{:S(2)}, u32[]{:S(2)}) %collective-permute-start.1) | collective-permute-done | bytes 131104 | tf_op jit(solution)/shard_map/ppermute | solution.py:113
  11.3 4.1 %collective-permute-done = f32[32768]{0:T(1024)S(1)} collective-permute-done((f32[32768]{0:T(1024)S(1)}, f32[32768]{0:T(1024)S(1)}, u32[]{:S(2)}, u32[]{:S(2)}) %collective-permute-start) | collective-permute-done | bytes 131104 | tf_op jit(solution)/shard_map/ppermute | solution.py:113
  15.5 0.5 pad_maximum_fusion
  16.0 0.8 gather_fusion
  16.8 0.4 select_reduce_fusion
  17.2 3.6 %fusion.5 = (f32[32768]{0:T(1024)S(1)}, f32[32768]{0:T(1024)S(1)}) fusion(bf16[40,32768]{1,0:T(8,128)(2,1)} %param.5, f32[32768]{0:T(1024)S(1)} %add_rsqrt_fusion, pred[40]{0:T(512)(128)(4,1)S(1)} %get-tuple-element.14, pred[40]{0:T(512)(128)(4,1)S(1)} %get-tuple-element.13), kind=kLoop, calls=%fused_computation.9 | loop fusion | flops 10420224 | bytes 3014736 | tf_op jit(solution)/shard_map/reduce_sum | solution.py:120
  20.9 0.1 collective-permute-start.5
  21.0 0.2 collective-permute-start.4
  21.2 1.2 %collective-permute-start.3 = (bf16[2,64,128]{2,1,0:T(8,128)(2,1)S(1)}, bf16[2,64,128]{2,1,0:T(8,128)(2,1)S(1)}, u32[]{:S(2)}, u32[]{:S(2)}) collective-permute-start(bf16[2,64,128]{2,1,0:T(8,128)(2,1)S(1)} %get-tuple-element.12), channel_id=1, source_target_pairs={{0,1},{1,2},{2,3},{3,0},{4,5},{5,6},{6,7},{7,4},{8,9},{9,10},{10,1... | collective-permute-start | bytes 98312 | tf_op jit(solution)/shard_map/ppermute | solution.py:128
  22.4 0.8 multiply_add_fusion
  23.2 0.1 broadcast_in_dim.49
  23.3 0.1 broadcast_in_dim.50
  23.4 0.4 collective-permute-done.5
  23.7 1.6 %collective-permute-done.4 = bf16[2,64,128]{2,1,0:T(8,128)(2,1)S(1)} collective-permute-done((bf16[2,64,128]{2,1,0:T(8,128)(2,1)S(1)}, bf16[2,64,128]{2,1,0:T(8,128)(2,1)S(1)}, u32[]{:S(2)}, u32[]{:S(2)}) %collective-permute-start.4) | collective-permute-done | bytes 32800 | tf_op jit(solution)/shard_map/ppermute | solution.py:128
  25.3 0.8 collective-permute-done.3
  26.2 0.6 gather_fusion.1
  26.7 0.1 copy_select_fusion
  26.8 0.2 convolution_convert_fusion.1
  27.0 0.8 all_to_all.14
  27.8 13.7 %all-to-all-start = ((bf16[64,2,1024]{2,1,0:T(2,128)(2,1)}), bf16[64,2,1024]{2,1,0:T(2,128)(2,1)S(1)}, u32[]{:S(2)}, u32[]{:S(2)}) async-start(bf16[64,2,1024]{2,1,0:T(2,128)(2,1)} %all_to_all.14), calls=%async_computation | async-start | bytes 524288 | tf_op jit(solution)/shard_map/all_to_all | solution.py:148
  41.6 0.0 copy-done
  41.6 4.7 %subtract_convert_fusion = (bf16[128,1536]{1,0:T(8,128)(2,1)}, bf16[128,1536]{1,0:T(8,128)(2,1)}) fusion(bf16[2048,1536]{1,0:T(8,128)(2,1)} %param.9, bf16[1,128,2048]{2,1,0:T(8,128)(2,1)S(1)} %copy-done), kind=kOutput, calls=%fused_computation.14 | convolution fusion | flops 806092800 | bytes 7602176 | tf_op jit(solution)/shard_map/dot_general | solution.py:150
  46.3 7.3 %all-to-all-done = bf16[64,2,1024]{2,1,0:T(2,128)(2,1)S(1)} async-done(((bf16[64,2,1024]{2,1,0:T(2,128)(2,1)}), bf16[64,2,1024]{2,1,0:T(2,128)(2,1)S(1)}, u32[]{:S(2)}, u32[]{:S(2)}) %all-to-all-start) | async-done | bytes 262176 | tf_op jit(solution)/shard_map/all_to_all | solution.py:148
  53.6 0.9 reshape.104.rows_ref
  54.4 14.3 %shard_map.55 = bf16[1024,320]{1,0:T(8,128)(2,1)} custom-call(bf16[1024,128]{1,0:T(8,128)(2,1)} %reshape.104.rows_ref, bf16[128,1536]{1,0:T(8,128)(2,1)} %get-tuple-element.8.hi_ref, bf16[128,1536]{1,0:T(8,128)(2,1)} %get-tuple-element.7.lo_ref), custom_call_target="tpu_custom_call" | custom-call | tf_op jit(solution)/shard_map/pallas_call | solution.py:74
  68.7 2.4 %all_to_all.16 = bf16[64,2,2560]{2,1,0:T(2,128)(2,1)S(1)} reshape(bf16[1024,320]{1,0:T(8,128)(2,1)} %shard_map.55) | data formatting | bytes 1310720 | tf_op jit(solution)/shard_map/all_to_all | solution.py:155
  71.2 25.9 %all_to_all.21 = bf16[64,2,2560]{2,1,0:T(2,128)(2,1)S(1)} all-to-all(bf16[64,2,2560]{2,1,0:T(2,128)(2,1)S(1)} %all_to_all.16), channel_id=1, replica_groups=mesh['wide'=64,'seq'=4] {'wide'}, dimensions={0} | all-to-all | bytes 1310720 | tf_op jit(solution)/shard_map/all_to_all | solution.py:155
  97.1 0.2 all_to_all.18
  97.3 0.3 convolution_convert_fusion
  97.6 0.3 reshape.105
  98.0 0.5 copy.11
  98.4 1.4 %bitcast_convert_fusion = bf16[64,2,128,4,8]{2,4,3,1,0:T(8,128)(2,1)} fusion(bf16[64,2,8,32]{2,3,1,0:T(8,128)(2,1)S(1)} %bitcast.46, bf16[64,8,320]{2,1,0:T(8,128)(2,1)S(1)} %reshape.105), kind=kOutput, calls=%fused_computation.12 | convolution fusion | flops 8912896 | bytes 2359296
  (8 shorter events, 0.1 us)
Async XLA Ops:
  0.0 41.6 %copy-start = (bf16[1,128,2048]{2,1,0:T(8,128)(2,1)S(1)}, bf16[1,128,2048]{2,1,0:T(8,128)(2,1)}, u32[]{:S(2)}) copy-start(bf16[1,128,2048]{2,1,0:T(8,128)(2,1)} %param.8) | copy-start | bytes 1572868
  2.5 7.0 %collective-permute-start.2 = (f32[32768]{0:T(1024)S(1)}, f32[32768]{0:T(1024)S(1)}, u32[]{:S(2)}, u32[]{:S(2)}) collective-permute-start(f32[32768]{0:T(1024)S(1)} %fusion), channel_id=1, source_target_pairs={{0,3},{1,0},{2,1},{3,2},{4,7},{5,4},{6,5},{7,6},{8,11},{9,8},{10,9... | collective-permute-start | bytes 393224 | tf_op jit(solution)/shard_map/ppermute | solution.py:113
  5.9 5.4 %collective-permute-start.1 = (f32[32768]{0:T(1024)S(1)}, f32[32768]{0:T(1024)S(1)}, u32[]{:S(2)}, u32[]{:S(2)}) collective-permute-start(f32[32768]{0:T(1024)S(1)} %fusion), channel_id=1, source_target_pairs={{0,2},{1,3},{2,0},{3,1},{4,6},{5,7},{6,4},{7,5},{8,10},{9,11},{10,... | collective-permute-start | bytes 393224 | tf_op jit(solution)/shard_map/ppermute | solution.py:113
  6.4 9.0 %collective-permute-start = (f32[32768]{0:T(1024)S(1)}, f32[32768]{0:T(1024)S(1)}, u32[]{:S(2)}, u32[]{:S(2)}) collective-permute-start(f32[32768]{0:T(1024)S(1)} %fusion), channel_id=1, source_target_pairs={{0,1},{1,2},{2,3},{3,0},{4,5},{5,6},{6,7},{7,4},{8,9},{9,10},{10,1... | collective-permute-start | bytes 393224 | tf_op jit(solution)/shard_map/ppermute | solution.py:113
  20.9 2.8 %collective-permute-start.5 = (bf16[2,64,128]{2,1,0:T(8,128)(2,1)S(1)}, bf16[2,64,128]{2,1,0:T(8,128)(2,1)S(1)}, u32[]{:S(2)}, u32[]{:S(2)}) collective-permute-start(bf16[2,64,128]{2,1,0:T(8,128)(2,1)S(1)} %get-tuple-element.10), channel_id=1, source_target_pairs={{0,3},{1,0},{2,1},{3,2},{4,7},{5,4},{6,5},{7,6},{8,11},{9,8},{10,9... | collective-permute-start | bytes 98312 | tf_op jit(solution)/shard_map/ppermute | solution.py:128
  21.0 4.4 %collective-permute-start.4 = (bf16[2,64,128]{2,1,0:T(8,128)(2,1)S(1)}, bf16[2,64,128]{2,1,0:T(8,128)(2,1)S(1)}, u32[]{:S(2)}, u32[]{:S(2)}) collective-permute-start(bf16[2,64,128]{2,1,0:T(8,128)(2,1)S(1)} %get-tuple-element.11), channel_id=1, source_target_pairs={{0,2},{1,3},{2,0},{3,1},{4,6},{5,7},{6,4},{7,5},{8,10},{9,11},{10,... | collective-permute-start | bytes 98312 | tf_op jit(solution)/shard_map/ppermute | solution.py:128
  21.2 4.9 %collective-permute-start.3 = (bf16[2,64,128]{2,1,0:T(8,128)(2,1)S(1)}, bf16[2,64,128]{2,1,0:T(8,128)(2,1)S(1)}, u32[]{:S(2)}, u32[]{:S(2)}) collective-permute-start(bf16[2,64,128]{2,1,0:T(8,128)(2,1)S(1)} %get-tuple-element.12), channel_id=1, source_target_pairs={{0,1},{1,2},{2,3},{3,0},{4,5},{5,6},{6,7},{7,4},{8,9},{9,10},{10,1... | collective-permute-start | bytes 98312 | tf_op jit(solution)/shard_map/ppermute | solution.py:128
  27.8 25.7 %all-to-all-start = ((bf16[64,2,1024]{2,1,0:T(2,128)(2,1)}), bf16[64,2,1024]{2,1,0:T(2,128)(2,1)S(1)}, u32[]{:S(2)}, u32[]{:S(2)}) async-start(bf16[64,2,1024]{2,1,0:T(2,128)(2,1)} %all_to_all.14), calls=%async_computation | async-start | bytes 524288 | tf_op jit(solution)/shard_map/all_to_all | solution.py:148

commit v10 on v9

--- a/solution.py
+++ b/solution.py
@@ -94,10 +94,38 @@
     return mixed.reshape(n, BINS, HEADS * HD).astype(jnp.bfloat16)
 
 
+WIDE_AXES = ("y", "z", "core")
+
+
+def relative_exchange(x, sizes):
+    ny, nz, nc = sizes
+    moved = [x[:, 0]]
+    for d in range(1, nz):
+        moved.append(lax.ppermute(x[:, d], "z", [(i, (i + d) % nz) for i in range(nz)]))
+    x = jnp.stack(moved)
+    moved = [x[:, 0]]
+    for d in range(1, ny):
+        moved.append(lax.ppermute(x[:, d], "y", [(i, (i + d) % ny) for i in range(ny)]))
+    x = jnp.stack(moved)
+    moved = [x[:, :, 0]]
+    for d in range(1, nc):
+        moved.append(lax.ppermute(x[:, :, d], "core", [(i, (i + d) % nc) for i in range(nc)]))
+    return jnp.stack(moved)
+
+
+def negate_offsets(x, axis):
+    head = lax.slice_in_dim(x, 0, 1, axis=axis)
+    tail = jnp.flip(lax.slice_in_dim(x, 1, x.shape[axis], axis=axis), axis=axis)
+    return jnp.concatenate([head, tail], axis=axis)
+
+
 def body(power, bin_index, session, readin_weight, qkv_weight):
-    wide_count = lax.axis_size("wide")
+    sizes = tuple(lax.axis_size(name) for name in WIDE_AXES)
+    ny, nz, nc = sizes
+    wide_count = ny * nz * nc
     seq_count = lax.axis_size("seq")
-    wide_index = lax.axis_index("wide")
+    my_y, my_z, my_c = (lax.axis_index(name) for name in WIDE_AXES)
+    wide_index = (my_y * nz + my_z) * nc + my_c
     seq_index = lax.axis_index("seq")
     sample_rows, channels = power.shape
     patch_count = channels // CH
@@ -137,28 +165,41 @@
     same = owners[:, None] == owners[None, :]
     earlier = jnp.arange(quarter)[None, :] < jnp.arange(quarter)[:, None]
     rank = jnp.sum((same & earlier).astype(jnp.int32), axis=1)
-    slot = owners * CAP + rank
+    owner_y = owners // (nz * nc)
+    owner_z = (owners // nc) % nz
+    owner_c = owners % nc
+    ahead = (((owner_y - my_y) % ny) * nz + (owner_z - my_z) % nz) * nc + (owner_c - my_c) % nc
+    behind = (((my_c - owner_c) % nc) * ny + (my_y - owner_y) % ny) * nz + (my_z - owner_z) % nz
     slot_count = wide_count * CAP
-    dispatch = (jnp.arange(slot_count, dtype=jnp.int32)[:, None] == slot[None, :]).astype(
-        jnp.bfloat16
-    )
+    slot_ids = jnp.arange(slot_count, dtype=jnp.int32)[:, None]
+    dispatch = (slot_ids == (ahead * CAP + rank)[None, :]).astype(jnp.bfloat16)
+    collect = (slot_ids == (behind * CAP + rank)[None, :]).astype(jnp.bfloat16)
     outgoing = jnp.dot(dispatch, block_rows, preferred_element_type=jnp.float32).astype(
         jnp.bfloat16
     )
-    arrived = lax.all_to_all(outgoing, "wide", split_axis=0, concat_axis=0, tiled=True)
+    arrived = relative_exchange(outgoing.reshape(ny, nz, nc, CAP, -1), sizes)
+    arrived = jnp.transpose(arrived, (1, 2, 0, 3, 4))
+    for axis in range(3):
+        arrived = negate_offsets(arrived, axis)
     weight_block = readin_weight[0]
     merged = jnp.dot(weight_block, qkv_weight, preferred_element_type=jnp.float32)
     merged_hi = merged.astype(jnp.bfloat16)
     merged_lo = (merged - merged_hi.astype(jnp.float32)).astype(jnp.bfloat16)
     rows = arrived.reshape(slot_count * all_bins, CH)
     payload = owner_payload(rows, merged_hi, merged_lo).reshape(slot_count, -1)
-    returned = lax.all_to_all(payload, "wide", split_axis=0, concat_axis=0, tiled=True)
-    mine = jnp.dot(dispatch.T, returned, preferred_element_type=jnp.float32).astype(jnp.bfloat16)
+    returned = relative_exchange(payload.reshape(ny, nz, nc, CAP, -1), sizes)
+    returned = returned.reshape(slot_count, -1)
+    mine = jnp.dot(collect.T, returned, preferred_element_type=jnp.float32).astype(jnp.bfloat16)
     return heads_from(mine.reshape(quarter, all_bins, -1))
 
 
 def solution(mesh):
-    placed = (P("seq", "wide"), P("seq"), P(), P("wide", None, None), P())
+    sizes = (4, 8, 2)
+    wide_total, seq_total = mesh.devices.shape
+    assert sizes[0] * sizes[1] * sizes[2] == wide_total
+    split = jax.sharding.Mesh(mesh.devices.reshape(*sizes, seq_total), WIDE_AXES + ("seq",))
+    placed = (P("seq", WIDE_AXES), P("seq"), P(), P(WIDE_AXES, None, None), P())
     return jax.shard_map(
-        body, mesh=mesh, in_specs=placed, out_specs=P(("wide", "seq"), None, None), check_vma=False
-    )
+        body, mesh=split, in_specs=placed, out_specs=P(WIDE_AXES + ("seq",), None, None),
+        check_vma=False,
+    )

time: 100 us -> 136 us (1.36); the launches traced: 99.8 us -> 134 us
  starting transfers between devices: 19.8 us -> 49.8 us
  blocking collectives: 25.9 us -> 0 us
  waiting for transfers between devices: 16.8 us -> 40.3 us
  other arithmetic: 8.82 us -> 13.1 us
  local copies, waits for them, and re-layouts: 7.46 us -> 9.86 us
    ppermute x0 -> x22, starting transfers between devices: none -> 43.7 us  [the longest x14 26.4 us: relative_exchange(): lax.ppermute(x[:, d], 'z', [(i, (i + d) % nz) for i in range(nz)])]
    ppermute x0 -> x22, waiting for transfers between devices: none -> 31.7 us  [the longest x14 19.7 us: relative_exchange(): lax.ppermute(x[:, d], 'z', [(i, (i + d) % nz) for i in range(nz)])]
    all_to_all x1 -> x0, blocking collectives: 25.9 us -> none  [body(): lax.all_to_all(payload, 'wide', split_axis=0, concat_axis=0, tiled=True)]
    all_to_all x1 -> x0, starting transfers between devices: 13.7 us -> none  [body(): lax.all_to_all(outgoing, 'wide', split_axis=0, concat_axis=0, tiled=True)]
    all_to_all x1 -> x0, waiting for transfers between devices: 7.29 us -> none  [body(): lax.all_to_all(outgoing, 'wide', split_axis=0, concat_axis=0, tiled=True)]
    another operation x0 -> x7, local copies, waits for them, and re-layouts: none -> 3.8 us  [the longest x1 2.43 us: body(): returned = relative_exchange(payload.reshape(ny, nz, nc, CAP, -1), sizes)]
    all_to_all x3 -> x0, local copies, waits for them, and re-layouts: 3.48 us -> none  [the longest x2 2.67 us: body(): lax.all_to_all(payload, 'wide', split_axis=0, concat_axis=0, tiled=True)]
    another operation x0 -> x3, other arithmetic: none -> 2.59 us  [the longest x2 1.67 us: relative_exchange(): x = jnp.stack(moved)]
  transfers between devices with their start and end apart: 7 -> 28, of which waited for: 7 -> 16; matrix products, arithmetic and copies ran while one was open for 7% -> 6% of each run, Pallas kernels for 0% -> 0%
where the time goes in v10:
time: 136 us; the launch traced here: 134 us
  starting transfers between devices  49.8 us (37%)
  waiting for transfers between devices  40.3 us (30%)
  Pallas kernels  14.3 us (11%)
  other arithmetic  13.1 us (10%)
  local copies, waits for them, and re-layouts  9.86 us (7%)
  matrix products  6.55 us (5%)
    ppermute x14, starting transfers between devices, relative_exchange(): lax.ppermute(x[:, d], 'z', [(i, (i + d) % nz) for i in range(nz)])  26.4 us
    ppermute x14, waiting for transfers between devices, relative_exchange(): lax.ppermute(x[:, d], 'z', [(i, (i + d) % nz) for i in range(nz)])  19.7 us
    pallas_call x1, Pallas kernels, owner_payload(): pl.pallas_call(_owner_kernel, out_shape=jax.ShapeDtypeStruct((total, KVH...  14.3 us
    ppermute x2, starting transfers between devices, relative_exchange(): lax.ppermute(x[:, :, d], 'core', [(i, (i + d) % nc) for i in range(nc)])  10.8 us
    ppermute x6, waiting for transfers between devices, relative_exchange(): lax.ppermute(x[:, d], 'y', [(i, (i + d) % ny) for i in range(ny)])  10.8 us
    ppermute x6, starting transfers between devices, relative_exchange(): lax.ppermute(x[:, d], 'y', [(i, (i + d) % ny) for i in range(ny)])  6.6 us
    ppermute x3, waiting for transfers between devices, body(): received.append(lax.ppermute(partial, 'seq', pairs))  5.93 us
    dot_general x1, matrix products, body(): jnp.dot(weight_block, qkv_weight, preferred_element_type=jnp.float32)  4.66 us
  transfers between devices with their start and end apart: 28, of which 16 were waited for; matrix products, arithmetic and copies ran while one was open for 6% of the time, Pallas kernels for 0%

profile of v10, /device:TPU:1, one launch (start us, length us, event | category | flops | bytes accessed | tf_op | source)
XLA Modules:
  0.0 134.4 jit_solution(8806541553165919340)
XLA Ops:
  0.0 2.5 %fusion = f32[32768]{0:T(1024)S(1)} fusion(bf16[40,32768]{1,0:T(8,128)(2,1)} %param.5), kind=kLoop, calls=%fused_computation.4 | loop fusion | flops 3899392 | bytes 2752512 | tf_op jit(solution)/shard_map/reduce_sum | solution.py:137
  2.5 3.4 %collective-permute-start.2 = (f32[32768]{0:T(1024)S(1)}, f32[32768]{0:T(1024)S(1)}, u32[]{:S(2)}, u32[]{:S(2)}) collective-permute-start(f32[32768]{0:T(1024)S(1)} %fusion), channel_id=1, source_target_pairs={{0,3},{1,0},{2,1},{3,2},{4,7},{5,4},{6,5},{7,6},{8,11},{9,8},{10,9... | collective-permute-start | bytes 393224 | tf_op jit(solution)/shard_map/ppermute | solution.py:141
  6.4 0.6 collective-permute-start
  7.1 0.8 dynamic_slice.10
  8.0 0.8 multiply_add_fusion.1
  8.8 0.7 subtract_compare_fusion
  9.5 1.8 %collective-permute-done.1 = f32[32768]{0:T(1024)S(1)} collective-permute-done((f32[32768]{0:T(1024)S(1)}, f32[32768]{0:T(1024)S(1)}, u32[]{:S(2)}, u32[]{:S(2)}) %collective-permute-start.1) | collective-permute-done | bytes 131104 | tf_op jit(solution)/shard_map/ppermute | solution.py:141
  11.3 4.1 %collective-permute-done = f32[32768]{0:T(1024)S(1)} collective-permute-done((f32[32768]{0:T(1024)S(1)}, f32[32768]{0:T(1024)S(1)}, u32[]{:S(2)}, u32[]{:S(2)}) %collective-permute-start) | collective-permute-done | bytes 131104 | tf_op jit(solution)/shard_map/ppermute | solution.py:141
  16.0 0.8 gather_fusion
  17.2 3.6 %fusion.5 = (f32[32768]{0:T(1024)S(1)}, f32[32768]{0:T(1024)S(1)}) fusion(bf16[40,32768]{1,0:T(8,128)(2,1)} %param.5, f32[32768]{0:T(1024)S(1)} %add_rsqrt_fusion, pred[40]{0:T(512)(128)(4,1)S(1)} %get-tuple-element.42, pred[40]{0:T(512)(128)(4,1)S(1)} %get-tuple-element.41), kind=kLoop, calls=%fused_computation.9 | loop fusion | flops 10420224 | bytes 3014736 | tf_op jit(solution)/shard_map/reduce_sum | solution.py:148
  21.2 1.2 collective-permute-start.3
  22.4 0.8 multiply_add_fusion
  23.7 1.6 %collective-permute-done.4 = bf16[2,64,128]{2,1,0:T(8,128)(2,1)S(1)} collective-permute-done((bf16[2,64,128]{2,1,0:T(8,128)(2,1)S(1)}, bf16[2,64,128]{2,1,0:T(8,128)(2,1)S(1)}, u32[]{:S(2)}, u32[]{:S(2)}) %collective-permute-start.4) | collective-permute-done | bytes 32800 | tf_op jit(solution)/shard_map/ppermute | solution.py:156
  25.3 0.8 collective-permute-done.3
  26.2 0.6 gather_fusion.1
  27.3 1.7 %collective-permute-start.6 = (bf16[4,2,2,1024]{3,2,1,0:T(2,128)(2,1)S(1)}, bf16[4,2,2,1024]{3,2,1,0:T(2,128)(2,1)S(1)}, u32[]{:S(2)}, u32[]{:S(2)}) collective-permute-start(bf16[4,2,2,1024]{3,2,1,0:T(2,128)(2,1)S(1)} %get-tuple-element.36), channel_id=1, source_target_pairs={{0,8},{8,16},{16,24},{24,32},{32,40},{40,48},{48,56},{56,0},{1,9},... | collective-permute-start | bytes 98312 | tf_op jit(solution)/shard_map/ppermute | solution.py:104
  29.1 4.0 %collective-permute-start.12 = (bf16[4,2,2,1024]{3,2,1,0:T(2,128)(2,1)S(1)}, bf16[4,2,2,1024]{3,2,1,0:T(2,128)(2,1)S(1)}, u32[]{:S(2)}, u32[]{:S(2)}) collective-permute-start(bf16[4,2,2,1024]{3,2,1,0:T(2,128)(2,1)S(1)} %get-tuple-element.30), channel_id=1, source_target_pairs={{0,56},{8,0},{16,8},{24,16},{32,24},{40,32},{48,40},{56,48},{1,57}... | collective-permute-start | bytes 98312 | tf_op jit(solution)/shard_map/ppermute | solution.py:104
  33.1 1.9 %collective-permute-start.11 = (bf16[4,2,2,1024]{3,2,1,0:T(2,128)(2,1)S(1)}, bf16[4,2,2,1024]{3,2,1,0:T(2,128)(2,1)S(1)}, u32[]{:S(2)}, u32[]{:S(2)}) collective-permute-start(bf16[4,2,2,1024]{3,2,1,0:T(2,128)(2,1)S(1)} %get-tuple-element.31), channel_id=1, source_target_pairs={{0,48},{8,56},{16,0},{24,8},{32,16},{40,24},{48,32},{56,40},{1,49}... | collective-permute-start | bytes 98312 | tf_op jit(solution)/shard_map/ppermute | solution.py:104
  35.0 2.2 %collective-permute-start.10 = (bf16[4,2,2,1024]{3,2,1,0:T(2,128)(2,1)S(1)}, bf16[4,2,2,1024]{3,2,1,0:T(2,128)(2,1)S(1)}, u32[]{:S(2)}, u32[]{:S(2)}) collective-permute-start(bf16[4,2,2,1024]{3,2,1,0:T(2,128)(2,1)S(1)} %get-tuple-element.32), channel_id=1, source_target_pairs={{0,40},{8,48},{16,56},{24,0},{32,8},{40,16},{48,24},{56,32},{1,41}... | collective-permute-start | bytes 98312 | tf_op jit(solution)/shard_map/ppermute | solution.py:104
  37.2 2.7 %collective-permute-start.9 = (bf16[4,2,2,1024]{3,2,1,0:T(2,128)(2,1)S(1)}, bf16[4,2,2,1024]{3,2,1,0:T(2,128)(2,1)S(1)}, u32[]{:S(2)}, u32[]{:S(2)}) collective-permute-start(bf16[4,2,2,1024]{3,2,1,0:T(2,128)(2,1)S(1)} %get-tuple-element.33), channel_id=1, source_target_pairs={{0,32},{8,40},{16,48},{24,56},{32,0},{40,8},{48,16},{56,24},{1,33}... | collective-permute-start | bytes 98312 | tf_op jit(solution)/shard_map/ppermute | solution.py:104
  40.0 5.1 %collective-permute-done.7 = bf16[4,2,2,1024]{3,2,1,0:T(2,128)(2,1)S(1)} collective-permute-done((bf16[4,2,2,1024]{3,2,1,0:T(2,128)(2,1)S(1)}, bf16[4,2,2,1024]{3,2,1,0:T(2,128)(2,1)S(1)}, u32[]{:S(2)}, u32[]{:S(2)}) %collective-permute-start.7) | collective-permute-done | bytes 32800 | tf_op jit(solution)/shard_map/ppermute | solution.py:104
  45.3 5.5 %collective-permute-done.8 = bf16[4,2,2,1024]{3,2,1,0:T(2,128)(2,1)S(1)} collective-permute-done((bf16[4,2,2,1024]{3,2,1,0:T(2,128)(2,1)S(1)}, bf16[4,2,2,1024]{3,2,1,0:T(2,128)(2,1)S(1)}, u32[]{:S(2)}, u32[]{:S(2)}) %collective-permute-start.8) | collective-permute-done | bytes 32800 | tf_op jit(solution)/shard_map/ppermute | solution.py:104
  51.3 2.8 %collective-permute-start.15 = (bf16[8,2,2,1024]{3,2,0,1:T(2,128)(2,1)S(1)}, bf16[8,2,2,1024]{3,2,0,1:T(2,128)(2,1)S(1)}, u32[]{:S(2)}, u32[]{:S(2)}) collective-permute-start(bf16[8,2,2,1024]{3,2,0,1:T(2,128)(2,1)S(1)} %get-tuple-element.27), channel_id=1, source_target_pairs={{0,192},{64,0},{128,64},{192,128},{1,193},{65,1},{129,65},{193,129... | collective-permute-start | bytes 196616 | tf_op jit(solution)/shard_map/ppermute | solution.py:108
  54.4 0.7 collective-permute-start.13
  55.4 3.4 %collective-permute-done.14 = bf16[8,2,2,1024]{3,2,0,1:T(2,128)(2,1)S(1)} collective-permute-done((bf16[8,2,2,1024]{3,2,0,1:T(2,128)(2,1)S(1)}, bf16[8,2,2,1024]{3,2,0,1:T(2,128)(2,1)S(1)}, u32[]{:S(2)}, u32[]{:S(2)}) %collective-permute-start.14) | collective-permute-done | bytes 65568 | tf_op jit(solution)/shard_map/ppermute | solution.py:108
  58.8 0.6 collective-permute-done.13
  60.1 7.1 %collective-permute-start.16 = (bf16[4,8,2,1024]{3,2,1,0:T(2,128)(2,1)S(1)}, bf16[4,8,2,1024]{3,2,1,0:T(2,128)(2,1)S(1)}, u32[]{:S(2)}, u32[]{:S(2)}) collective-permute-start(bf16[4,8,2,1024]{3,2,1,0:T(2,128)(2,1)S(1)} %get-tuple-element.25), channel_id=1, source_target_pairs={{0,4},{4,0},{1,5},{5,1},{2,6},{6,2},{3,7},{7,3},{8,12},{12,8},{9,1... | collective-permute-start | bytes 393224 | tf_op jit(solution)/shard_map/ppermute | solution.py:112
  67.1 4.7 %subtract_convert_fusion = (bf16[128,1536]{1,0:T(8,128)(2,1)}, bf16[128,1536]{1,0:T(8,128)(2,1)}) fusion(bf16[2048,1536]{1,0:T(8,128)(2,1)} %param.9, bf16[1,128,2048]{2,1,0:T(8,128)(2,1)S(1)} %copy-done), kind=kOutput, calls=%fused_computation.14 | convolution fusion | flops 806092800 | bytes 7602176 | tf_op jit(solution)/shard_map/dot_general | solution.py:185
  73.2 0.9 reshape.105.rows_ref
  74.1 14.3 %shard_map.55 = bf16[1024,320]{1,0:T(8,128)(2,1)} custom-call(bf16[1024,128]{1,0:T(8,128)(2,1)} %reshape.105.rows_ref, bf16[128,1536]{1,0:T(8,128)(2,1)} %get-tuple-element.10.hi_ref, bf16[128,1536]{1,0:T(8,128)(2,1)} %get-tuple-element.9.lo_ref), custom_call_target="tpu_custom_call" | custom-call | tf_op jit(solution)/shard_map/pallas_call | solution.py:74
  88.4 2.4 %reshape_reshape.3 = bf16[4,8,2,2,2560]{4,3,2,1,0:T(2,128)(2,1)S(1)} reshape(bf16[1024,320]{1,0:T(8,128)(2,1)} %shard_map.55) | data formatting | bytes 1310720 | tf_op jit(solution)/shard_map/reshape;reshape | solution.py:190
  91.4 2.9 %collective-permute-start.23 = (bf16[4,2,2,2560]{3,2,1,0:T(2,128)(2,1)S(1)}, bf16[4,2,2,2560]{3,2,1,0:T(2,128)(2,1)S(1)}, u32[]{:S(2)}, u32[]{:S(2)}) collective-permute-start(bf16[4,2,2,2560]{3,2,1,0:T(2,128)(2,1)S(1)} %get-tuple-element.17), channel_id=1, source_target_pairs={{0,56},{8,0},{16,8},{24,16},{32,24},{40,32},{48,40},{56,48},{1,57}... | collective-permute-start | bytes 245768 | tf_op jit(solution)/shard_map/ppermute | solution.py:104
  94.3 1.6 %collective-permute-start.21 = (bf16[4,2,2,2560]{3,2,1,0:T(2,128)(2,1)S(1)}, bf16[4,2,2,2560]{3,2,1,0:T(2,128)(2,1)S(1)}, u32[]{:S(2)}, u32[]{:S(2)}) collective-permute-start(bf16[4,2,2,2560]{3,2,1,0:T(2,128)(2,1)S(1)} %get-tuple-element.18), channel_id=1, source_target_pairs={{0,40},{8,48},{16,56},{24,0},{32,8},{40,16},{48,24},{56,32},{1,41}... | collective-permute-start | bytes 245768 | tf_op jit(solution)/shard_map/ppermute | solution.py:104
  95.9 1.5 %collective-permute-start.20 = (bf16[4,2,2,2560]{3,2,1,0:T(2,128)(2,1)S(1)}, bf16[4,2,2,2560]{3,2,1,0:T(2,128)(2,1)S(1)}, u32[]{:S(2)}, u32[]{:S(2)}) collective-permute-start(bf16[4,2,2,2560]{3,2,1,0:T(2,128)(2,1)S(1)} %get-tuple-element.19), channel_id=1, source_target_pairs={{0,32},{8,40},{16,48},{24,56},{32,0},{40,8},{48,16},{56,24},{1,33}... | collective-permute-start | bytes 245768 | tf_op jit(solution)/shard_map/ppermute | solution.py:104
  97.4 2.5 %collective-permute-start.19 = (bf16[4,2,2,2560]{3,2,1,0:T(2,128)(2,1)S(1)}, bf16[4,2,2,2560]{3,2,1,0:T(2,128)(2,1)S(1)}, u32[]{:S(2)}, u32[]{:S(2)}) collective-permute-start(bf16[4,2,2,2560]{3,2,1,0:T(2,128)(2,1)S(1)} %get-tuple-element.20), channel_id=1, source_target_pairs={{0,24},{8,32},{16,40},{24,48},{32,56},{40,0},{48,8},{56,16},{1,25}... | collective-permute-start | bytes 245768 | tf_op jit(solution)/shard_map/ppermute | solution.py:104
  99.9 1.4 %collective-permute-start.18 = (bf16[4,2,2,2560]{3,2,1,0:T(2,128)(2,1)S(1)}, bf16[4,2,2,2560]{3,2,1,0:T(2,128)(2,1)S(1)}, u32[]{:S(2)}, u32[]{:S(2)}) collective-permute-start(bf16[4,2,2,2560]{3,2,1,0:T(2,128)(2,1)S(1)} %get-tuple-element.21), channel_id=1, source_target_pairs={{0,16},{8,24},{16,32},{24,40},{32,48},{40,56},{48,0},{56,8},{1,17}... | collective-permute-start | bytes 245768 | tf_op jit(solution)/shard_map/ppermute | solution.py:104
  101.4 7.8 %collective-permute-done.18 = bf16[4,2,2,2560]{3,2,1,0:T(2,128)(2,1)S(1)} collective-permute-done((bf16[4,2,2,2560]{3,2,1,0:T(2,128)(2,1)S(1)}, bf16[4,2,2,2560]{3,2,1,0:T(2,128)(2,1)S(1)}, u32[]{:S(2)}, u32[]{:S(2)}) %collective-permute-start.18) | collective-permute-done | bytes 81952 | tf_op jit(solution)/shard_map/ppermute | solution.py:104
  109.2 3.5 %collective-permute-start.22 = (bf16[4,2,2,2560]{3,2,1,0:T(2,128)(2,1)S(1)}, bf16[4,2,2,2560]{3,2,1,0:T(2,128)(2,1)S(1)}, u32[]{:S(2)}, u32[]{:S(2)}) collective-permute-start(bf16[4,2,2,2560]{3,2,1,0:T(2,128)(2,1)S(1)} %get-tuple-element.23), channel_id=1, source_target_pairs={{0,48},{8,56},{16,0},{24,8},{32,16},{40,24},{48,32},{56,40},{1,49}... | collective-permute-start | bytes 245768 | tf_op jit(solution)/shard_map/ppermute | solution.py:104
  113.0 1.2 collective-permute-done.22
  114.9 2.7 %collective-permute-start.26 = (bf16[8,2,2,2560]{3,2,1,0:T(2,128)(2,1)S(1)}, bf16[8,2,2,2560]{3,2,1,0:T(2,128)(2,1)S(1)}, u32[]{:S(2)}, u32[]{:S(2)}) collective-permute-start(bf16[8,2,2,2560]{3,2,1,0:T(2,128)(2,1)S(1)} %get-tuple-element.15), channel_id=1, source_target_pairs={{0,192},{64,0},{128,64},{192,128},{1,193},{65,1},{129,65},{193,129... | collective-permute-start | bytes 491528 | tf_op jit(solution)/shard_map/ppermute | solution.py:108
  117.6 2.7 %collective-permute-done.24 = bf16[8,2,2,2560]{3,2,1,0:T(2,128)(2,1)S(1)} collective-permute-done((bf16[8,2,2,2560]{3,2,1,0:T(2,128)(2,1)S(1)}, bf16[8,2,2,2560]{3,2,1,0:T(2,128)(2,1)S(1)}, u32[]{:S(2)}, u32[]{:S(2)}) %collective-permute-start.24) | collective-permute-done | bytes 163872 | tf_op jit(solution)/shard_map/ppermute | solution.py:108
  120.3 1.3 collective-permute-done.26
  121.6 2.5 %collective-permute-done.25 = bf16[8,2,2,2560]{3,2,1,0:T(2,128)(2,1)S(1)} collective-permute-done((bf16[8,2,2,2560]{3,2,1,0:T(2,128)(2,1)S(1)}, bf16[8,2,2,2560]{3,2,1,0:T(2,128)(2,1)S(1)}, u32[]{:S(2)}, u32[]{:S(2)}) %collective-permute-start.25) | collective-permute-done | bytes 163872 | tf_op jit(solution)/shard_map/ppermute | solution.py:108
  124.1 1.2 pad_maximum_fusion
  125.7 3.7 %collective-permute-start.27 = (bf16[4,8,2,2560]{3,2,1,0:T(2,128)(2,1)S(1)}, bf16[4,8,2,2560]{3,2,1,0:T(2,128)(2,1)S(1)}, u32[]{:S(2)}, u32[]{:S(2)}) collective-permute-start(bf16[4,8,2,2560]{3,2,1,0:T(2,128)(2,1)S(1)} %get-tuple-element.12), channel_id=1, source_target_pairs={{0,4},{4,0},{1,5},{5,1},{2,6},{6,2},{3,7},{7,3},{8,12},{12,8},{9,1... | collective-permute-start | bytes 983048 | tf_op jit(solution)/shard_map/ppermute | solution.py:112
  129.4 1.3 collective-permute-done.27
  130.7 0.9 pad_maximum_fusion.1
  133.0 1.4 %bitcast_convert_fusion = bf16[64,2,128,4,8]{2,4,3,1,0:T(8,128)(2,1)} fusion(bf16[64,2,8,32]{2,3,1,0:T(8,128)(2,1)S(1)} %bitcast.190, bf16[64,8,320]{2,1,0:T(8,128)(2,1)S(1)} %reshape.107), kind=kOutput, calls=%fused_computation.12 | convolution fusion | flops 8912896 | bytes 2359296
  (75 shorter events, 9.9 us)
Async XLA Ops:
  0.0 67.1 %copy-start = (bf16[1,128,2048]{2,1,0:T(8,128)(2,1)S(1)}, bf16[1,128,2048]{2,1,0:T(8,128)(2,1)}, u32[]{:S(2)}) copy-start(bf16[1,128,2048]{2,1,0:T(8,128)(2,1)} %param.8) | copy-start | bytes 1572868
  2.5 7.0 %collective-permute-start.2 = (f32[32768]{0:T(1024)S(1)}, f32[32768]{0:T(1024)S(1)}, u32[]{:S(2)}, u32[]{:S(2)}) collective-permute-start(f32[32768]{0:T(1024)S(1)} %fusion), channel_id=1, source_target_pairs={{0,3},{1,0},{2,1},{3,2},{4,7},{5,4},{6,5},{7,6},{8,11},{9,8},{10,9... | collective-permute-start | bytes 393224 | tf_op jit(solution)/shard_map/ppermute | solution.py:141
  5.9 5.4 %collective-permute-start.1 = (f32[32768]{0:T(1024)S(1)}, f32[32768]{0:T(1024)S(1)}, u32[]{:S(2)}, u32[]{:S(2)}) collective-permute-start(f32[32768]{0:T(1024)S(1)} %fusion), channel_id=1, source_target_pairs={{0,2},{1,3},{2,0},{3,1},{4,6},{5,7},{6,4},{7,5},{8,10},{9,11},{10,... | collective-permute-start | bytes 393224 | tf_op jit(solution)/shard_map/ppermute | solution.py:141
  6.4 9.0 %collective-permute-start = (f32[32768]{0:T(1024)S(1)}, f32[32768]{0:T(1024)S(1)}, u32[]{:S(2)}, u32[]{:S(2)}) collective-permute-start(f32[32768]{0:T(1024)S(1)} %fusion), channel_id=1, source_target_pairs={{0,1},{1,2},{2,3},{3,0},{4,5},{5,6},{6,7},{7,4},{8,9},{9,10},{10,1... | collective-permute-start | bytes 393224 | tf_op jit(solution)/shard_map/ppermute | solution.py:141
  20.9 2.8 %collective-permute-start.5 = (bf16[2,64,128]{2,1,0:T(8,128)(2,1)S(1)}, bf16[2,64,128]{2,1,0:T(8,128)(2,1)S(1)}, u32[]{:S(2)}, u32[]{:S(2)}) collective-permute-start(bf16[2,64,128]{2,1,0:T(8,128)(2,1)S(1)} %get-tuple-element.38), channel_id=1, source_target_pairs={{0,3},{1,0},{2,1},{3,2},{4,7},{5,4},{6,5},{7,6},{8,11},{9,8},{10,9... | collective-permute-start | bytes 98312 | tf_op jit(solution)/shard_map/ppermute | solution.py:156
  21.0 4.4 %collective-permute-start.4 = (bf16[2,64,128]{2,1,0:T(8,128)(2,1)S(1)}, bf16[2,64,128]{2,1,0:T(8,128)(2,1)S(1)}, u32[]{:S(2)}, u32[]{:S(2)}) collective-permute-start(bf16[2,64,128]{2,1,0:T(8,128)(2,1)S(1)} %get-tuple-element.39), channel_id=1, source_target_pairs={{0,2},{1,3},{2,0},{3,1},{4,6},{5,7},{6,4},{7,5},{8,10},{9,11},{10,... | collective-permute-start | bytes 98312 | tf_op jit(solution)/shard_map/ppermute | solution.py:156
  21.2 4.9 %collective-permute-start.3 = (bf16[2,64,128]{2,1,0:T(8,128)(2,1)S(1)}, bf16[2,64,128]{2,1,0:T(8,128)(2,1)S(1)}, u32[]{:S(2)}, u32[]{:S(2)}) collective-permute-start(bf16[2,64,128]{2,1,0:T(8,128)(2,1)S(1)} %get-tuple-element.40), channel_id=1, source_target_pairs={{0,1},{1,2},{2,3},{3,0},{4,5},{5,6},{6,7},{7,4},{8,9},{9,10},{10,1... | collective-permute-start | bytes 98312 | tf_op jit(solution)/shard_map/ppermute | solution.py:156
  27.3 12.6 %collective-permute-start.6 = (bf16[4,2,2,1024]{3,2,1,0:T(2,128)(2,1)S(1)}, bf16[4,2,2,1024]{3,2,1,0:T(2,128)(2,1)S(1)}, u32[]{:S(2)}, u32[]{:S(2)}) collective-permute-start(bf16[4,2,2,1024]{3,2,1,0:T(2,128)(2,1)S(1)} %get-tuple-element.36), channel_id=1, source_target_pairs={{0,8},{8,16},{16,24},{24,32},{32,40},{40,48},{48,56},{56,0},{1,9},... | collective-permute-start | bytes 98312 | tf_op jit(solution)/shard_map/ppermute | solution.py:104
  29.1 22.0 %collective-permute-start.12 = (bf16[4,2,2,1024]{3,2,1,0:T(2,128)(2,1)S(1)}, bf16[4,2,2,1024]{3,2,1,0:T(2,128)(2,1)S(1)}, u32[]{:S(2)}, u32[]{:S(2)}) collective-permute-start(bf16[4,2,2,1024]{3,2,1,0:T(2,128)(2,1)S(1)} %get-tuple-element.30), channel_id=1, source_target_pairs={{0,56},{8,0},{16,8},{24,16},{32,24},{40,32},{48,40},{56,48},{1,57}... | collective-permute-start | bytes 98312 | tf_op jit(solution)/shard_map/ppermute | solution.py:104
  33.1 17.9 %collective-permute-start.11 = (bf16[4,2,2,1024]{3,2,1,0:T(2,128)(2,1)S(1)}, bf16[4,2,2,1024]{3,2,1,0:T(2,128)(2,1)S(1)}, u32[]{:S(2)}, u32[]{:S(2)}) collective-permute-start(bf16[4,2,2,1024]{3,2,1,0:T(2,128)(2,1)S(1)} %get-tuple-element.31), channel_id=1, source_target_pairs={{0,48},{8,56},{16,0},{24,8},{32,16},{40,24},{48,32},{56,40},{1,49}... | collective-permute-start | bytes 98312 | tf_op jit(solution)/shard_map/ppermute | solution.py:104
  35.0 15.9 %collective-permute-start.10 = (bf16[4,2,2,1024]{3,2,1,0:T(2,128)(2,1)S(1)}, bf16[4,2,2,1024]{3,2,1,0:T(2,128)(2,1)S(1)}, u32[]{:S(2)}, u32[]{:S(2)}) collective-permute-start(bf16[4,2,2,1024]{3,2,1,0:T(2,128)(2,1)S(1)} %get-tuple-element.32), channel_id=1, source_target_pairs={{0,40},{8,48},{16,56},{24,0},{32,8},{40,16},{48,24},{56,32},{1,41}... | collective-permute-start | bytes 98312 | tf_op jit(solution)/shard_map/ppermute | solution.py:104
  37.2 13.7 %collective-permute-start.9 = (bf16[4,2,2,1024]{3,2,1,0:T(2,128)(2,1)S(1)}, bf16[4,2,2,1024]{3,2,1,0:T(2,128)(2,1)S(1)}, u32[]{:S(2)}, u32[]{:S(2)}) collective-permute-start(bf16[4,2,2,1024]{3,2,1,0:T(2,128)(2,1)S(1)} %get-tuple-element.33), channel_id=1, source_target_pairs={{0,32},{8,40},{16,48},{24,56},{32,0},{40,8},{48,16},{56,24},{1,33}... | collective-permute-start | bytes 98312 | tf_op jit(solution)/shard_map/ppermute | solution.py:104
  39.9 5.2 %collective-permute-start.7 = (bf16[4,2,2,1024]{3,2,1,0:T(2,128)(2,1)S(1)}, bf16[4,2,2,1024]{3,2,1,0:T(2,128)(2,1)S(1)}, u32[]{:S(2)}, u32[]{:S(2)}) collective-permute-start(bf16[4,2,2,1024]{3,2,1,0:T(2,128)(2,1)S(1)} %get-tuple-element.35), channel_id=1, source_target_pairs={{0,16},{8,24},{16,32},{24,40},{32,48},{40,56},{48,0},{56,8},{1,17}... | collective-permute-start | bytes 98312 | tf_op jit(solution)/shard_map/ppermute | solution.py:104
  45.1 5.8 %collective-permute-start.8 = (bf16[4,2,2,1024]{3,2,1,0:T(2,128)(2,1)S(1)}, bf16[4,2,2,1024]{3,2,1,0:T(2,128)(2,1)S(1)}, u32[]{:S(2)}, u32[]{:S(2)}) collective-permute-start(bf16[4,2,2,1024]{3,2,1,0:T(2,128)(2,1)S(1)} %get-tuple-element.34), channel_id=1, source_target_pairs={{0,24},{8,32},{16,40},{24,48},{32,56},{40,0},{48,8},{56,16},{1,25}... | collective-permute-start | bytes 98312 | tf_op jit(solution)/shard_map/ppermute | solution.py:104
  51.3 4.1 %collective-permute-start.15 = (bf16[8,2,2,1024]{3,2,0,1:T(2,128)(2,1)S(1)}, bf16[8,2,2,1024]{3,2,0,1:T(2,128)(2,1)S(1)}, u32[]{:S(2)}, u32[]{:S(2)}) collective-permute-start(bf16[8,2,2,1024]{3,2,0,1:T(2,128)(2,1)S(1)} %get-tuple-element.27), channel_id=1, source_target_pairs={{0,192},{64,0},{128,64},{192,128},{1,193},{65,1},{129,65},{193,129... | collective-permute-start | bytes 196616 | tf_op jit(solution)/shard_map/ppermute | solution.py:108
  54.1 4.7 %collective-permute-start.14 = (bf16[8,2,2,1024]{3,2,0,1:T(2,128)(2,1)S(1)}, bf16[8,2,2,1024]{3,2,0,1:T(2,128)(2,1)S(1)}, u32[]{:S(2)}, u32[]{:S(2)}) collective-permute-start(bf16[8,2,2,1024]{3,2,0,1:T(2,128)(2,1)S(1)} %get-tuple-element.28), channel_id=1, source_target_pairs={{0,128},{64,192},{128,0},{192,64},{1,129},{65,193},{129,1},{193,65... | collective-permute-start | bytes 196616 | tf_op jit(solution)/shard_map/ppermute | solution.py:108
  54.4 5.0 %collective-permute-start.13 = (bf16[8,2,2,1024]{3,2,0,1:T(2,128)(2,1)S(1)}, bf16[8,2,2,1024]{3,2,0,1:T(2,128)(2,1)S(1)}, u32[]{:S(2)}, u32[]{:S(2)}) collective-permute-start(bf16[8,2,2,1024]{3,2,0,1:T(2,128)(2,1)S(1)} %get-tuple-element.29), channel_id=1, source_target_pairs={{0,64},{64,128},{128,192},{192,0},{1,65},{65,129},{129,193},{193,1... | collective-permute-start | bytes 196616 | tf_op jit(solution)/shard_map/ppermute | solution.py:108
  60.1 11.7 %collective-permute-start.16 = (bf16[4,8,2,1024]{3,2,1,0:T(2,128)(2,1)S(1)}, bf16[4,8,2,1024]{3,2,1,0:T(2,128)(2,1)S(1)}, u32[]{:S(2)}, u32[]{:S(2)}) collective-permute-start(bf16[4,8,2,1024]{3,2,1,0:T(2,128)(2,1)S(1)} %get-tuple-element.25), channel_id=1, source_target_pairs={{0,4},{4,0},{1,5},{5,1},{2,6},{6,2},{3,7},{7,3},{8,12},{12,8},{9,1... | collective-permute-start | bytes 393224 | tf_op jit(solution)/shard_map/ppermute | solution.py:112
  91.2 8.7 %collective-permute-start.17 = (bf16[4,2,2,2560]{3,2,1,0:T(2,128)(2,1)S(1)}, bf16[4,2,2,2560]{3,2,1,0:T(2,128)(2,1)S(1)}, u32[]{:S(2)}, u32[]{:S(2)}) collective-permute-start(bf16[4,2,2,2560]{3,2,1,0:T(2,128)(2,1)S(1)} %get-tuple-element.22), channel_id=1, source_target_pairs={{0,8},{8,16},{16,24},{24,32},{32,40},{40,48},{48,56},{56,0},{1,9},... | collective-permute-start | bytes 245768 | tf_op jit(solution)/shard_map/ppermute | solution.py:104
  91.4 22.9 %collective-permute-start.23 = (bf16[4,2,2,2560]{3,2,1,0:T(2,128)(2,1)S(1)}, bf16[4,2,2,2560]{3,2,1,0:T(2,128)(2,1)S(1)}, u32[]{:S(2)}, u32[]{:S(2)}) collective-permute-start(bf16[4,2,2,2560]{3,2,1,0:T(2,128)(2,1)S(1)} %get-tuple-element.17), channel_id=1, source_target_pairs={{0,56},{8,0},{16,8},{24,16},{32,24},{40,32},{48,40},{56,48},{1,57}... | collective-permute-start | bytes 245768 | tf_op jit(solution)/shard_map/ppermute | solution.py:104
  94.3 18.7 %collective-permute-start.21 = (bf16[4,2,2,2560]{3,2,1,0:T(2,128)(2,1)S(1)}, bf16[4,2,2,2560]{3,2,1,0:T(2,128)(2,1)S(1)}, u32[]{:S(2)}, u32[]{:S(2)}) collective-permute-start(bf16[4,2,2,2560]{3,2,1,0:T(2,128)(2,1)S(1)} %get-tuple-element.18), channel_id=1, source_target_pairs={{0,40},{8,48},{16,56},{24,0},{32,8},{40,16},{48,24},{56,32},{1,41}... | collective-permute-start | bytes 245768 | tf_op jit(solution)/shard_map/ppermute | solution.py:104
  95.9 17.0 %collective-permute-start.20 = (bf16[4,2,2,2560]{3,2,1,0:T(2,128)(2,1)S(1)}, bf16[4,2,2,2560]{3,2,1,0:T(2,128)(2,1)S(1)}, u32[]{:S(2)}, u32[]{:S(2)}) collective-permute-start(bf16[4,2,2,2560]{3,2,1,0:T(2,128)(2,1)S(1)} %get-tuple-element.19), channel_id=1, source_target_pairs={{0,32},{8,40},{16,48},{24,56},{32,0},{40,8},{48,16},{56,24},{1,33}... | collective-permute-start | bytes 245768 | tf_op jit(solution)/shard_map/ppermute | solution.py:104
  97.4 15.4 %collective-permute-start.19 = (bf16[4,2,2,2560]{3,2,1,0:T(2,128)(2,1)S(1)}, bf16[4,2,2,2560]{3,2,1,0:T(2,128)(2,1)S(1)}, u32[]{:S(2)}, u32[]{:S(2)}) collective-permute-start(bf16[4,2,2,2560]{3,2,1,0:T(2,128)(2,1)S(1)} %get-tuple-element.20), channel_id=1, source_target_pairs={{0,24},{8,32},{16,40},{24,48},{32,56},{40,0},{48,8},{56,16},{1,25}... | collective-permute-start | bytes 245768 | tf_op jit(solution)/shard_map/ppermute | solution.py:104
  99.9 9.3 %collective-permute-start.18 = (bf16[4,2,2,2560]{3,2,1,0:T(2,128)(2,1)S(1)}, bf16[4,2,2,2560]{3,2,1,0:T(2,128)(2,1)S(1)}, u32[]{:S(2)}, u32[]{:S(2)}) collective-permute-start(bf16[4,2,2,2560]{3,2,1,0:T(2,128)(2,1)S(1)} %get-tuple-element.21), channel_id=1, source_target_pairs={{0,16},{8,24},{16,32},{24,40},{32,48},{40,56},{48,0},{56,8},{1,17}... | collective-permute-start | bytes 245768 | tf_op jit(solution)/shard_map/ppermute | solution.py:104
  109.2 5.0 %collective-permute-start.22 = (bf16[4,2,2,2560]{3,2,1,0:T(2,128)(2,1)S(1)}, bf16[4,2,2,2560]{3,2,1,0:T(2,128)(2,1)S(1)}, u32[]{:S(2)}, u32[]{:S(2)}) collective-permute-start(bf16[4,2,2,2560]{3,2,1,0:T(2,128)(2,1)S(1)} %get-tuple-element.23), channel_id=1, source_target_pairs={{0,48},{8,56},{16,0},{24,8},{32,16},{40,24},{48,32},{56,40},{1,49}... | collective-permute-start | bytes 245768 | tf_op jit(solution)/shard_map/ppermute | solution.py:104
  114.8 5.5 %collective-permute-start.24 = (bf16[8,2,2,2560]{3,2,1,0:T(2,128)(2,1)S(1)}, bf16[8,2,2,2560]{3,2,1,0:T(2,128)(2,1)S(1)}, u32[]{:S(2)}, u32[]{:S(2)}) collective-permute-start(bf16[8,2,2,2560]{3,2,1,0:T(2,128)(2,1)S(1)} %get-tuple-element.14), channel_id=1, source_target_pairs={{0,64},{64,128},{128,192},{192,0},{1,65},{65,129},{129,193},{193,1... | collective-permute-start | bytes 491528 | tf_op jit(solution)/shard_map/ppermute | solution.py:108
  114.9 6.7 %collective-permute-start.26 = (bf16[8,2,2,2560]{3,2,1,0:T(2,128)(2,1)S(1)}, bf16[8,2,2,2560]{3,2,1,0:T(2,128)(2,1)S(1)}, u32[]{:S(2)}, u32[]{:S(2)}) collective-permute-start(bf16[8,2,2,2560]{3,2,1,0:T(2,128)(2,1)S(1)} %get-tuple-element.15), channel_id=1, source_target_pairs={{0,192},{64,0},{128,64},{192,128},{1,193},{65,1},{129,65},{193,129... | collective-permute-start | bytes 491528 | tf_op jit(solution)/shard_map/ppermute | solution.py:108
  117.6 6.5 %collective-permute-start.25 = (bf16[8,2,2,2560]{3,2,1,0:T(2,128)(2,1)S(1)}, bf16[8,2,2,2560]{3,2,1,0:T(2,128)(2,1)S(1)}, u32[]{:S(2)}, u32[]{:S(2)}) collective-permute-start(bf16[8,2,2,2560]{3,2,1,0:T(2,128)(2,1)S(1)} %get-tuple-element.16), channel_id=1, source_target_pairs={{0,128},{64,192},{128,0},{192,64},{1,129},{65,193},{129,1},{193,65... | collective-permute-start | bytes 491528 | tf_op jit(solution)/shard_map/ppermute | solution.py:108
  125.7 5.0 %collective-permute-start.27 = (bf16[4,8,2,2560]{3,2,1,0:T(2,128)(2,1)S(1)}, bf16[4,8,2,2560]{3,2,1,0:T(2,128)(2,1)S(1)}, u32[]{:S(2)}, u32[]{:S(2)}) collective-permute-start(bf16[4,8,2,2560]{3,2,1,0:T(2,128)(2,1)S(1)} %get-tuple-element.12), channel_id=1, source_target_pairs={{0,4},{4,0},{1,5},{5,1},{2,6},{6,2},{3,7},{7,3},{8,12},{12,8},{9,1... | collective-permute-start | bytes 983048 | tf_op jit(solution)/shard_map/ppermute | solution.py:112

commit v11 on v9

--- a/solution.py
+++ b/solution.py
@@ -30,7 +30,7 @@
     row_patch = lax.broadcasted_iota(jnp.int32, (sub_rows, cols), 0) // BINS
     col_patch = lax.broadcasted_iota(jnp.int32, (sub_rows, cols), 1) // (group_size * BINS)
     same = row_patch == col_patch
-    ones = jnp.ones((8, HD), jnp.float32)
+    ones = jnp.ones((8, HD), jnp.bfloat16)
     for sg in range(rows_ref.shape[0] // sub_rows):
         base = sg * sub_rows
         xs = projected[base : base + sub_rows, :]
@@ -45,10 +45,15 @@
                     pieces.append(xs[p * BINS : (p + 1) * BINS, h * HD : (h + 1) * HD])
             q = jnp.concatenate(pieces, axis=0)
             qf = q.astype(jnp.float32)
+            q2 = qf * qf
+            q2_hi = q2.astype(jnp.bfloat16)
+            q2_lo = (q2 - q2_hi.astype(jnp.float32)).astype(jnp.bfloat16)
             q_sums = lax.dot_general(
-                ones, qf * qf, (((1,), (1,)), ((), ())), precision=lax.Precision.HIGHEST,
-                preferred_element_type=jnp.float32,
-            )[0:1, :]
+                ones, q2_hi, (((1,), (1,)), ((), ())), preferred_element_type=jnp.float32
+            ) + lax.dot_general(
+                ones, q2_lo, (((1,), (1,)), ((), ())), preferred_element_type=jnp.float32
+            )
+            q_sums = q_sums[0:1, :]
             q_scale = 1.0 / jnp.sqrt(q_sums / HD + 1e-06)
             raw = lax.dot_general(
                 k, q, (((1,), (1,)), ((), ())), preferred_element_type=jnp.float32
@@ -111,8 +116,9 @@
     for shift in range(1, seq_count):
         pairs = [(i, (i + shift) % seq_count) for i in range(seq_count)]
         received.append(lax.ppermute(partial, "seq", pairs))
-    order = (seq_index - jnp.arange(seq_count, dtype=jnp.int32)) % seq_count
-    squares = jnp.sum(jnp.take(jnp.stack(received), order, axis=0), axis=0)
+    squares = received[0]
+    for piece in received[1:]:
+        squares = squares + piece
     inv_rms = 1.0 / jnp.sqrt(squares / (sample_rows * seq_count) + 1e-06)
     active = jnp.maximum(signal * inv_rms[None, :] - 0.8, 0.0)
     local_bins = bin_index - seq_index * bin_count

time: 100 us -> 93.4 us (0.934)
  Pallas kernels: 14.3 us -> 9.88 us
  waiting for transfers between devices: 16.8 us -> 15.8 us
    pallas_call x1, Pallas kernels: 14.3 us -> 9.88 us  [owner_payload(): pl.pallas_call(_owner_kernel, out_shape=jax.ShapeDtypeStruct((total, KVH...]
    reduce_sum x1, other arithmetic: 3.59 us -> 1.81 us  [body(): jnp.sum(jnp.where((local_bins == b)[:, None], active, 0.0), axis=0)]
    ppermute x3, waiting for transfers between devices: 6.74 us -> 4.99 us  [body(): received.append(lax.ppermute(partial, 'seq', pairs))]
  transfers between devices with their start and end apart: 7 -> 7, of which waited for: 7 -> 6; matrix products, arithmetic and copies ran while one was open for 7% -> 9% of each run, Pallas kernels for 0% -> 0%
where the time goes in v11:
time: 93.4 us; the launch traced here: 93.1 us
  blocking collectives  26 us (28%)
  starting transfers between devices  19.8 us (21%)
  waiting for transfers between devices  15.8 us (17%)
  Pallas kernels  9.88 us (11%)
  other arithmetic  8.32 us (9%)
  local copies, waits for them, and re-layouts  6.64 us (7%)
  matrix products  6.55 us (7%)
    all_to_all x1, blocking collectives, body(): lax.all_to_all(payload, 'wide', split_axis=0, concat_axis=0, tiled=True)  26 us
    all_to_all x1, starting transfers between devices, body(): lax.all_to_all(outgoing, 'wide', split_axis=0, concat_axis=0, tiled=True)  13.7 us
    pallas_call x1, Pallas kernels, owner_payload(): pl.pallas_call(_owner_kernel, out_shape=jax.ShapeDtypeStruct((total, KVH...  9.88 us
    all_to_all x1, waiting for transfers between devices, body(): lax.all_to_all(outgoing, 'wide', split_axis=0, concat_axis=0, tiled=True)  7.29 us
    ppermute x3, waiting for transfers between devices, body(): received.append(lax.ppermute(partial, 'seq', pairs))  4.99 us
    dot_general x1, matrix products, body(): jnp.dot(weight_block, qkv_weight, preferred_element_type=jnp.float32)  4.66 us
    ppermute x3, starting transfers between devices, body(): received.append(lax.ppermute(partial, 'seq', pairs))  4.5 us
    ppermute x3, waiting for transfers between devices, body(): received.append(lax.ppermute(piece, 'seq', pairs))  3.51 us
  transfers between devices with their start and end apart: 7, of which 6 were waited for; matrix products, arithmetic and copies ran while one was open for 9% of the time, Pallas kernels for 0%

profile of v11, /device:TPU:1, one launch (start us, length us, event | category | flops | bytes accessed | tf_op | source)
XLA Modules:
  0.0 93.1 jit_solution(734687980217048347)
XLA Ops:
  0.0 0.0 copy-start
  0.0 0.0 copy-start.1
  0.0 2.6 %fusion = f32[32768]{0:T(1024)S(1)} fusion(bf16[40,32768]{1,0:T(8,128)(2,1)} %param.5), kind=kLoop, calls=%fused_computation.3 | loop fusion | flops 3899392 | bytes 2752512 | tf_op jit(solution)/shard_map/reduce_sum | solution.py:114
  2.6 3.4 %collective-permute-start.2 = (f32[32768]{0:T(1024)S(1)}, f32[32768]{0:T(1024)S(1)}, u32[]{:S(2)}, u32[]{:S(2)}) collective-permute-start(f32[32768]{0:T(1024)S(1)} %fusion), channel_id=1, source_target_pairs={{0,3},{1,0},{2,1},{3,2},{4,7},{5,4},{6,5},{7,6},{8,11},{9,8},{10,9... | collective-permute-start | bytes 393224 | tf_op jit(solution)/shard_map/ppermute | solution.py:118
  6.0 0.5 collective-permute-start.1
  6.5 0.6 collective-permute-start
  7.1 0.8 dynamic_slice.10
  7.9 0.2 convert_reduce_fusion
  8.1 0.8 multiply_add_fusion
  8.8 0.7 subtract_compare_fusion
  9.5 0.5 fusion.17
  10.0 0.7 pad_clamp_fusion
  10.7 0.0 collective-permute-done.2
  10.7 0.7 collective-permute-done.1
  11.4 4.3 %collective-permute-done = f32[32768]{0:T(1024)} collective-permute-done((f32[32768]{0:T(1024)S(1)}, f32[32768]{0:T(1024)}, u32[]{:S(2)}, u32[]{:S(2)}) %collective-permute-start) | collective-permute-done | bytes 131104 | tf_op jit(solution)/shard_map/ppermute | solution.py:118
  15.7 1.0 %add_rsqrt_fusion = f32[32768]{0:T(1024)S(1)} fusion(f32[32768]{0:T(1024)S(1)} %collective-permute-done.2, f32[32768]{0:T(1024)S(1)} %collective-permute-done.1, f32[32768]{0:T(1024)S(1)} %fusion, f32[32768]{0:T(1024)} %collective-permute-done), kind=kLoop, calls=%fused_computation.23 | loop fusion | flops 163840 | bytes 655360 | tf_op jit(solution)/shard_map/sqrt | solution.py:122
  16.6 0.0 copy-done.1
  16.6 1.8 %fusion.5 = (f32[32768]{0:T(1024)S(1)}, f32[32768]{0:T(1024)S(1)}) fusion(bf16[40,32768]{1,0:T(8,128)(2,1)S(1)} %copy-done.1, f32[32768]{0:T(1024)S(1)} %add_rsqrt_fusion, pred[40]{0:T(512)(128)(4,1)S(1)} %get-tuple-element.14, pred[40]{0:T(512)(128)(4,1)S(1)} %get-tuple-element.13), kind=kLoop, calls=%fused_computation.8 | loop fusion | flops 10420224 | bytes 3014736 | tf_op jit(solution)/shard_map/reduce_sum | solution.py:126
  18.5 0.1 collective-permute-start.5
  18.6 0.2 collective-permute-start.4
  18.9 1.2 %collective-permute-start.3 = (bf16[2,64,128]{2,1,0:T(8,128)(2,1)S(1)}, bf16[2,64,128]{2,1,0:T(8,128)(2,1)S(1)}, u32[]{:S(2)}, u32[]{:S(2)}) collective-permute-start(bf16[2,64,128]{2,1,0:T(8,128)(2,1)S(1)} %get-tuple-element.12), channel_id=1, source_target_pairs={{0,1},{1,2},{2,3},{3,0},{4,5},{5,6},{6,7},{7,4},{8,9},{9,10},{10,1... | collective-permute-start | bytes 98312 | tf_op jit(solution)/shard_map/ppermute | solution.py:134
  20.1 0.1 broadcast_in_dim.39
  20.2 0.1 broadcast_in_dim.40
  20.3 1.1 %collective-permute-done.5 = bf16[2,64,128]{2,1,0:T(8,128)(2,1)S(1)} collective-permute-done((bf16[2,64,128]{2,1,0:T(8,128)(2,1)S(1)}, bf16[2,64,128]{2,1,0:T(8,128)(2,1)S(1)}, u32[]{:S(2)}, u32[]{:S(2)}) %collective-permute-start.5) | collective-permute-done | bytes 32800 | tf_op jit(solution)/shard_map/ppermute | solution.py:134
  21.4 1.6 %collective-permute-done.4 = bf16[2,64,128]{2,1,0:T(8,128)(2,1)S(1)} collective-permute-done((bf16[2,64,128]{2,1,0:T(8,128)(2,1)S(1)}, bf16[2,64,128]{2,1,0:T(8,128)(2,1)S(1)}, u32[]{:S(2)}, u32[]{:S(2)}) %collective-permute-start.4) | collective-permute-done | bytes 32800 | tf_op jit(solution)/shard_map/ppermute | solution.py:134
  23.0 0.8 collective-permute-done.3
  23.8 0.6 gather_fusion
  24.4 0.1 copy_select_fusion
  24.5 0.2 convolution_convert_fusion.1
  24.7 0.8 all_to_all.14
  25.5 13.7 %all-to-all-start = ((bf16[64,2,1024]{2,1,0:T(2,128)(2,1)}), bf16[64,2,1024]{2,1,0:T(2,128)(2,1)S(1)}, u32[]{:S(2)}, u32[]{:S(2)}) async-start(bf16[64,2,1024]{2,1,0:T(2,128)(2,1)} %all_to_all.14), calls=%async_computation | async-start | bytes 524288 | tf_op jit(solution)/shard_map/all_to_all | solution.py:154
  39.2 0.0 copy-done
  39.2 4.7 %subtract_convert_fusion = (bf16[128,1536]{1,0:T(8,128)(2,1)}, bf16[128,1536]{1,0:T(8,128)(2,1)}) fusion(bf16[2048,1536]{1,0:T(8,128)(2,1)} %param.9, bf16[1,128,2048]{2,1,0:T(8,128)(2,1)S(1)} %copy-done), kind=kOutput, calls=%fused_computation.13 | convolution fusion | flops 806092800 | bytes 7602176 | tf_op jit(solution)/shard_map/dot_general | solution.py:156
  43.9 7.3 %all-to-all-done = bf16[64,2,1024]{2,1,0:T(2,128)(2,1)S(1)} async-done(((bf16[64,2,1024]{2,1,0:T(2,128)(2,1)}), bf16[64,2,1024]{2,1,0:T(2,128)(2,1)S(1)}, u32[]{:S(2)}, u32[]{:S(2)}) %all-to-all-start) | async-done | bytes 262176 | tf_op jit(solution)/shard_map/all_to_all | solution.py:154
  51.2 0.9 reshape.100.rows_ref
  52.1 9.9 %shard_map.55 = bf16[1024,320]{1,0:T(8,128)(2,1)} custom-call(bf16[1024,128]{1,0:T(8,128)(2,1)} %reshape.100.rows_ref, bf16[128,1536]{1,0:T(8,128)(2,1)} %get-tuple-element.8.hi_ref, bf16[128,1536]{1,0:T(8,128)(2,1)} %get-tuple-element.7.lo_ref), custom_call_target="tpu_custom_call" | custom-call | tf_op jit(solution)/shard_map/pallas_call | solution.py:79
  61.9 2.4 %all_to_all.16 = bf16[64,2,2560]{2,1,0:T(2,128)(2,1)S(1)} reshape(bf16[1024,320]{1,0:T(8,128)(2,1)} %shard_map.55) | data formatting | bytes 1310720 | tf_op jit(solution)/shard_map/all_to_all | solution.py:161
  64.4 26.0 %all_to_all.21 = bf16[64,2,2560]{2,1,0:T(2,128)(2,1)S(1)} all-to-all(bf16[64,2,2560]{2,1,0:T(2,128)(2,1)S(1)} %all_to_all.16), channel_id=1, replica_groups=mesh['wide'=64,'seq'=4] {'wide'}, dimensions={0} | all-to-all | bytes 1310720 | tf_op jit(solution)/shard_map/all_to_all | solution.py:161
  90.3 0.2 all_to_all.18
  90.6 0.3 convolution_convert_fusion
  90.9 0.3 reshape.101
  91.2 0.5 copy.11
  91.7 1.4 %bitcast_convert_fusion = bf16[64,2,128,4,8]{2,4,3,1,0:T(8,128)(2,1)} fusion(bf16[64,2,8,32]{2,3,1,0:T(8,128)(2,1)S(1)} %bitcast.42, bf16[64,8,320]{2,1,0:T(8,128)(2,1)S(1)} %reshape.101), kind=kOutput, calls=%fused_computation.11 | convolution fusion | flops 8912896 | bytes 2359296
  (5 shorter events, 0.1 us)
Async XLA Ops:
  0.0 39.2 %copy-start = (bf16[1,128,2048]{2,1,0:T(8,128)(2,1)S(1)}, bf16[1,128,2048]{2,1,0:T(8,128)(2,1)}, u32[]{:S(2)}) copy-start(bf16[1,128,2048]{2,1,0:T(8,128)(2,1)} %param.8) | copy-start | bytes 1572868
  0.0 16.6 %copy-start.1 = (bf16[40,32768]{1,0:T(8,128)(2,1)S(1)}, bf16[40,32768]{1,0:T(8,128)(2,1)}, u32[]{:S(2)}) copy-start(bf16[40,32768]{1,0:T(8,128)(2,1)} %param.5) | copy-start | bytes 7864324
  2.6 8.1 %collective-permute-start.2 = (f32[32768]{0:T(1024)S(1)}, f32[32768]{0:T(1024)S(1)}, u32[]{:S(2)}, u32[]{:S(2)}) collective-permute-start(f32[32768]{0:T(1024)S(1)} %fusion), channel_id=1, source_target_pairs={{0,3},{1,0},{2,1},{3,2},{4,7},{5,4},{6,5},{7,6},{8,11},{9,8},{10,9... | collective-permute-start | bytes 393224 | tf_op jit(solution)/shard_map/ppermute | solution.py:118
  6.0 5.4 %collective-permute-start.1 = (f32[32768]{0:T(1024)S(1)}, f32[32768]{0:T(1024)S(1)}, u32[]{:S(2)}, u32[]{:S(2)}) collective-permute-start(f32[32768]{0:T(1024)S(1)} %fusion), channel_id=1, source_target_pairs={{0,2},{1,3},{2,0},{3,1},{4,6},{5,7},{6,4},{7,5},{8,10},{9,11},{10,... | collective-permute-start | bytes 393224 | tf_op jit(solution)/shard_map/ppermute | solution.py:118
  6.5 9.2 %collective-permute-start = (f32[32768]{0:T(1024)S(1)}, f32[32768]{0:T(1024)}, u32[]{:S(2)}, u32[]{:S(2)}) collective-permute-start(f32[32768]{0:T(1024)S(1)} %fusion), channel_id=1, source_target_pairs={{0,1},{1,2},{2,3},{3,0},{4,5},{5,6},{6,7},{7,4},{8,9},{9,10},{10,1... | collective-permute-start | bytes 393224 | tf_op jit(solution)/shard_map/ppermute | solution.py:118
  18.5 2.8 %collective-permute-start.5 = (bf16[2,64,128]{2,1,0:T(8,128)(2,1)S(1)}, bf16[2,64,128]{2,1,0:T(8,128)(2,1)S(1)}, u32[]{:S(2)}, u32[]{:S(2)}) collective-permute-start(bf16[2,64,128]{2,1,0:T(8,128)(2,1)S(1)} %get-tuple-element.10), channel_id=1, source_target_pairs={{0,3},{1,0},{2,1},{3,2},{4,7},{5,4},{6,5},{7,6},{8,11},{9,8},{10,9... | collective-permute-start | bytes 98312 | tf_op jit(solution)/shard_map/ppermute | solution.py:134
  18.6 4.4 %collective-permute-start.4 = (bf16[2,64,128]{2,1,0:T(8,128)(2,1)S(1)}, bf16[2,64,128]{2,1,0:T(8,128)(2,1)S(1)}, u32[]{:S(2)}, u32[]{:S(2)}) collective-permute-start(bf16[2,64,128]{2,1,0:T(8,128)(2,1)S(1)} %get-tuple-element.11), channel_id=1, source_target_pairs={{0,2},{1,3},{2,0},{3,1},{4,6},{5,7},{6,4},{7,5},{8,10},{9,11},{10,... | collective-permute-start | bytes 98312 | tf_op jit(solution)/shard_map/ppermute | solution.py:134
  18.9 4.9 %collective-permute-start.3 = (bf16[2,64,128]{2,1,0:T(8,128)(2,1)S(1)}, bf16[2,64,128]{2,1,0:T(8,128)(2,1)S(1)}, u32[]{:S(2)}, u32[]{:S(2)}) collective-permute-start(bf16[2,64,128]{2,1,0:T(8,128)(2,1)S(1)} %get-tuple-element.12), channel_id=1, source_target_pairs={{0,1},{1,2},{2,3},{3,0},{4,5},{5,6},{6,7},{7,4},{8,9},{9,10},{10,1... | collective-permute-start | bytes 98312 | tf_op jit(solution)/shard_map/ppermute | solution.py:134
  25.5 25.7 %all-to-all-start = ((bf16[64,2,1024]{2,1,0:T(2,128)(2,1)}), bf16[64,2,1024]{2,1,0:T(2,128)(2,1)S(1)}, u32[]{:S(2)}, u32[]{:S(2)}) async-start(bf16[64,2,1024]{2,1,0:T(2,128)(2,1)} %all_to_all.14), calls=%async_computation | async-start | bytes 524288 | tf_op jit(solution)/shard_map/all_to_all | solution.py:154

commit v12 on v11

--- a/solution.py
+++ b/solution.py
@@ -135,7 +135,7 @@
     order = (seq_index - jnp.arange(seq_count, dtype=jnp.int32)) % seq_count
     binned = jnp.take(jnp.stack(received), order, axis=0)
     block_rows = binned.reshape(all_bins, quarter, CH).transpose(1, 0, 2).reshape(
-        quarter, all_bins * CH
+        quarter * all_bins, CH
     )
 
     block = wide_index * seq_count + seq_index
@@ -145,20 +145,30 @@
     rank = jnp.sum((same & earlier).astype(jnp.int32), axis=1)
     slot = owners * CAP + rank
     slot_count = wide_count * CAP
-    dispatch = (jnp.arange(slot_count, dtype=jnp.int32)[:, None] == slot[None, :]).astype(
-        jnp.bfloat16
-    )
+    row_ids = jnp.arange(slot_count * all_bins, dtype=jnp.int32)
+    col_ids = jnp.arange(quarter * all_bins, dtype=jnp.int32)
+    col_slot = jnp.repeat(slot, all_bins)
+    dispatch = (
+        (row_ids[:, None] // all_bins == col_slot[None, :])
+        & (row_ids[:, None] % all_bins == col_ids[None, :] % all_bins)
+    ).astype(jnp.bfloat16)
     outgoing = jnp.dot(dispatch, block_rows, preferred_element_type=jnp.float32).astype(
         jnp.bfloat16
     )
-    arrived = lax.all_to_all(outgoing, "wide", split_axis=0, concat_axis=0, tiled=True)
+    chunk = CAP * all_bins
+    arrived = lax.all_to_all(
+        outgoing.reshape(wide_count, chunk, CH), "wide", split_axis=0, concat_axis=0, tiled=True
+    )
     weight_block = readin_weight[0]
     merged = jnp.dot(weight_block, qkv_weight, preferred_element_type=jnp.float32)
     merged_hi = merged.astype(jnp.bfloat16)
     merged_lo = (merged - merged_hi.astype(jnp.float32)).astype(jnp.bfloat16)
     rows = arrived.reshape(slot_count * all_bins, CH)
-    payload = owner_payload(rows, merged_hi, merged_lo).reshape(slot_count, -1)
-    returned = lax.all_to_all(payload, "wide", split_axis=0, concat_axis=0, tiled=True)
+    payload = owner_payload(rows, merged_hi, merged_lo)
+    returned = lax.all_to_all(
+        payload.reshape(wide_count, chunk, -1), "wide", split_axis=0, concat_axis=0, tiled=True
+    )
+    returned = returned.reshape(slot_count * all_bins, -1)
     mine = jnp.dot(dispatch.T, returned, preferred_element_type=jnp.float32).astype(jnp.bfloat16)
     return heads_from(mine.reshape(quarter, all_bins, -1))
 

time: 93.4 us -> 96.1 us (1.029)
  local copies, waits for them, and re-layouts: 6.64 us -> 3.08 us
  blocking collectives: 26 us -> 29 us
  matrix products: 6.55 us -> 9.26 us
    all_to_all x3 -> x0, local copies, waits for them, and re-layouts: 3.48 us -> none  [the longest x2 2.67 us: body(): lax.all_to_all(payload, 'wide', split_axis=0, concat_axis=0, tiled=True)]
    all_to_all x1, blocking collectives: 26 us -> 29 us  [body(): lax.all_to_all(payload.reshape(wide_count, chunk, -1), 'wide', split_axis...]
    dot_general x1, matrix products: 0.21 us -> 2.28 us  [body(): jnp.dot(dispatch, block_rows, preferred_element_type=jnp.float32)]
    reshape x2 -> x0, local copies, waits for them, and re-layouts: 1.16 us -> none  [the longest x1 0.87 us: body(): rows = arrived.reshape(slot_count * all_bins, CH)]
where the time goes in v12:
time: 96.1 us; the launch traced here: 95.6 us
  blocking collectives  29 us (30%)
  starting transfers between devices  19.8 us (21%)
  waiting for transfers between devices  15.7 us (16%)
  Pallas kernels  9.88 us (10%)
  matrix products  9.26 us (10%)
  other arithmetic  8.86 us (9%)
  local copies, waits for them, and re-layouts  3.08 us (3%)
    all_to_all x1, blocking collectives, body(): lax.all_to_all(payload.reshape(wide_count, chunk, -1), 'wide', split_axis...  29 us
    all_to_all x1, starting transfers between devices, body(): lax.all_to_all(outgoing.reshape(wide_count, chunk, CH), 'wide', split_axi...  13.7 us
    pallas_call x1, Pallas kernels, owner_payload(): pl.pallas_call(_owner_kernel, out_shape=jax.ShapeDtypeStruct((total, KVH...  9.88 us
    all_to_all x1, waiting for transfers between devices, body(): lax.all_to_all(outgoing.reshape(wide_count, chunk, CH), 'wide', split_axi...  7.27 us
    ppermute x3, waiting for transfers between devices, body(): received.append(lax.ppermute(partial, 'seq', pairs))  5.05 us
    dot_general x1, matrix products, body(): jnp.dot(weight_block, qkv_weight, preferred_element_type=jnp.float32)  4.68 us
    ppermute x3, starting transfers between devices, body(): received.append(lax.ppermute(partial, 'seq', pairs))  4.5 us
    ppermute x3, waiting for transfers between devices, body(): received.append(lax.ppermute(piece, 'seq', pairs))  3.34 us
  transfers between devices with their start and end apart: 7, of which 6 were waited for; matrix products, arithmetic and copies ran while one was open for 9% of the time, Pallas kernels for 0%

profile of v12, /device:TPU:1, one launch (start us, length us, event | category | flops | bytes accessed | tf_op | source)
XLA Modules:
  0.0 95.6 jit_solution(8601796096215766132)
XLA Ops:
  0.0 0.0 copy-start
  0.0 0.0 copy-start.1
  0.0 2.6 %fusion = f32[32768]{0:T(1024)S(1)} fusion(bf16[40,32768]{1,0:T(8,128)(2,1)} %param.5), kind=kLoop, calls=%fused_computation.3 | loop fusion | flops 3899392 | bytes 2752512 | tf_op jit(solution)/shard_map/reduce_sum | solution.py:114
  2.6 3.4 %collective-permute-start.2 = (f32[32768]{0:T(1024)S(1)}, f32[32768]{0:T(1024)S(1)}, u32[]{:S(2)}, u32[]{:S(2)}) collective-permute-start(f32[32768]{0:T(1024)S(1)} %fusion), channel_id=1, source_target_pairs={{0,3},{1,0},{2,1},{3,2},{4,7},{5,4},{6,5},{7,6},{8,11},{9,8},{10,9... | collective-permute-start | bytes 393224 | tf_op jit(solution)/shard_map/ppermute | solution.py:118
  6.0 0.5 collective-permute-start.1
  6.5 0.6 collective-permute-start
  7.1 0.8 dynamic_slice.10
  7.9 0.2 convert_reduce_fusion
  8.1 0.8 multiply_add_fusion
  8.9 1.2 %subtract_compare_fusion = (pred[40]{0:T(512)(128)(4,1)}, pred[40]{0:T(512)(128)(4,1)}) fusion(s32[40]{0:T(128)} %param.6, s32[]{:T(128)S(6)} %mul.37), kind=kLoop, calls=%fused_computation.73 | loop fusion | flops 120 | bytes 244 | tf_op jit(solution)/shard_map/eq | solution.py:126
  10.0 0.6 add_select_fusion.1
  10.6 0.0 collective-permute-done.2
  10.6 0.8 collective-permute-done.1
  11.4 4.3 %collective-permute-done = f32[32768]{0:T(1024)} collective-permute-done((f32[32768]{0:T(1024)S(1)}, f32[32768]{0:T(1024)}, u32[]{:S(2)}, u32[]{:S(2)}) %collective-permute-start) | collective-permute-done | bytes 131104 | tf_op jit(solution)/shard_map/ppermute | solution.py:118
  15.7 1.0 %add_rsqrt_fusion = f32[32768]{0:T(1024)S(1)} fusion(f32[32768]{0:T(1024)S(1)} %collective-permute-done.2, f32[32768]{0:T(1024)S(1)} %collective-permute-done.1, f32[32768]{0:T(1024)S(1)} %fusion, f32[32768]{0:T(1024)} %collective-permute-done), kind=kLoop, calls=%fused_computation.33 | loop fusion | flops 163840 | bytes 655360 | tf_op jit(solution)/shard_map/sqrt | solution.py:122
  16.6 0.0 copy-done.1
  16.6 2.5 %fusion.5 = (f32[32768]{0:T(1024)S(1)}, f32[32768]{0:T(1024)S(1)}) fusion(bf16[40,32768]{1,0:T(8,128)(2,1)S(1)} %copy-done.1, f32[32768]{0:T(1024)S(1)} %add_rsqrt_fusion, pred[40]{0:T(512)(128)(4,1)} %get-tuple-element.14, pred[40]{0:T(512)(128)(4,1)} %get-tuple-element.13), kind=kLoop, calls=%fused_computation.8 | loop fusion | flops 10420224 | bytes 3014736 | tf_op jit(solution)/shard_map/reduce_sum | solution.py:126
  19.2 0.1 collective-permute-start.5
  19.3 0.2 collective-permute-start.4
  19.6 1.2 %collective-permute-start.3 = (bf16[2,64,128]{2,1,0:T(8,128)(2,1)S(1)}, bf16[2,64,128]{2,1,0:T(8,128)(2,1)S(1)}, u32[]{:S(2)}, u32[]{:S(2)}) collective-permute-start(bf16[2,64,128]{2,1,0:T(8,128)(2,1)S(1)} %get-tuple-element.12), channel_id=1, source_target_pairs={{0,1},{1,2},{2,3},{3,0},{4,5},{5,6},{6,7},{7,4},{8,9},{9,10},{10,1... | collective-permute-start | bytes 98312 | tf_op jit(solution)/shard_map/ppermute | solution.py:134
  20.8 0.1 broadcast_in_dim.44
  20.9 0.1 broadcast_in_dim.45
  20.9 0.1 broadcast_in_dim.43
  21.0 0.1 eq.67
  21.1 0.9 collective-permute-done.5
  22.1 1.6 %collective-permute-done.4 = bf16[2,64,128]{2,1,0:T(8,128)(2,1)S(1)} collective-permute-done((bf16[2,64,128]{2,1,0:T(8,128)(2,1)S(1)}, bf16[2,64,128]{2,1,0:T(8,128)(2,1)S(1)}, u32[]{:S(2)}, u32[]{:S(2)}) %collective-permute-start.4) | collective-permute-done | bytes 32800 | tf_op jit(solution)/shard_map/ppermute | solution.py:134
  23.7 0.8 collective-permute-done.3
  24.5 0.6 gather_fusion
  25.1 2.3 %fusion.10 = bf16[1024,128]{1,0:T(8,128)(2,1)} fusion(s32[512]{0:T(512)} %add_select_fusion.1, s32[512]{0:T(512)S(1)} %eq.67, s32[1024]{0:T(1024)S(1)} %get-tuple-element.15, s32[1024]{0:T(1024)S(1)} %get-tuple-element.16, bf16[8,64,128]{2,1,0:T(8,128)(2,1)S(1)} %bitcast.55, pred[8]{0:T(512)(128)(4,1)S(1)} %broadcast_in_dim.45), kind=kOutput, calls=%fused_computation.15 | convolution fusion | flops 135987200 | bytes 405512 | tf_op jit(solution)/shard_map/dot_general | solution.py:155
  27.3 13.7 %all-to-all-start = ((bf16[64,16,128]{2,1,0:T(8,128)(2,1)}), bf16[64,16,128]{2,1,0:T(8,128)(2,1)S(1)}, u32[]{:S(2)}, u32[]{:S(2)}) async-start(bf16[64,16,128]{2,1,0:T(8,128)(2,1)} %bitcast.13), calls=%async_computation | async-start | bytes 524288 | tf_op jit(solution)/shard_map/all_to_all | solution.py:159
  41.1 0.0 copy-done
  41.1 0.0 copy-start.3
  41.1 4.7 %subtract_convert_fusion = (bf16[128,1536]{1,0:T(8,128)(2,1)}, bf16[128,1536]{1,0:T(8,128)(2,1)}) fusion(bf16[2048,1536]{1,0:T(8,128)(2,1)} %param.9, bf16[1,128,2048]{2,1,0:T(8,128)(2,1)S(1)} %copy-done), kind=kOutput, calls=%fused_computation.24 | convolution fusion | flops 806092800 | bytes 7602176 | tf_op jit(solution)/shard_map/dot_general | solution.py:163
  45.8 7.3 %all-to-all-done = bf16[64,16,128]{2,1,0:T(8,128)(2,1)S(1)} async-done(((bf16[64,16,128]{2,1,0:T(8,128)(2,1)}), bf16[64,16,128]{2,1,0:T(8,128)(2,1)S(1)}, u32[]{:S(2)}, u32[]{:S(2)}) %all-to-all-start) | async-done | bytes 262176 | tf_op jit(solution)/shard_map/all_to_all | solution.py:159
  53.1 0.0 copy-start.2
  53.1 0.7 copy-done.2
  53.8 9.9 %shard_map.55 = bf16[1024,320]{1,0:T(8,128)(2,1)} custom-call(bf16[1024,128]{1,0:T(8,128)(2,1)} %bitcast.51, bf16[128,1536]{1,0:T(8,128)(2,1)} %get-tuple-element.8.hi_ref, bf16[128,1536]{1,0:T(8,128)(2,1)} %get-tuple-element.7.lo_ref), custom_call_target="tpu_custom_call" | custom-call | tf_op jit(solution)/shard_map/pallas_call | solution.py:79
  63.6 29.0 %all_to_all.10 = bf16[64,16,320]{2,1,0:T(8,128)(2,1)S(1)} all-to-all(bf16[64,16,320]{2,1,0:T(8,128)(2,1)} %bitcast.48), channel_id=1, replica_groups=mesh['wide'=64,'seq'=4] {'wide'}, dimensions={0} | all-to-all | bytes 1310720 | tf_op jit(solution)/shard_map/all_to_all | solution.py:168
  92.6 0.0 copy-done.3
  92.6 0.9 fusion.9
  93.5 0.2 copy.13
  93.8 0.5 copy.14
  94.2 1.4 %bitcast_convert_fusion = bf16[64,2,128,4,8]{2,4,3,1,0:T(8,128)(2,1)} fusion(bf16[64,2,8,32]{2,3,1,0:T(8,128)(2,1)S(1)} %bitcast.47, bf16[64,8,320]{2,1,0:T(8,128)(2,1)S(1)} %bitcast.50), kind=kOutput, calls=%fused_computation.10 | convolution fusion | flops 8912896 | bytes 2359296
  (8 shorter events, 0.1 us)
Async XLA Ops:
  0.0 41.1 %copy-start = (bf16[1,128,2048]{2,1,0:T(8,128)(2,1)S(1)}, bf16[1,128,2048]{2,1,0:T(8,128)(2,1)}, u32[]{:S(2)}) copy-start(bf16[1,128,2048]{2,1,0:T(8,128)(2,1)} %param.8) | copy-start | bytes 1572868
  0.0 16.6 %copy-start.1 = (bf16[40,32768]{1,0:T(8,128)(2,1)S(1)}, bf16[40,32768]{1,0:T(8,128)(2,1)}, u32[]{:S(2)}) copy-start(bf16[40,32768]{1,0:T(8,128)(2,1)} %param.5) | copy-start | bytes 7864324
  2.6 8.0 %collective-permute-start.2 = (f32[32768]{0:T(1024)S(1)}, f32[32768]{0:T(1024)S(1)}, u32[]{:S(2)}, u32[]{:S(2)}) collective-permute-start(f32[32768]{0:T(1024)S(1)} %fusion), channel_id=1, source_target_pairs={{0,3},{1,0},{2,1},{3,2},{4,7},{5,4},{6,5},{7,6},{8,11},{9,8},{10,9... | collective-permute-start | bytes 393224 | tf_op jit(solution)/shard_map/ppermute | solution.py:118
  6.0 5.4 %collective-permute-start.1 = (f32[32768]{0:T(1024)S(1)}, f32[32768]{0:T(1024)S(1)}, u32[]{:S(2)}, u32[]{:S(2)}) collective-permute-start(f32[32768]{0:T(1024)S(1)} %fusion), channel_id=1, source_target_pairs={{0,2},{1,3},{2,0},{3,1},{4,6},{5,7},{6,4},{7,5},{8,10},{9,11},{10,... | collective-permute-start | bytes 393224 | tf_op jit(solution)/shard_map/ppermute | solution.py:118
  6.5 9.2 %collective-permute-start = (f32[32768]{0:T(1024)S(1)}, f32[32768]{0:T(1024)}, u32[]{:S(2)}, u32[]{:S(2)}) collective-permute-start(f32[32768]{0:T(1024)S(1)} %fusion), channel_id=1, source_target_pairs={{0,1},{1,2},{2,3},{3,0},{4,5},{5,6},{6,7},{7,4},{8,9},{9,10},{10,1... | collective-permute-start | bytes 393224 | tf_op jit(solution)/shard_map/ppermute | solution.py:118
  19.2 2.8 %collective-permute-start.5 = (bf16[2,64,128]{2,1,0:T(8,128)(2,1)S(1)}, bf16[2,64,128]{2,1,0:T(8,128)(2,1)S(1)}, u32[]{:S(2)}, u32[]{:S(2)}) collective-permute-start(bf16[2,64,128]{2,1,0:T(8,128)(2,1)S(1)} %get-tuple-element.10), channel_id=1, source_target_pairs={{0,3},{1,0},{2,1},{3,2},{4,7},{5,4},{6,5},{7,6},{8,11},{9,8},{10,9... | collective-permute-start | bytes 98312 | tf_op jit(solution)/shard_map/ppermute | solution.py:134
  19.3 4.4 %collective-permute-start.4 = (bf16[2,64,128]{2,1,0:T(8,128)(2,1)S(1)}, bf16[2,64,128]{2,1,0:T(8,128)(2,1)S(1)}, u32[]{:S(2)}, u32[]{:S(2)}) collective-permute-start(bf16[2,64,128]{2,1,0:T(8,128)(2,1)S(1)} %get-tuple-element.11), channel_id=1, source_target_pairs={{0,2},{1,3},{2,0},{3,1},{4,6},{5,7},{6,4},{7,5},{8,10},{9,11},{10,... | collective-permute-start | bytes 98312 | tf_op jit(solution)/shard_map/ppermute | solution.py:134
  19.6 4.9 %collective-permute-start.3 = (bf16[2,64,128]{2,1,0:T(8,128)(2,1)S(1)}, bf16[2,64,128]{2,1,0:T(8,128)(2,1)S(1)}, u32[]{:S(2)}, u32[]{:S(2)}) collective-permute-start(bf16[2,64,128]{2,1,0:T(8,128)(2,1)S(1)} %get-tuple-element.12), channel_id=1, source_target_pairs={{0,1},{1,2},{2,3},{3,0},{4,5},{5,6},{6,7},{7,4},{8,9},{9,10},{10,1... | collective-permute-start | bytes 98312 | tf_op jit(solution)/shard_map/ppermute | solution.py:134
  27.3 25.7 %all-to-all-start = ((bf16[64,16,128]{2,1,0:T(8,128)(2,1)}), bf16[64,16,128]{2,1,0:T(8,128)(2,1)S(1)}, u32[]{:S(2)}, u32[]{:S(2)}) async-start(bf16[64,16,128]{2,1,0:T(8,128)(2,1)} %bitcast.13), calls=%async_computation | async-start | bytes 524288 | tf_op jit(solution)/shard_map/all_to_all | solution.py:159
  41.1 51.5 %copy-start.3 = (s32[512]{0:T(512)S(1)}, s32[512]{0:T(512)}, u32[]{:S(2)}) copy-start(s32[512]{0:T(512)} %add_select_fusion.1) | copy-start | bytes 6148
  53.1 0.7 copy-start.2

commit v13 on v11

--- a/solution.py
+++ b/solution.py
@@ -12,7 +12,7 @@
 SPB = 20
 CAP = 2
 BINS = 8
-ROWS = 128
+ROWS = 256
 SUB = 4
 
 

time: 93.4 us -> 91.7 us (0.982)
  Pallas kernels: 9.88 us -> 8.21 us
    pallas_call x1, Pallas kernels: 9.88 us -> 8.21 us  [owner_payload(): pl.pallas_call(_owner_kernel, out_shape=jax.ShapeDtypeStruct((total, KVH...]
where the time goes in v13:
time: 91.7 us; the launch traced here: 91.4 us
  blocking collectives  25.9 us (28%)
  starting transfers between devices  19.8 us (22%)
  waiting for transfers between devices  15.8 us (17%)
  other arithmetic  8.32 us (9%)
  Pallas kernels  8.21 us (9%)
  local copies, waits for them, and re-layouts  6.64 us (7%)
  matrix products  6.55 us (7%)
    all_to_all x1, blocking collectives, body(): lax.all_to_all(payload, 'wide', split_axis=0, concat_axis=0, tiled=True)  25.9 us
    all_to_all x1, starting transfers between devices, body(): lax.all_to_all(outgoing, 'wide', split_axis=0, concat_axis=0, tiled=True)  13.7 us
    pallas_call x1, Pallas kernels, owner_payload(): pl.pallas_call(_owner_kernel, out_shape=jax.ShapeDtypeStruct((total, KVH...  8.21 us
    all_to_all x1, waiting for transfers between devices, body(): lax.all_to_all(outgoing, 'wide', split_axis=0, concat_axis=0, tiled=True)  7.29 us
    ppermute x3, waiting for transfers between devices, body(): received.append(lax.ppermute(partial, 'seq', pairs))  4.99 us
    dot_general x1, matrix products, body(): jnp.dot(weight_block, qkv_weight, preferred_element_type=jnp.float32)  4.66 us
    ppermute x3, starting transfers between devices, body(): received.append(lax.ppermute(partial, 'seq', pairs))  4.5 us
    ppermute x3, waiting for transfers between devices, body(): received.append(lax.ppermute(piece, 'seq', pairs))  3.51 us
  transfers between devices with their start and end apart: 7, of which 6 were waited for; matrix products, arithmetic and copies ran while one was open for 9% of the time, Pallas kernels for 0%

profile of v13, /device:TPU:1, one launch (start us, length us, event | category | flops | bytes accessed | tf_op | source)
XLA Modules:
  0.0 91.4 jit_solution(18440726640425641968)
XLA Ops:
  0.0 0.0 copy-start
  0.0 0.0 copy-start.1
  0.0 2.6 %fusion = f32[32768]{0:T(1024)S(1)} fusion(bf16[40,32768]{1,0:T(8,128)(2,1)} %param.5), kind=kLoop, calls=%fused_computation.3 | loop fusion | flops 3899392 | bytes 2752512 | tf_op jit(solution)/shard_map/reduce_sum | solution.py:114
  2.6 3.4 %collective-permute-start.2 = (f32[32768]{0:T(1024)S(1)}, f32[32768]{0:T(1024)S(1)}, u32[]{:S(2)}, u32[]{:S(2)}) collective-permute-start(f32[32768]{0:T(1024)S(1)} %fusion), channel_id=1, source_target_pairs={{0,3},{1,0},{2,1},{3,2},{4,7},{5,4},{6,5},{7,6},{8,11},{9,8},{10,9... | collective-permute-start | bytes 393224 | tf_op jit(solution)/shard_map/ppermute | solution.py:118
  6.0 0.5 collective-permute-start.1
  6.5 0.6 collective-permute-start
  7.1 0.8 dynamic_slice.10
  7.9 0.2 convert_reduce_fusion
  8.1 0.8 multiply_add_fusion
  8.8 0.7 subtract_compare_fusion
  9.5 0.5 fusion.17
  10.0 0.7 pad_clamp_fusion
  10.7 0.0 collective-permute-done.2
  10.7 0.7 collective-permute-done.1
  11.4 4.3 %collective-permute-done = f32[32768]{0:T(1024)} collective-permute-done((f32[32768]{0:T(1024)S(1)}, f32[32768]{0:T(1024)}, u32[]{:S(2)}, u32[]{:S(2)}) %collective-permute-start) | collective-permute-done | bytes 131104 | tf_op jit(solution)/shard_map/ppermute | solution.py:118
  15.7 1.0 %add_rsqrt_fusion = f32[32768]{0:T(1024)S(1)} fusion(f32[32768]{0:T(1024)S(1)} %collective-permute-done.2, f32[32768]{0:T(1024)S(1)} %collective-permute-done.1, f32[32768]{0:T(1024)S(1)} %fusion, f32[32768]{0:T(1024)} %collective-permute-done), kind=kLoop, calls=%fused_computation.23 | loop fusion | flops 163840 | bytes 655360 | tf_op jit(solution)/shard_map/sqrt | solution.py:122
  16.6 0.0 copy-done.1
  16.6 1.8 %fusion.5 = (f32[32768]{0:T(1024)S(1)}, f32[32768]{0:T(1024)S(1)}) fusion(bf16[40,32768]{1,0:T(8,128)(2,1)S(1)} %copy-done.1, f32[32768]{0:T(1024)S(1)} %add_rsqrt_fusion, pred[40]{0:T(512)(128)(4,1)S(1)} %get-tuple-element.14, pred[40]{0:T(512)(128)(4,1)S(1)} %get-tuple-element.13), kind=kLoop, calls=%fused_computation.8 | loop fusion | flops 10420224 | bytes 3014736 | tf_op jit(solution)/shard_map/reduce_sum | solution.py:126
  18.5 0.1 collective-permute-start.5
  18.6 0.2 collective-permute-start.4
  18.9 1.2 %collective-permute-start.3 = (bf16[2,64,128]{2,1,0:T(8,128)(2,1)S(1)}, bf16[2,64,128]{2,1,0:T(8,128)(2,1)S(1)}, u32[]{:S(2)}, u32[]{:S(2)}) collective-permute-start(bf16[2,64,128]{2,1,0:T(8,128)(2,1)S(1)} %get-tuple-element.12), channel_id=1, source_target_pairs={{0,1},{1,2},{2,3},{3,0},{4,5},{5,6},{6,7},{7,4},{8,9},{9,10},{10,1... | collective-permute-start | bytes 98312 | tf_op jit(solution)/shard_map/ppermute | solution.py:134
  20.1 0.1 broadcast_in_dim.39
  20.2 0.1 broadcast_in_dim.40
  20.3 1.1 %collective-permute-done.5 = bf16[2,64,128]{2,1,0:T(8,128)(2,1)S(1)} collective-permute-done((bf16[2,64,128]{2,1,0:T(8,128)(2,1)S(1)}, bf16[2,64,128]{2,1,0:T(8,128)(2,1)S(1)}, u32[]{:S(2)}, u32[]{:S(2)}) %collective-permute-start.5) | collective-permute-done | bytes 32800 | tf_op jit(solution)/shard_map/ppermute | solution.py:134
  21.4 1.6 %collective-permute-done.4 = bf16[2,64,128]{2,1,0:T(8,128)(2,1)S(1)} collective-permute-done((bf16[2,64,128]{2,1,0:T(8,128)(2,1)S(1)}, bf16[2,64,128]{2,1,0:T(8,128)(2,1)S(1)}, u32[]{:S(2)}, u32[]{:S(2)}) %collective-permute-start.4) | collective-permute-done | bytes 32800 | tf_op jit(solution)/shard_map/ppermute | solution.py:134
  23.0 0.8 collective-permute-done.3
  23.8 0.6 gather_fusion
  24.4 0.1 copy_select_fusion
  24.5 0.2 convolution_convert_fusion.1
  24.7 0.8 all_to_all.14
  25.5 13.7 %all-to-all-start = ((bf16[64,2,1024]{2,1,0:T(2,128)(2,1)}), bf16[64,2,1024]{2,1,0:T(2,128)(2,1)S(1)}, u32[]{:S(2)}, u32[]{:S(2)}) async-start(bf16[64,2,1024]{2,1,0:T(2,128)(2,1)} %all_to_all.14), calls=%async_computation | async-start | bytes 524288 | tf_op jit(solution)/shard_map/all_to_all | solution.py:154
  39.2 0.0 copy-done
  39.2 4.7 %subtract_convert_fusion = (bf16[128,1536]{1,0:T(8,128)(2,1)}, bf16[128,1536]{1,0:T(8,128)(2,1)}) fusion(bf16[2048,1536]{1,0:T(8,128)(2,1)} %param.9, bf16[1,128,2048]{2,1,0:T(8,128)(2,1)S(1)} %copy-done), kind=kOutput, calls=%fused_computation.13 | convolution fusion | flops 806092800 | bytes 7602176 | tf_op jit(solution)/shard_map/dot_general | solution.py:156
  43.9 7.3 %all-to-all-done = bf16[64,2,1024]{2,1,0:T(2,128)(2,1)S(1)} async-done(((bf16[64,2,1024]{2,1,0:T(2,128)(2,1)}), bf16[64,2,1024]{2,1,0:T(2,128)(2,1)S(1)}, u32[]{:S(2)}, u32[]{:S(2)}) %all-to-all-start) | async-done | bytes 262176 | tf_op jit(solution)/shard_map/all_to_all | solution.py:154
  51.2 0.9 reshape.100.rows_ref
  52.1 8.2 %shard_map.55 = bf16[1024,320]{1,0:T(8,128)(2,1)} custom-call(bf16[1024,128]{1,0:T(8,128)(2,1)} %reshape.100.rows_ref, bf16[128,1536]{1,0:T(8,128)(2,1)} %get-tuple-element.8.hi_ref, bf16[128,1536]{1,0:T(8,128)(2,1)} %get-tuple-element.7.lo_ref), custom_call_target="tpu_custom_call" | custom-call | tf_op jit(solution)/shard_map/pallas_call | solution.py:79
  60.3 2.4 %all_to_all.16 = bf16[64,2,2560]{2,1,0:T(2,128)(2,1)S(1)} reshape(bf16[1024,320]{1,0:T(8,128)(2,1)} %shard_map.55) | data formatting | bytes 1310720 | tf_op jit(solution)/shard_map/all_to_all | solution.py:161
  62.7 25.9 %all_to_all.21 = bf16[64,2,2560]{2,1,0:T(2,128)(2,1)S(1)} all-to-all(bf16[64,2,2560]{2,1,0:T(2,128)(2,1)S(1)} %all_to_all.16), channel_id=1, replica_groups=mesh['wide'=64,'seq'=4] {'wide'}, dimensions={0} | all-to-all | bytes 1310720 | tf_op jit(solution)/shard_map/all_to_all | solution.py:161
  88.6 0.2 all_to_all.18
  88.9 0.3 convolution_convert_fusion
  89.2 0.3 reshape.101
  89.5 0.5 copy.11
  90.0 1.4 %bitcast_convert_fusion = bf16[64,2,128,4,8]{2,4,3,1,0:T(8,128)(2,1)} fusion(bf16[64,2,8,32]{2,3,1,0:T(8,128)(2,1)S(1)} %bitcast.42, bf16[64,8,320]{2,1,0:T(8,128)(2,1)S(1)} %reshape.101), kind=kOutput, calls=%fused_computation.11 | convolution fusion | flops 8912896 | bytes 2359296
  (5 shorter events, 0.1 us)
Async XLA Ops:
  0.0 39.2 %copy-start = (bf16[1,128,2048]{2,1,0:T(8,128)(2,1)S(1)}, bf16[1,128,2048]{2,1,0:T(8,128)(2,1)}, u32[]{:S(2)}) copy-start(bf16[1,128,2048]{2,1,0:T(8,128)(2,1)} %param.8) | copy-start | bytes 1572868
  0.0 16.6 %copy-start.1 = (bf16[40,32768]{1,0:T(8,128)(2,1)S(1)}, bf16[40,32768]{1,0:T(8,128)(2,1)}, u32[]{:S(2)}) copy-start(bf16[40,32768]{1,0:T(8,128)(2,1)} %param.5) | copy-start | bytes 7864324
  2.6 8.1 %collective-permute-start.2 = (f32[32768]{0:T(1024)S(1)}, f32[32768]{0:T(1024)S(1)}, u32[]{:S(2)}, u32[]{:S(2)}) collective-permute-start(f32[32768]{0:T(1024)S(1)} %fusion), channel_id=1, source_target_pairs={{0,3},{1,0},{2,1},{3,2},{4,7},{5,4},{6,5},{7,6},{8,11},{9,8},{10,9... | collective-permute-start | bytes 393224 | tf_op jit(solution)/shard_map/ppermute | solution.py:118
  6.0 5.4 %collective-permute-start.1 = (f32[32768]{0:T(1024)S(1)}, f32[32768]{0:T(1024)S(1)}, u32[]{:S(2)}, u32[]{:S(2)}) collective-permute-start(f32[32768]{0:T(1024)S(1)} %fusion), channel_id=1, source_target_pairs={{0,2},{1,3},{2,0},{3,1},{4,6},{5,7},{6,4},{7,5},{8,10},{9,11},{10,... | collective-permute-start | bytes 393224 | tf_op jit(solution)/shard_map/ppermute | solution.py:118
  6.5 9.2 %collective-permute-start = (f32[32768]{0:T(1024)S(1)}, f32[32768]{0:T(1024)}, u32[]{:S(2)}, u32[]{:S(2)}) collective-permute-start(f32[32768]{0:T(1024)S(1)} %fusion), channel_id=1, source_target_pairs={{0,1},{1,2},{2,3},{3,0},{4,5},{5,6},{6,7},{7,4},{8,9},{9,10},{10,1... | collective-permute-start | bytes 393224 | tf_op jit(solution)/shard_map/ppermute | solution.py:118
  18.5 2.8 %collective-permute-start.5 = (bf16[2,64,128]{2,1,0:T(8,128)(2,1)S(1)}, bf16[2,64,128]{2,1,0:T(8,128)(2,1)S(1)}, u32[]{:S(2)}, u32[]{:S(2)}) collective-permute-start(bf16[2,64,128]{2,1,0:T(8,128)(2,1)S(1)} %get-tuple-element.10), channel_id=1, source_target_pairs={{0,3},{1,0},{2,1},{3,2},{4,7},{5,4},{6,5},{7,6},{8,11},{9,8},{10,9... | collective-permute-start | bytes 98312 | tf_op jit(solution)/shard_map/ppermute | solution.py:134
  18.6 4.4 %collective-permute-start.4 = (bf16[2,64,128]{2,1,0:T(8,128)(2,1)S(1)}, bf16[2,64,128]{2,1,0:T(8,128)(2,1)S(1)}, u32[]{:S(2)}, u32[]{:S(2)}) collective-permute-start(bf16[2,64,128]{2,1,0:T(8,128)(2,1)S(1)} %get-tuple-element.11), channel_id=1, source_target_pairs={{0,2},{1,3},{2,0},{3,1},{4,6},{5,7},{6,4},{7,5},{8,10},{9,11},{10,... | collective-permute-start | bytes 98312 | tf_op jit(solution)/shard_map/ppermute | solution.py:134
  18.9 4.9 %collective-permute-start.3 = (bf16[2,64,128]{2,1,0:T(8,128)(2,1)S(1)}, bf16[2,64,128]{2,1,0:T(8,128)(2,1)S(1)}, u32[]{:S(2)}, u32[]{:S(2)}) collective-permute-start(bf16[2,64,128]{2,1,0:T(8,128)(2,1)S(1)} %get-tuple-element.12), channel_id=1, source_target_pairs={{0,1},{1,2},{2,3},{3,0},{4,5},{5,6},{6,7},{7,4},{8,9},{9,10},{10,1... | collective-permute-start | bytes 98312 | tf_op jit(solution)/shard_map/ppermute | solution.py:134
  25.5 25.7 %all-to-all-start = ((bf16[64,2,1024]{2,1,0:T(2,128)(2,1)}), bf16[64,2,1024]{2,1,0:T(2,128)(2,1)S(1)}, u32[]{:S(2)}, u32[]{:S(2)}) async-start(bf16[64,2,1024]{2,1,0:T(2,128)(2,1)} %all_to_all.14), calls=%async_computation | async-start | bytes 524288 | tf_op jit(solution)/shard_map/all_to_all | solution.py:154

commit v14 on v13

--- a/solution.py
+++ b/solution.py
@@ -12,7 +12,7 @@
 SPB = 20
 CAP = 2
 BINS = 8
-ROWS = 256
+ROWS = 512
 SUB = 4
 
 

time: 91.7 us -> 91 us (level)
  no operation moved by 1% of the time
where the time goes in v14:
time: 91 us; the launch traced here: 90.7 us
  blocking collectives  25.9 us (28%)
  starting transfers between devices  19.8 us (22%)
  waiting for transfers between devices  15.8 us (17%)
  other arithmetic  8.32 us (9%)
  Pallas kernels  7.52 us (8%)
  local copies, waits for them, and re-layouts  6.64 us (7%)
  matrix products  6.55 us (7%)
    all_to_all x1, blocking collectives, body(): lax.all_to_all(payload, 'wide', split_axis=0, concat_axis=0, tiled=True)  25.9 us
    all_to_all x1, starting transfers between devices, body(): lax.all_to_all(outgoing, 'wide', split_axis=0, concat_axis=0, tiled=True)  13.7 us
    pallas_call x1, Pallas kernels, owner_payload(): pl.pallas_call(_owner_kernel, out_shape=jax.ShapeDtypeStruct((total, KVH...  7.52 us
    all_to_all x1, waiting for transfers between devices, body(): lax.all_to_all(outgoing, 'wide', split_axis=0, concat_axis=0, tiled=True)  7.29 us
    ppermute x3, waiting for transfers between devices, body(): received.append(lax.ppermute(partial, 'seq', pairs))  4.99 us
    dot_general x1, matrix products, body(): jnp.dot(weight_block, qkv_weight, preferred_element_type=jnp.float32)  4.66 us
    ppermute x3, starting transfers between devices, body(): received.append(lax.ppermute(partial, 'seq', pairs))  4.5 us
    ppermute x3, waiting for transfers between devices, body(): received.append(lax.ppermute(piece, 'seq', pairs))  3.51 us
  transfers between devices with their start and end apart: 7, of which 6 were waited for; matrix products, arithmetic and copies ran while one was open for 9% of the time, Pallas kernels for 0%

profile of v14, /device:TPU:1, one launch (start us, length us, event | category | flops | bytes accessed | tf_op | source)
XLA Modules:
  0.0 90.7 jit_solution(2242704011463480652)
XLA Ops:
  0.0 0.0 copy-start
  0.0 0.0 copy-start.1
  0.0 2.6 %fusion = f32[32768]{0:T(1024)S(1)} fusion(bf16[40,32768]{1,0:T(8,128)(2,1)} %param.5), kind=kLoop, calls=%fused_computation.3 | loop fusion | flops 3899392 | bytes 2752512 | tf_op jit(solution)/shard_map/reduce_sum | solution.py:114
  2.6 3.4 %collective-permute-start.2 = (f32[32768]{0:T(1024)S(1)}, f32[32768]{0:T(1024)S(1)}, u32[]{:S(2)}, u32[]{:S(2)}) collective-permute-start(f32[32768]{0:T(1024)S(1)} %fusion), channel_id=1, source_target_pairs={{0,3},{1,0},{2,1},{3,2},{4,7},{5,4},{6,5},{7,6},{8,11},{9,8},{10,9... | collective-permute-start | bytes 393224 | tf_op jit(solution)/shard_map/ppermute | solution.py:118
  6.0 0.5 collective-permute-start.1
  6.5 0.6 collective-permute-start
  7.1 0.8 dynamic_slice.10
  7.9 0.2 convert_reduce_fusion
  8.1 0.8 multiply_add_fusion
  8.8 0.7 subtract_compare_fusion
  9.5 0.5 fusion.17
  10.0 0.7 pad_clamp_fusion
  10.7 0.0 collective-permute-done.2
  10.7 0.7 collective-permute-done.1
  11.4 4.3 %collective-permute-done = f32[32768]{0:T(1024)} collective-permute-done((f32[32768]{0:T(1024)S(1)}, f32[32768]{0:T(1024)}, u32[]{:S(2)}, u32[]{:S(2)}) %collective-permute-start) | collective-permute-done | bytes 131104 | tf_op jit(solution)/shard_map/ppermute | solution.py:118
  15.7 1.0 %add_rsqrt_fusion = f32[32768]{0:T(1024)S(1)} fusion(f32[32768]{0:T(1024)S(1)} %collective-permute-done.2, f32[32768]{0:T(1024)S(1)} %collective-permute-done.1, f32[32768]{0:T(1024)S(1)} %fusion, f32[32768]{0:T(1024)} %collective-permute-done), kind=kLoop, calls=%fused_computation.23 | loop fusion | flops 163840 | bytes 655360 | tf_op jit(solution)/shard_map/sqrt | solution.py:122
  16.6 0.0 copy-done.1
  16.6 1.8 %fusion.5 = (f32[32768]{0:T(1024)S(1)}, f32[32768]{0:T(1024)S(1)}) fusion(bf16[40,32768]{1,0:T(8,128)(2,1)S(1)} %copy-done.1, f32[32768]{0:T(1024)S(1)} %add_rsqrt_fusion, pred[40]{0:T(512)(128)(4,1)S(1)} %get-tuple-element.14, pred[40]{0:T(512)(128)(4,1)S(1)} %get-tuple-element.13), kind=kLoop, calls=%fused_computation.8 | loop fusion | flops 10420224 | bytes 3014736 | tf_op jit(solution)/shard_map/reduce_sum | solution.py:126
  18.5 0.1 collective-permute-start.5
  18.6 0.2 collective-permute-start.4
  18.9 1.2 %collective-permute-start.3 = (bf16[2,64,128]{2,1,0:T(8,128)(2,1)S(1)}, bf16[2,64,128]{2,1,0:T(8,128)(2,1)S(1)}, u32[]{:S(2)}, u32[]{:S(2)}) collective-permute-start(bf16[2,64,128]{2,1,0:T(8,128)(2,1)S(1)} %get-tuple-element.12), channel_id=1, source_target_pairs={{0,1},{1,2},{2,3},{3,0},{4,5},{5,6},{6,7},{7,4},{8,9},{9,10},{10,1... | collective-permute-start | bytes 98312 | tf_op jit(solution)/shard_map/ppermute | solution.py:134
  20.1 0.1 broadcast_in_dim.39
  20.2 0.1 broadcast_in_dim.40
  20.3 1.1 %collective-permute-done.5 = bf16[2,64,128]{2,1,0:T(8,128)(2,1)S(1)} collective-permute-done((bf16[2,64,128]{2,1,0:T(8,128)(2,1)S(1)}, bf16[2,64,128]{2,1,0:T(8,128)(2,1)S(1)}, u32[]{:S(2)}, u32[]{:S(2)}) %collective-permute-start.5) | collective-permute-done | bytes 32800 | tf_op jit(solution)/shard_map/ppermute | solution.py:134
  21.4 1.6 %collective-permute-done.4 = bf16[2,64,128]{2,1,0:T(8,128)(2,1)S(1)} collective-permute-done((bf16[2,64,128]{2,1,0:T(8,128)(2,1)S(1)}, bf16[2,64,128]{2,1,0:T(8,128)(2,1)S(1)}, u32[]{:S(2)}, u32[]{:S(2)}) %collective-permute-start.4) | collective-permute-done | bytes 32800 | tf_op jit(solution)/shard_map/ppermute | solution.py:134
  23.0 0.8 collective-permute-done.3
  23.8 0.6 gather_fusion
  24.4 0.1 copy_select_fusion
  24.5 0.2 convolution_convert_fusion.1
  24.7 0.8 all_to_all.14
  25.5 13.7 %all-to-all-start = ((bf16[64,2,1024]{2,1,0:T(2,128)(2,1)}), bf16[64,2,1024]{2,1,0:T(2,128)(2,1)S(1)}, u32[]{:S(2)}, u32[]{:S(2)}) async-start(bf16[64,2,1024]{2,1,0:T(2,128)(2,1)} %all_to_all.14), calls=%async_computation | async-start | bytes 524288 | tf_op jit(solution)/shard_map/all_to_all | solution.py:154
  39.2 0.0 copy-done
  39.2 4.7 %subtract_convert_fusion = (bf16[128,1536]{1,0:T(8,128)(2,1)}, bf16[128,1536]{1,0:T(8,128)(2,1)}) fusion(bf16[2048,1536]{1,0:T(8,128)(2,1)} %param.9, bf16[1,128,2048]{2,1,0:T(8,128)(2,1)S(1)} %copy-done), kind=kOutput, calls=%fused_computation.13 | convolution fusion | flops 806092800 | bytes 7602176 | tf_op jit(solution)/shard_map/dot_general | solution.py:156
  43.9 7.3 %all-to-all-done = bf16[64,2,1024]{2,1,0:T(2,128)(2,1)S(1)} async-done(((bf16[64,2,1024]{2,1,0:T(2,128)(2,1)}), bf16[64,2,1024]{2,1,0:T(2,128)(2,1)S(1)}, u32[]{:S(2)}, u32[]{:S(2)}) %all-to-all-start) | async-done | bytes 262176 | tf_op jit(solution)/shard_map/all_to_all | solution.py:154
  51.2 0.9 reshape.100.rows_ref
  52.1 7.5 %shard_map.55 = bf16[1024,320]{1,0:T(8,128)(2,1)} custom-call(bf16[1024,128]{1,0:T(8,128)(2,1)} %reshape.100.rows_ref, bf16[128,1536]{1,0:T(8,128)(2,1)} %get-tuple-element.8.hi_ref, bf16[128,1536]{1,0:T(8,128)(2,1)} %get-tuple-element.7.lo_ref), custom_call_target="tpu_custom_call" | custom-call | tf_op jit(solution)/shard_map/pallas_call | solution.py:79
  59.6 2.4 %all_to_all.16 = bf16[64,2,2560]{2,1,0:T(2,128)(2,1)S(1)} reshape(bf16[1024,320]{1,0:T(8,128)(2,1)} %shard_map.55) | data formatting | bytes 1310720 | tf_op jit(solution)/shard_map/all_to_all | solution.py:161
  62.0 25.9 %all_to_all.21 = bf16[64,2,2560]{2,1,0:T(2,128)(2,1)S(1)} all-to-all(bf16[64,2,2560]{2,1,0:T(2,128)(2,1)S(1)} %all_to_all.16), channel_id=1, replica_groups=mesh['wide'=64,'seq'=4] {'wide'}, dimensions={0} | all-to-all | bytes 1310720 | tf_op jit(solution)/shard_map/all_to_all | solution.py:161
  87.9 0.2 all_to_all.18
  88.2 0.3 convolution_convert_fusion
  88.5 0.3 reshape.101
  88.8 0.5 copy.11
  89.3 1.4 %bitcast_convert_fusion = bf16[64,2,128,4,8]{2,4,3,1,0:T(8,128)(2,1)} fusion(bf16[64,2,8,32]{2,3,1,0:T(8,128)(2,1)S(1)} %bitcast.42, bf16[64,8,320]{2,1,0:T(8,128)(2,1)S(1)} %reshape.101), kind=kOutput, calls=%fused_computation.11 | convolution fusion | flops 8912896 | bytes 2359296
  (5 shorter events, 0.1 us)
Async XLA Ops:
  0.0 39.2 %copy-start = (bf16[1,128,2048]{2,1,0:T(8,128)(2,1)S(1)}, bf16[1,128,2048]{2,1,0:T(8,128)(2,1)}, u32[]{:S(2)}) copy-start(bf16[1,128,2048]{2,1,0:T(8,128)(2,1)} %param.8) | copy-start | bytes 1572868
  0.0 16.6 %copy-start.1 = (bf16[40,32768]{1,0:T(8,128)(2,1)S(1)}, bf16[40,32768]{1,0:T(8,128)(2,1)}, u32[]{:S(2)}) copy-start(bf16[40,32768]{1,0:T(8,128)(2,1)} %param.5) | copy-start | bytes 7864324
  2.6 8.1 %collective-permute-start.2 = (f32[32768]{0:T(1024)S(1)}, f32[32768]{0:T(1024)S(1)}, u32[]{:S(2)}, u32[]{:S(2)}) collective-permute-start(f32[32768]{0:T(1024)S(1)} %fusion), channel_id=1, source_target_pairs={{0,3},{1,0},{2,1},{3,2},{4,7},{5,4},{6,5},{7,6},{8,11},{9,8},{10,9... | collective-permute-start | bytes 393224 | tf_op jit(solution)/shard_map/ppermute | solution.py:118
  6.0 5.4 %collective-permute-start.1 = (f32[32768]{0:T(1024)S(1)}, f32[32768]{0:T(1024)S(1)}, u32[]{:S(2)}, u32[]{:S(2)}) collective-permute-start(f32[32768]{0:T(1024)S(1)} %fusion), channel_id=1, source_target_pairs={{0,2},{1,3},{2,0},{3,1},{4,6},{5,7},{6,4},{7,5},{8,10},{9,11},{10,... | collective-permute-start | bytes 393224 | tf_op jit(solution)/shard_map/ppermute | solution.py:118
  6.5 9.2 %collective-permute-start = (f32[32768]{0:T(1024)S(1)}, f32[32768]{0:T(1024)}, u32[]{:S(2)}, u32[]{:S(2)}) collective-permute-start(f32[32768]{0:T(1024)S(1)} %fusion), channel_id=1, source_target_pairs={{0,1},{1,2},{2,3},{3,0},{4,5},{5,6},{6,7},{7,4},{8,9},{9,10},{10,1... | collective-permute-start | bytes 393224 | tf_op jit(solution)/shard_map/ppermute | solution.py:118
  18.5 2.8 %collective-permute-start.5 = (bf16[2,64,128]{2,1,0:T(8,128)(2,1)S(1)}, bf16[2,64,128]{2,1,0:T(8,128)(2,1)S(1)}, u32[]{:S(2)}, u32[]{:S(2)}) collective-permute-start(bf16[2,64,128]{2,1,0:T(8,128)(2,1)S(1)} %get-tuple-element.10), channel_id=1, source_target_pairs={{0,3},{1,0},{2,1},{3,2},{4,7},{5,4},{6,5},{7,6},{8,11},{9,8},{10,9... | collective-permute-start | bytes 98312 | tf_op jit(solution)/shard_map/ppermute | solution.py:134
  18.6 4.4 %collective-permute-start.4 = (bf16[2,64,128]{2,1,0:T(8,128)(2,1)S(1)}, bf16[2,64,128]{2,1,0:T(8,128)(2,1)S(1)}, u32[]{:S(2)}, u32[]{:S(2)}) collective-permute-start(bf16[2,64,128]{2,1,0:T(8,128)(2,1)S(1)} %get-tuple-element.11), channel_id=1, source_target_pairs={{0,2},{1,3},{2,0},{3,1},{4,6},{5,7},{6,4},{7,5},{8,10},{9,11},{10,... | collective-permute-start | bytes 98312 | tf_op jit(solution)/shard_map/ppermute | solution.py:134
  18.9 4.9 %collective-permute-start.3 = (bf16[2,64,128]{2,1,0:T(8,128)(2,1)S(1)}, bf16[2,64,128]{2,1,0:T(8,128)(2,1)S(1)}, u32[]{:S(2)}, u32[]{:S(2)}) collective-permute-start(bf16[2,64,128]{2,1,0:T(8,128)(2,1)S(1)} %get-tuple-element.12), channel_id=1, source_target_pairs={{0,1},{1,2},{2,3},{3,0},{4,5},{5,6},{6,7},{7,4},{8,9},{9,10},{10,1... | collective-permute-start | bytes 98312 | tf_op jit(solution)/shard_map/ppermute | solution.py:134
  25.5 25.7 %all-to-all-start = ((bf16[64,2,1024]{2,1,0:T(2,128)(2,1)}), bf16[64,2,1024]{2,1,0:T(2,128)(2,1)S(1)}, u32[]{:S(2)}, u32[]{:S(2)}) async-start(bf16[64,2,1024]{2,1,0:T(2,128)(2,1)} %all_to_all.14), calls=%async_computation | async-start | bytes 524288 | tf_op jit(solution)/shard_map/all_to_all | solution.py:154

commit v15 on v14

--- a/solution.py
+++ b/solution.py
@@ -12,7 +12,7 @@
 SPB = 20
 CAP = 2
 BINS = 8
-ROWS = 512
+ROWS = 1024
 SUB = 4
 
 

time: 91 us -> 90.9 us (level)
  no operation moved by 1% of the time
where the time goes in v15:
time: 90.9 us; the launch traced here: 90.5 us
  blocking collectives  25.9 us (28%)
  starting transfers between devices  19.8 us (22%)
  waiting for transfers between devices  15.8 us (17%)
  other arithmetic  8.32 us (9%)
  Pallas kernels  7.35 us (8%)
  local copies, waits for them, and re-layouts  6.64 us (7%)
  matrix products  6.55 us (7%)
    all_to_all x1, blocking collectives, body(): lax.all_to_all(payload, 'wide', split_axis=0, concat_axis=0, tiled=True)  25.9 us
    all_to_all x1, starting transfers between devices, body(): lax.all_to_all(outgoing, 'wide', split_axis=0, concat_axis=0, tiled=True)  13.7 us
    pallas_call x1, Pallas kernels, owner_payload(): pl.pallas_call(_owner_kernel, out_shape=jax.ShapeDtypeStruct((total, KVH...  7.35 us
    all_to_all x1, waiting for transfers between devices, body(): lax.all_to_all(outgoing, 'wide', split_axis=0, concat_axis=0, tiled=True)  7.29 us
    ppermute x3, waiting for transfers between devices, body(): received.append(lax.ppermute(partial, 'seq', pairs))  4.99 us
    dot_general x1, matrix products, body(): jnp.dot(weight_block, qkv_weight, preferred_element_type=jnp.float32)  4.66 us
    ppermute x3, starting transfers between devices, body(): received.append(lax.ppermute(partial, 'seq', pairs))  4.5 us
    ppermute x3, waiting for transfers between devices, body(): received.append(lax.ppermute(piece, 'seq', pairs))  3.51 us
  transfers between devices with their start and end apart: 7, of which 6 were waited for; matrix products, arithmetic and copies ran while one was open for 9% of the time, Pallas kernels for 0%

profile of v15, /device:TPU:1, one launch (start us, length us, event | category | flops | bytes accessed | tf_op | source)
XLA Modules:
  0.0 90.5 jit_solution(10774272832607809339)
XLA Ops:
  0.0 0.0 copy-start
  0.0 0.0 copy-start.1
  0.0 2.6 %fusion = f32[32768]{0:T(1024)S(1)} fusion(bf16[40,32768]{1,0:T(8,128)(2,1)} %param.5), kind=kLoop, calls=%fused_computation.3 | loop fusion | flops 3899392 | bytes 2752512 | tf_op jit(solution)/shard_map/reduce_sum | solution.py:114
  2.6 3.4 %collective-permute-start.2 = (f32[32768]{0:T(1024)S(1)}, f32[32768]{0:T(1024)S(1)}, u32[]{:S(2)}, u32[]{:S(2)}) collective-permute-start(f32[32768]{0:T(1024)S(1)} %fusion), channel_id=1, source_target_pairs={{0,3},{1,0},{2,1},{3,2},{4,7},{5,4},{6,5},{7,6},{8,11},{9,8},{10,9... | collective-permute-start | bytes 393224 | tf_op jit(solution)/shard_map/ppermute | solution.py:118
  6.0 0.5 collective-permute-start.1
  6.5 0.6 collective-permute-start
  7.1 0.8 dynamic_slice.10
  7.9 0.2 convert_reduce_fusion
  8.1 0.8 multiply_add_fusion
  8.8 0.7 subtract_compare_fusion
  9.5 0.5 fusion.17
  10.0 0.7 pad_clamp_fusion
  10.7 0.0 collective-permute-done.2
  10.7 0.7 collective-permute-done.1
  11.4 4.3 %collective-permute-done = f32[32768]{0:T(1024)} collective-permute-done((f32[32768]{0:T(1024)S(1)}, f32[32768]{0:T(1024)}, u32[]{:S(2)}, u32[]{:S(2)}) %collective-permute-start) | collective-permute-done | bytes 131104 | tf_op jit(solution)/shard_map/ppermute | solution.py:118
  15.7 1.0 %add_rsqrt_fusion = f32[32768]{0:T(1024)S(1)} fusion(f32[32768]{0:T(1024)S(1)} %collective-permute-done.2, f32[32768]{0:T(1024)S(1)} %collective-permute-done.1, f32[32768]{0:T(1024)S(1)} %fusion, f32[32768]{0:T(1024)} %collective-permute-done), kind=kLoop, calls=%fused_computation.23 | loop fusion | flops 163840 | bytes 655360 | tf_op jit(solution)/shard_map/sqrt | solution.py:122
  16.6 0.0 copy-done.1
  16.6 1.8 %fusion.5 = (f32[32768]{0:T(1024)S(1)}, f32[32768]{0:T(1024)S(1)}) fusion(bf16[40,32768]{1,0:T(8,128)(2,1)S(1)} %copy-done.1, f32[32768]{0:T(1024)S(1)} %add_rsqrt_fusion, pred[40]{0:T(512)(128)(4,1)S(1)} %get-tuple-element.14, pred[40]{0:T(512)(128)(4,1)S(1)} %get-tuple-element.13), kind=kLoop, calls=%fused_computation.8 | loop fusion | flops 10420224 | bytes 3014736 | tf_op jit(solution)/shard_map/reduce_sum | solution.py:126
  18.5 0.1 collective-permute-start.5
  18.6 0.2 collective-permute-start.4
  18.9 1.2 %collective-permute-start.3 = (bf16[2,64,128]{2,1,0:T(8,128)(2,1)S(1)}, bf16[2,64,128]{2,1,0:T(8,128)(2,1)S(1)}, u32[]{:S(2)}, u32[]{:S(2)}) collective-permute-start(bf16[2,64,128]{2,1,0:T(8,128)(2,1)S(1)} %get-tuple-element.12), channel_id=1, source_target_pairs={{0,1},{1,2},{2,3},{3,0},{4,5},{5,6},{6,7},{7,4},{8,9},{9,10},{10,1... | collective-permute-start | bytes 98312 | tf_op jit(solution)/shard_map/ppermute | solution.py:134
  20.1 0.1 broadcast_in_dim.39
  20.2 0.1 broadcast_in_dim.40
  20.3 1.1 %collective-permute-done.5 = bf16[2,64,128]{2,1,0:T(8,128)(2,1)S(1)} collective-permute-done((bf16[2,64,128]{2,1,0:T(8,128)(2,1)S(1)}, bf16[2,64,128]{2,1,0:T(8,128)(2,1)S(1)}, u32[]{:S(2)}, u32[]{:S(2)}) %collective-permute-start.5) | collective-permute-done | bytes 32800 | tf_op jit(solution)/shard_map/ppermute | solution.py:134
  21.4 1.6 %collective-permute-done.4 = bf16[2,64,128]{2,1,0:T(8,128)(2,1)S(1)} collective-permute-done((bf16[2,64,128]{2,1,0:T(8,128)(2,1)S(1)}, bf16[2,64,128]{2,1,0:T(8,128)(2,1)S(1)}, u32[]{:S(2)}, u32[]{:S(2)}) %collective-permute-start.4) | collective-permute-done | bytes 32800 | tf_op jit(solution)/shard_map/ppermute | solution.py:134
  23.0 0.8 collective-permute-done.3
  23.8 0.6 gather_fusion
  24.4 0.1 copy_select_fusion
  24.5 0.2 convolution_convert_fusion.1
  24.7 0.8 all_to_all.14
  25.5 13.7 %all-to-all-start = ((bf16[64,2,1024]{2,1,0:T(2,128)(2,1)}), bf16[64,2,1024]{2,1,0:T(2,128)(2,1)S(1)}, u32[]{:S(2)}, u32[]{:S(2)}) async-start(bf16[64,2,1024]{2,1,0:T(2,128)(2,1)} %all_to_all.14), calls=%async_computation | async-start | bytes 524288 | tf_op jit(solution)/shard_map/all_to_all | solution.py:154
  39.2 0.0 copy-done
  39.2 4.7 %subtract_convert_fusion = (bf16[128,1536]{1,0:T(8,128)(2,1)}, bf16[128,1536]{1,0:T(8,128)(2,1)}) fusion(bf16[2048,1536]{1,0:T(8,128)(2,1)} %param.9, bf16[1,128,2048]{2,1,0:T(8,128)(2,1)S(1)} %copy-done), kind=kOutput, calls=%fused_computation.13 | convolution fusion | flops 806092800 | bytes 7602176 | tf_op jit(solution)/shard_map/dot_general | solution.py:156
  43.9 7.3 %all-to-all-done = bf16[64,2,1024]{2,1,0:T(2,128)(2,1)S(1)} async-done(((bf16[64,2,1024]{2,1,0:T(2,128)(2,1)}), bf16[64,2,1024]{2,1,0:T(2,128)(2,1)S(1)}, u32[]{:S(2)}, u32[]{:S(2)}) %all-to-all-start) | async-done | bytes 262176 | tf_op jit(solution)/shard_map/all_to_all | solution.py:154
  51.2 0.9 reshape.100.rows_ref
  52.1 7.4 %shard_map.55 = bf16[1024,320]{1,0:T(8,128)(2,1)} custom-call(bf16[1024,128]{1,0:T(8,128)(2,1)} %reshape.100.rows_ref, bf16[128,1536]{1,0:T(8,128)(2,1)} %get-tuple-element.8.hi_ref, bf16[128,1536]{1,0:T(8,128)(2,1)} %get-tuple-element.7.lo_ref), custom_call_target="tpu_custom_call" | custom-call | tf_op jit(solution)/shard_map/pallas_call | solution.py:79
  59.4 2.4 %all_to_all.16 = bf16[64,2,2560]{2,1,0:T(2,128)(2,1)S(1)} reshape(bf16[1024,320]{1,0:T(8,128)(2,1)} %shard_map.55) | data formatting | bytes 1310720 | tf_op jit(solution)/shard_map/all_to_all | solution.py:161
  61.8 25.9 %all_to_all.21 = bf16[64,2,2560]{2,1,0:T(2,128)(2,1)S(1)} all-to-all(bf16[64,2,2560]{2,1,0:T(2,128)(2,1)S(1)} %all_to_all.16), channel_id=1, replica_groups=mesh['wide'=64,'seq'=4] {'wide'}, dimensions={0} | all-to-all | bytes 1310720 | tf_op jit(solution)/shard_map/all_to_all | solution.py:161
  87.8 0.2 all_to_all.18
  88.0 0.3 convolution_convert_fusion
  88.3 0.3 reshape.101
  88.6 0.5 copy.11
  89.1 1.4 %bitcast_convert_fusion = bf16[64,2,128,4,8]{2,4,3,1,0:T(8,128)(2,1)} fusion(bf16[64,2,8,32]{2,3,1,0:T(8,128)(2,1)S(1)} %bitcast.42, bf16[64,8,320]{2,1,0:T(8,128)(2,1)S(1)} %reshape.101), kind=kOutput, calls=%fused_computation.11 | convolution fusion | flops 8912896 | bytes 2359296
  (5 shorter events, 0.1 us)
Async XLA Ops:
  0.0 39.2 %copy-start = (bf16[1,128,2048]{2,1,0:T(8,128)(2,1)S(1)}, bf16[1,128,2048]{2,1,0:T(8,128)(2,1)}, u32[]{:S(2)}) copy-start(bf16[1,128,2048]{2,1,0:T(8,128)(2,1)} %param.8) | copy-start | bytes 1572868
  0.0 16.6 %copy-start.1 = (bf16[40,32768]{1,0:T(8,128)(2,1)S(1)}, bf16[40,32768]{1,0:T(8,128)(2,1)}, u32[]{:S(2)}) copy-start(bf16[40,32768]{1,0:T(8,128)(2,1)} %param.5) | copy-start | bytes 7864324
  2.6 8.1 %collective-permute-start.2 = (f32[32768]{0:T(1024)S(1)}, f32[32768]{0:T(1024)S(1)}, u32[]{:S(2)}, u32[]{:S(2)}) collective-permute-start(f32[32768]{0:T(1024)S(1)} %fusion), channel_id=1, source_target_pairs={{0,3},{1,0},{2,1},{3,2},{4,7},{5,4},{6,5},{7,6},{8,11},{9,8},{10,9... | collective-permute-start | bytes 393224 | tf_op jit(solution)/shard_map/ppermute | solution.py:118
  6.0 5.4 %collective-permute-start.1 = (f32[32768]{0:T(1024)S(1)}, f32[32768]{0:T(1024)S(1)}, u32[]{:S(2)}, u32[]{:S(2)}) collective-permute-start(f32[32768]{0:T(1024)S(1)} %fusion), channel_id=1, source_target_pairs={{0,2},{1,3},{2,0},{3,1},{4,6},{5,7},{6,4},{7,5},{8,10},{9,11},{10,... | collective-permute-start | bytes 393224 | tf_op jit(solution)/shard_map/ppermute | solution.py:118
  6.5 9.2 %collective-permute-start = (f32[32768]{0:T(1024)S(1)}, f32[32768]{0:T(1024)}, u32[]{:S(2)}, u32[]{:S(2)}) collective-permute-start(f32[32768]{0:T(1024)S(1)} %fusion), channel_id=1, source_target_pairs={{0,1},{1,2},{2,3},{3,0},{4,5},{5,6},{6,7},{7,4},{8,9},{9,10},{10,1... | collective-permute-start | bytes 393224 | tf_op jit(solution)/shard_map/ppermute | solution.py:118
  18.5 2.8 %collective-permute-start.5 = (bf16[2,64,128]{2,1,0:T(8,128)(2,1)S(1)}, bf16[2,64,128]{2,1,0:T(8,128)(2,1)S(1)}, u32[]{:S(2)}, u32[]{:S(2)}) collective-permute-start(bf16[2,64,128]{2,1,0:T(8,128)(2,1)S(1)} %get-tuple-element.10), channel_id=1, source_target_pairs={{0,3},{1,0},{2,1},{3,2},{4,7},{5,4},{6,5},{7,6},{8,11},{9,8},{10,9... | collective-permute-start | bytes 98312 | tf_op jit(solution)/shard_map/ppermute | solution.py:134
  18.6 4.4 %collective-permute-start.4 = (bf16[2,64,128]{2,1,0:T(8,128)(2,1)S(1)}, bf16[2,64,128]{2,1,0:T(8,128)(2,1)S(1)}, u32[]{:S(2)}, u32[]{:S(2)}) collective-permute-start(bf16[2,64,128]{2,1,0:T(8,128)(2,1)S(1)} %get-tuple-element.11), channel_id=1, source_target_pairs={{0,2},{1,3},{2,0},{3,1},{4,6},{5,7},{6,4},{7,5},{8,10},{9,11},{10,... | collective-permute-start | bytes 98312 | tf_op jit(solution)/shard_map/ppermute | solution.py:134
  18.9 4.9 %collective-permute-start.3 = (bf16[2,64,128]{2,1,0:T(8,128)(2,1)S(1)}, bf16[2,64,128]{2,1,0:T(8,128)(2,1)S(1)}, u32[]{:S(2)}, u32[]{:S(2)}) collective-permute-start(bf16[2,64,128]{2,1,0:T(8,128)(2,1)S(1)} %get-tuple-element.12), channel_id=1, source_target_pairs={{0,1},{1,2},{2,3},{3,0},{4,5},{5,6},{6,7},{7,4},{8,9},{9,10},{10,1... | collective-permute-start | bytes 98312 | tf_op jit(solution)/shard_map/ppermute | solution.py:134
  25.5 25.7 %all-to-all-start = ((bf16[64,2,1024]{2,1,0:T(2,128)(2,1)}), bf16[64,2,1024]{2,1,0:T(2,128)(2,1)S(1)}, u32[]{:S(2)}, u32[]{:S(2)}) async-start(bf16[64,2,1024]{2,1,0:T(2,128)(2,1)} %all_to_all.14), calls=%async_computation | async-start | bytes 524288 | tf_op jit(solution)/shard_map/all_to_all | solution.py:154

commit v16 on v14

--- a/solution.py
+++ b/solution.py
@@ -16,7 +16,7 @@
 SUB = 4
 
 
-def _owner_kernel(rows_ref, hi_ref, lo_ref, o_ref, w_ref):
+def _owner_kernel(rows_ref, hi_ref, lo_ref, o_ref, w_ref, v_ref):
     group_size = HEADS // KVH
     sub_rows = SUB * BINS
     cols = SUB * group_size * BINS
@@ -26,7 +26,9 @@
         rows, lo_ref[...], preferred_element_type=jnp.float32
     )
     projected = projected.astype(jnp.bfloat16)
-    o_ref[:, :value_width] = projected[:, (HEADS + KVH) * HD :]
+    for g in range(KVH):
+        col = (HEADS + KVH + g) * HD
+        v_ref[g] = projected[:, col : col + HD].astype(jnp.float32)
     row_patch = lax.broadcasted_iota(jnp.int32, (sub_rows, cols), 0) // BINS
     col_patch = lax.broadcasted_iota(jnp.int32, (sub_rows, cols), 1) // (group_size * BINS)
     same = row_patch == col_patch
@@ -70,7 +72,15 @@
                     compact = compact + tile[:, c * width : (c + 1) * width]
                 row0 = base + p * BINS
                 w_ref[row0 : row0 + BINS, g * width : (g + 1) * width] = compact
-    o_ref[:, value_width:] = w_ref[...].astype(jnp.bfloat16)
+    slots = rows_ref.shape[0] // BINS
+    weight_width = HEADS * BINS
+    for j in range(BINS):
+        picked = pl.ds(j, slots, stride=BINS)
+        for g in range(KVH):
+            col = j * value_width + g * HD
+            o_ref[:, col : col + HD] = v_ref[g, picked, :].astype(jnp.bfloat16)
+        base = BINS * value_width + j * weight_width
+        o_ref[:, base : base + weight_width] = w_ref[picked, :][:, :weight_width].astype(jnp.bfloat16)
 
 
 def owner_payload(rows, merged_hi, merged_lo):
@@ -78,23 +88,31 @@
     width = merged_hi.shape[1]
     return pl.pallas_call(
         _owner_kernel,
-        out_shape=jax.ShapeDtypeStruct((total, KVH * HD + HEADS * BINS), jnp.bfloat16),
+        out_shape=jax.ShapeDtypeStruct(
+            (total // BINS, BINS * (KVH * HD + HEADS * BINS)), jnp.bfloat16
+        ),
         grid=(total // ROWS,),
         in_specs=[
             pl.BlockSpec((ROWS, depth), lambda i: (i, 0)),
             pl.BlockSpec((depth, width), lambda i: (0, 0)),
             pl.BlockSpec((depth, width), lambda i: (0, 0)),
         ],
-        out_specs=pl.BlockSpec((ROWS, KVH * HD + HEADS * BINS), lambda i: (i, 0)),
-        scratch_shapes=[pltpu.VMEM((ROWS, HEADS * BINS), jnp.float32)],
+        out_specs=pl.BlockSpec(
+            (ROWS // BINS, BINS * (KVH * HD + HEADS * BINS)), lambda i: (i, 0)
+        ),
+        scratch_shapes=[
+            pltpu.VMEM((ROWS, HD), jnp.float32),
+            pltpu.VMEM((KVH, ROWS, HD), jnp.float32),
+        ],
     )(rows, merged_hi, merged_lo)
 
 
 def heads_from(payload):
     n = payload.shape[0]
     group_size = HEADS // KVH
-    v = payload[:, :, : KVH * HD].reshape(n, BINS, KVH, HD)
-    w = payload[:, :, KVH * HD :].reshape(n, BINS, KVH, group_size, BINS)
+    split = BINS * KVH * HD
+    v = payload[:, :split].reshape(n, BINS, KVH, HD)
+    w = payload[:, split:].reshape(n, BINS, KVH, group_size, BINS)
     mixed = jnp.einsum("pjgri,pjge->pigre", w, v, preferred_element_type=jnp.float32)
     return mixed.reshape(n, BINS, HEADS * HD).astype(jnp.bfloat16)
 
@@ -160,7 +178,7 @@
     payload = owner_payload(rows, merged_hi, merged_lo).reshape(slot_count, -1)
     returned = lax.all_to_all(payload, "wide", split_axis=0, concat_axis=0, tiled=True)
     mine = jnp.dot(dispatch.T, returned, preferred_element_type=jnp.float32).astype(jnp.bfloat16)
-    return heads_from(mine.reshape(quarter, all_bins, -1))
+    return heads_from(mine)
 
 
 def solution(mesh):

time: 91 us -> 91.8 us (level)
    reshape x1 -> x2, local copies, waits for them, and re-layouts: 0.3 us -> 1.75 us  [the longest x1 1.57 us: heads_from(): w = payload[:, split:].reshape(n, BINS, KVH, group_size, BINS)]
where the time goes in v16:
time: 91.8 us; the launch traced here: 91.5 us
  blocking collectives  25.9 us (28%)
  starting transfers between devices  19.8 us (22%)
  waiting for transfers between devices  15.8 us (17%)
  other arithmetic  8.32 us (9%)
  Pallas kernels  7.65 us (8%)
  local copies, waits for them, and re-layouts  7.31 us (8%)
  matrix products  6.55 us (7%)
    all_to_all x1, blocking collectives, body(): lax.all_to_all(payload, 'wide', split_axis=0, concat_axis=0, tiled=True)  25.9 us
    all_to_all x1, starting transfers between devices, body(): lax.all_to_all(outgoing, 'wide', split_axis=0, concat_axis=0, tiled=True)  13.7 us
    pallas_call x1, Pallas kernels, owner_payload(): pl.pallas_call(_owner_kernel, out_shape=jax.ShapeDtypeStruct((total // BI...  7.65 us
    all_to_all x1, waiting for transfers between devices, body(): lax.all_to_all(outgoing, 'wide', split_axis=0, concat_axis=0, tiled=True)  7.29 us
    ppermute x3, waiting for transfers between devices, body(): received.append(lax.ppermute(partial, 'seq', pairs))  4.99 us
    dot_general x1, matrix products, body(): jnp.dot(weight_block, qkv_weight, preferred_element_type=jnp.float32)  4.66 us
    ppermute x3, starting transfers between devices, body(): received.append(lax.ppermute(partial, 'seq', pairs))  4.5 us
    ppermute x3, waiting for transfers between devices, body(): received.append(lax.ppermute(piece, 'seq', pairs))  3.51 us
  transfers between devices with their start and end apart: 7, of which 6 were waited for; matrix products, arithmetic and copies ran while one was open for 9% of the time, Pallas kernels for 0%

profile of v16, /device:TPU:1, one launch (start us, length us, event | category | flops | bytes accessed | tf_op | source)
XLA Modules:
  0.0 91.5 jit_solution(1840024959109877840)
XLA Ops:
  0.0 0.0 copy-start
  0.0 0.0 copy-start.1
  0.0 2.6 %fusion = f32[32768]{0:T(1024)S(1)} fusion(bf16[40,32768]{1,0:T(8,128)(2,1)} %param.5), kind=kLoop, calls=%fused_computation.3 | loop fusion | flops 3899392 | bytes 2752512 | tf_op jit(solution)/shard_map/reduce_sum | solution.py:132
  2.6 3.4 %collective-permute-start.2 = (f32[32768]{0:T(1024)S(1)}, f32[32768]{0:T(1024)S(1)}, u32[]{:S(2)}, u32[]{:S(2)}) collective-permute-start(f32[32768]{0:T(1024)S(1)} %fusion), channel_id=1, source_target_pairs={{0,3},{1,0},{2,1},{3,2},{4,7},{5,4},{6,5},{7,6},{8,11},{9,8},{10,9... | collective-permute-start | bytes 393224 | tf_op jit(solution)/shard_map/ppermute | solution.py:136
  6.0 0.5 collective-permute-start.1
  6.5 0.6 collective-permute-start
  7.1 0.8 dynamic_slice.10
  7.9 0.2 convert_reduce_fusion
  8.1 0.8 multiply_add_fusion
  8.8 0.7 subtract_compare_fusion
  9.5 0.5 fusion.19
  10.0 0.7 pad_clamp_fusion
  10.7 0.0 collective-permute-done.2
  10.7 0.7 collective-permute-done.1
  11.4 4.3 %collective-permute-done = f32[32768]{0:T(1024)} collective-permute-done((f32[32768]{0:T(1024)S(1)}, f32[32768]{0:T(1024)}, u32[]{:S(2)}, u32[]{:S(2)}) %collective-permute-start) | collective-permute-done | bytes 131104 | tf_op jit(solution)/shard_map/ppermute | solution.py:136
  15.7 1.0 %add_rsqrt_fusion = f32[32768]{0:T(1024)S(1)} fusion(f32[32768]{0:T(1024)S(1)} %collective-permute-done.2, f32[32768]{0:T(1024)S(1)} %collective-permute-done.1, f32[32768]{0:T(1024)S(1)} %fusion, f32[32768]{0:T(1024)} %collective-permute-done), kind=kLoop, calls=%fused_computation.24 | loop fusion | flops 163840 | bytes 655360 | tf_op jit(solution)/shard_map/sqrt | solution.py:140
  16.6 0.0 copy-done.1
  16.6 1.8 %fusion.5 = (f32[32768]{0:T(1024)S(1)}, f32[32768]{0:T(1024)S(1)}) fusion(bf16[40,32768]{1,0:T(8,128)(2,1)S(1)} %copy-done.1, f32[32768]{0:T(1024)S(1)} %add_rsqrt_fusion, pred[40]{0:T(512)(128)(4,1)S(1)} %get-tuple-element.14, pred[40]{0:T(512)(128)(4,1)S(1)} %get-tuple-element.13), kind=kLoop, calls=%fused_computation.8 | loop fusion | flops 10420224 | bytes 3014736 | tf_op jit(solution)/shard_map/reduce_sum | solution.py:144
  18.5 0.1 collective-permute-start.5
  18.6 0.2 collective-permute-start.4
  18.9 1.2 %collective-permute-start.3 = (bf16[2,64,128]{2,1,0:T(8,128)(2,1)S(1)}, bf16[2,64,128]{2,1,0:T(8,128)(2,1)S(1)}, u32[]{:S(2)}, u32[]{:S(2)}) collective-permute-start(bf16[2,64,128]{2,1,0:T(8,128)(2,1)S(1)} %get-tuple-element.12), channel_id=1, source_target_pairs={{0,1},{1,2},{2,3},{3,0},{4,5},{5,6},{6,7},{7,4},{8,9},{9,10},{10,1... | collective-permute-start | bytes 98312 | tf_op jit(solution)/shard_map/ppermute | solution.py:152
  20.1 0.1 broadcast_in_dim.39
  20.2 0.1 broadcast_in_dim.40
  20.3 1.1 %collective-permute-done.5 = bf16[2,64,128]{2,1,0:T(8,128)(2,1)S(1)} collective-permute-done((bf16[2,64,128]{2,1,0:T(8,128)(2,1)S(1)}, bf16[2,64,128]{2,1,0:T(8,128)(2,1)S(1)}, u32[]{:S(2)}, u32[]{:S(2)}) %collective-permute-start.5) | collective-permute-done | bytes 32800 | tf_op jit(solution)/shard_map/ppermute | solution.py:152
  21.4 1.6 %collective-permute-done.4 = bf16[2,64,128]{2,1,0:T(8,128)(2,1)S(1)} collective-permute-done((bf16[2,64,128]{2,1,0:T(8,128)(2,1)S(1)}, bf16[2,64,128]{2,1,0:T(8,128)(2,1)S(1)}, u32[]{:S(2)}, u32[]{:S(2)}) %collective-permute-start.4) | collective-permute-done | bytes 32800 | tf_op jit(solution)/shard_map/ppermute | solution.py:152
  23.0 0.8 collective-permute-done.3
  23.8 0.6 gather_fusion
  24.4 0.1 copy_select_fusion
  24.5 0.2 convolution_convert_fusion.1
  24.7 0.8 all_to_all.14
  25.5 13.7 %all-to-all-start = ((bf16[64,2,1024]{2,1,0:T(2,128)(2,1)}), bf16[64,2,1024]{2,1,0:T(2,128)(2,1)S(1)}, u32[]{:S(2)}, u32[]{:S(2)}) async-start(bf16[64,2,1024]{2,1,0:T(2,128)(2,1)} %all_to_all.14), calls=%async_computation | async-start | bytes 524288 | tf_op jit(solution)/shard_map/all_to_all | solution.py:172
  39.2 0.0 copy-done
  39.2 4.7 %subtract_convert_fusion = (bf16[128,1536]{1,0:T(8,128)(2,1)}, bf16[128,1536]{1,0:T(8,128)(2,1)}) fusion(bf16[2048,1536]{1,0:T(8,128)(2,1)} %param.9, bf16[1,128,2048]{2,1,0:T(8,128)(2,1)S(1)} %copy-done), kind=kOutput, calls=%fused_computation.14 | convolution fusion | flops 806092800 | bytes 7602176 | tf_op jit(solution)/shard_map/dot_general | solution.py:174
  43.9 7.3 %all-to-all-done = bf16[64,2,1024]{2,1,0:T(2,128)(2,1)S(1)} async-done(((bf16[64,2,1024]{2,1,0:T(2,128)(2,1)}), bf16[64,2,1024]{2,1,0:T(2,128)(2,1)S(1)}, u32[]{:S(2)}, u32[]{:S(2)}) %all-to-all-start) | async-done | bytes 262176 | tf_op jit(solution)/shard_map/all_to_all | solution.py:172
  51.2 0.9 reshape.95.rows_ref
  52.1 7.7 %shard_map.55 = bf16[128,2560]{1,0:T(8,128)(2,1)} custom-call(bf16[1024,128]{1,0:T(8,128)(2,1)} %reshape.95.rows_ref, bf16[128,1536]{1,0:T(8,128)(2,1)} %get-tuple-element.8.hi_ref, bf16[128,1536]{1,0:T(8,128)(2,1)} %get-tuple-element.7.lo_ref), custom_call_target="tpu_custom_call" | custom-call | tf_op jit(solution)/shard_map/pallas_call | solution.py:89
  59.7 2.0 %all_to_all.16 = bf16[64,2,2560]{2,1,0:T(2,128)(2,1)S(1)} reshape(bf16[128,2560]{1,0:T(8,128)(2,1)} %shard_map.55) | data formatting | bytes 1310720 | tf_op jit(solution)/shard_map/all_to_all | solution.py:179
  61.7 25.9 %all_to_all.21 = bf16[64,2,2560]{2,1,0:T(2,128)(2,1)S(1)} all-to-all(bf16[64,2,2560]{2,1,0:T(2,128)(2,1)S(1)} %all_to_all.16), channel_id=1, replica_groups=mesh['wide'=64,'seq'=4] {'wide'}, dimensions={0} | all-to-all | bytes 1310720 | tf_op jit(solution)/shard_map/all_to_all | solution.py:179
  87.6 0.2 all_to_all.18
  87.9 0.3 convolution_convert_fusion
  88.2 0.2 reshape.96
  88.4 0.1 copy.16
  88.5 1.6 %copy.18 = bf16[64,8,2,4,8]{1,4,3,2,0:T(8,128)(2,1)S(1)} copy(bf16[64,8,2,4,8]{0,4,3,2,1:T(8,128)(2,1)S(1)} %bitcast.41) | data formatting | bytes 131072 | tf_op jit(solution)/shard_map/reshape | solution.py:115
  90.1 1.4 %bitcast_convert_fusion = bf16[64,2,128,4,8]{2,4,3,1,0:T(8,128)(2,1)} fusion(bf16[64,8,2,4,8]{1,4,3,2,0:T(8,128)(2,1)S(1)} %copy.18, bf16[64,8,2,128]{3,2,1,0:T(2,128)(2,1)S(1)} %reshape.96), kind=kOutput, calls=%fused_computation.11 | convolution fusion | flops 8912896 | bytes 1376256
  (6 shorter events, 0.1 us)
Async XLA Ops:
  0.0 39.2 %copy-start = (bf16[1,128,2048]{2,1,0:T(8,128)(2,1)S(1)}, bf16[1,128,2048]{2,1,0:T(8,128)(2,1)}, u32[]{:S(2)}) copy-start(bf16[1,128,2048]{2,1,0:T(8,128)(2,1)} %param.8) | copy-start | bytes 1572868
  0.0 16.6 %copy-start.1 = (bf16[40,32768]{1,0:T(8,128)(2,1)S(1)}, bf16[40,32768]{1,0:T(8,128)(2,1)}, u32[]{:S(2)}) copy-start(bf16[40,32768]{1,0:T(8,128)(2,1)} %param.5) | copy-start | bytes 7864324
  2.6 8.1 %collective-permute-start.2 = (f32[32768]{0:T(1024)S(1)}, f32[32768]{0:T(1024)S(1)}, u32[]{:S(2)}, u32[]{:S(2)}) collective-permute-start(f32[32768]{0:T(1024)S(1)} %fusion), channel_id=1, source_target_pairs={{0,3},{1,0},{2,1},{3,2},{4,7},{5,4},{6,5},{7,6},{8,11},{9,8},{10,9... | collective-permute-start | bytes 393224 | tf_op jit(solution)/shard_map/ppermute | solution.py:136
  6.0 5.4 %collective-permute-start.1 = (f32[32768]{0:T(1024)S(1)}, f32[32768]{0:T(1024)S(1)}, u32[]{:S(2)}, u32[]{:S(2)}) collective-permute-start(f32[32768]{0:T(1024)S(1)} %fusion), channel_id=1, source_target_pairs={{0,2},{1,3},{2,0},{3,1},{4,6},{5,7},{6,4},{7,5},{8,10},{9,11},{10,... | collective-permute-start | bytes 393224 | tf_op jit(solution)/shard_map/ppermute | solution.py:136
  6.5 9.2 %collective-permute-start = (f32[32768]{0:T(1024)S(1)}, f32[32768]{0:T(1024)}, u32[]{:S(2)}, u32[]{:S(2)}) collective-permute-start(f32[32768]{0:T(1024)S(1)} %fusion), channel_id=1, source_target_pairs={{0,1},{1,2},{2,3},{3,0},{4,5},{5,6},{6,7},{7,4},{8,9},{9,10},{10,1... | collective-permute-start | bytes 393224 | tf_op jit(solution)/shard_map/ppermute | solution.py:136
  18.5 2.8 %collective-permute-start.5 = (bf16[2,64,128]{2,1,0:T(8,128)(2,1)S(1)}, bf16[2,64,128]{2,1,0:T(8,128)(2,1)S(1)}, u32[]{:S(2)}, u32[]{:S(2)}) collective-permute-start(bf16[2,64,128]{2,1,0:T(8,128)(2,1)S(1)} %get-tuple-element.10), channel_id=1, source_target_pairs={{0,3},{1,0},{2,1},{3,2},{4,7},{5,4},{6,5},{7,6},{8,11},{9,8},{10,9... | collective-permute-start | bytes 98312 | tf_op jit(solution)/shard_map/ppermute | solution.py:152
  18.6 4.4 %collective-permute-start.4 = (bf16[2,64,128]{2,1,0:T(8,128)(2,1)S(1)}, bf16[2,64,128]{2,1,0:T(8,128)(2,1)S(1)}, u32[]{:S(2)}, u32[]{:S(2)}) collective-permute-start(bf16[2,64,128]{2,1,0:T(8,128)(2,1)S(1)} %get-tuple-element.11), channel_id=1, source_target_pairs={{0,2},{1,3},{2,0},{3,1},{4,6},{5,7},{6,4},{7,5},{8,10},{9,11},{10,... | collective-permute-start | bytes 98312 | tf_op jit(solution)/shard_map/ppermute | solution.py:152
  18.9 4.9 %collective-permute-start.3 = (bf16[2,64,128]{2,1,0:T(8,128)(2,1)S(1)}, bf16[2,64,128]{2,1,0:T(8,128)(2,1)S(1)}, u32[]{:S(2)}, u32[]{:S(2)}) collective-permute-start(bf16[2,64,128]{2,1,0:T(8,128)(2,1)S(1)} %get-tuple-element.12), channel_id=1, source_target_pairs={{0,1},{1,2},{2,3},{3,0},{4,5},{5,6},{6,7},{7,4},{8,9},{9,10},{10,1... | collective-permute-start | bytes 98312 | tf_op jit(solution)/shard_map/ppermute | solution.py:152
  25.5 25.7 %all-to-all-start = ((bf16[64,2,1024]{2,1,0:T(2,128)(2,1)}), bf16[64,2,1024]{2,1,0:T(2,128)(2,1)S(1)}, u32[]{:S(2)}, u32[]{:S(2)}) async-start(bf16[64,2,1024]{2,1,0:T(2,128)(2,1)} %all_to_all.14), calls=%async_computation | async-start | bytes 524288 | tf_op jit(solution)/shard_map/all_to_all | solution.py:172

commit v17 on v14

--- a/solution.py
+++ b/solution.py
@@ -13,7 +13,7 @@
 CAP = 2
 BINS = 8
 ROWS = 512
-SUB = 4
+SUB = 8
 
 
 def _owner_kernel(rows_ref, hi_ref, lo_ref, o_ref, w_ref):

time: 91 us -> 90 us (0.989)
  Pallas kernels: 7.52 us -> 6.43 us
    pallas_call x1, Pallas kernels: 7.52 us -> 6.43 us  [owner_payload(): pl.pallas_call(_owner_kernel, out_shape=jax.ShapeDtypeStruct((total, KVH...]
where the time goes in v17:
time: 90 us; the launch traced here: 89.6 us
  blocking collectives  25.9 us (29%)
  starting transfers between devices  19.8 us (22%)
  waiting for transfers between devices  15.8 us (18%)
  other arithmetic  8.32 us (9%)
  local copies, waits for them, and re-layouts  6.64 us (7%)
  matrix products  6.55 us (7%)
  Pallas kernels  6.43 us (7%)
    all_to_all x1, blocking collectives, body(): lax.all_to_all(payload, 'wide', split_axis=0, concat_axis=0, tiled=True)  25.9 us
    all_to_all x1, starting transfers between devices, body(): lax.all_to_all(outgoing, 'wide', split_axis=0, concat_axis=0, tiled=True)  13.7 us
    all_to_all x1, waiting for transfers between devices, body(): lax.all_to_all(outgoing, 'wide', split_axis=0, concat_axis=0, tiled=True)  7.29 us
    pallas_call x1, Pallas kernels, owner_payload(): pl.pallas_call(_owner_kernel, out_shape=jax.ShapeDtypeStruct((total, KVH...  6.43 us
    ppermute x3, waiting for transfers between devices, body(): received.append(lax.ppermute(partial, 'seq', pairs))  4.99 us
    dot_general x1, matrix products, body(): jnp.dot(weight_block, qkv_weight, preferred_element_type=jnp.float32)  4.66 us
    ppermute x3, starting transfers between devices, body(): received.append(lax.ppermute(partial, 'seq', pairs))  4.5 us
    ppermute x3, waiting for transfers between devices, body(): received.append(lax.ppermute(piece, 'seq', pairs))  3.51 us
  transfers between devices with their start and end apart: 7, of which 6 were waited for; matrix products, arithmetic and copies ran while one was open for 9% of the time, Pallas kernels for 0%

profile of v17, /device:TPU:1, one launch (start us, length us, event | category | flops | bytes accessed | tf_op | source)
XLA Modules:
  0.0 89.6 jit_solution(9819587728704687849)
XLA Ops:
  0.0 0.0 copy-start
  0.0 0.0 copy-start.1
  0.0 2.6 %fusion = f32[32768]{0:T(1024)S(1)} fusion(bf16[40,32768]{1,0:T(8,128)(2,1)} %param.5), kind=kLoop, calls=%fused_computation.3 | loop fusion | flops 3899392 | bytes 2752512 | tf_op jit(solution)/shard_map/reduce_sum | solution.py:114
  2.6 3.4 %collective-permute-start.2 = (f32[32768]{0:T(1024)S(1)}, f32[32768]{0:T(1024)S(1)}, u32[]{:S(2)}, u32[]{:S(2)}) collective-permute-start(f32[32768]{0:T(1024)S(1)} %fusion), channel_id=1, source_target_pairs={{0,3},{1,0},{2,1},{3,2},{4,7},{5,4},{6,5},{7,6},{8,11},{9,8},{10,9... | collective-permute-start | bytes 393224 | tf_op jit(solution)/shard_map/ppermute | solution.py:118
  6.0 0.5 collective-permute-start.1
  6.5 0.6 collective-permute-start
  7.1 0.8 dynamic_slice.10
  7.9 0.2 convert_reduce_fusion
  8.1 0.8 multiply_add_fusion
  8.8 0.7 subtract_compare_fusion
  9.5 0.5 fusion.17
  10.0 0.7 pad_clamp_fusion
  10.7 0.0 collective-permute-done.2
  10.7 0.7 collective-permute-done.1
  11.4 4.3 %collective-permute-done = f32[32768]{0:T(1024)} collective-permute-done((f32[32768]{0:T(1024)S(1)}, f32[32768]{0:T(1024)}, u32[]{:S(2)}, u32[]{:S(2)}) %collective-permute-start) | collective-permute-done | bytes 131104 | tf_op jit(solution)/shard_map/ppermute | solution.py:118
  15.7 1.0 %add_rsqrt_fusion = f32[32768]{0:T(1024)S(1)} fusion(f32[32768]{0:T(1024)S(1)} %collective-permute-done.2, f32[32768]{0:T(1024)S(1)} %collective-permute-done.1, f32[32768]{0:T(1024)S(1)} %fusion, f32[32768]{0:T(1024)} %collective-permute-done), kind=kLoop, calls=%fused_computation.23 | loop fusion | flops 163840 | bytes 655360 | tf_op jit(solution)/shard_map/sqrt | solution.py:122
  16.6 0.0 copy-done.1
  16.6 1.8 %fusion.5 = (f32[32768]{0:T(1024)S(1)}, f32[32768]{0:T(1024)S(1)}) fusion(bf16[40,32768]{1,0:T(8,128)(2,1)S(1)} %copy-done.1, f32[32768]{0:T(1024)S(1)} %add_rsqrt_fusion, pred[40]{0:T(512)(128)(4,1)S(1)} %get-tuple-element.14, pred[40]{0:T(512)(128)(4,1)S(1)} %get-tuple-element.13), kind=kLoop, calls=%fused_computation.8 | loop fusion | flops 10420224 | bytes 3014736 | tf_op jit(solution)/shard_map/reduce_sum | solution.py:126
  18.5 0.1 collective-permute-start.5
  18.6 0.2 collective-permute-start.4
  18.9 1.2 %collective-permute-start.3 = (bf16[2,64,128]{2,1,0:T(8,128)(2,1)S(1)}, bf16[2,64,128]{2,1,0:T(8,128)(2,1)S(1)}, u32[]{:S(2)}, u32[]{:S(2)}) collective-permute-start(bf16[2,64,128]{2,1,0:T(8,128)(2,1)S(1)} %get-tuple-element.12), channel_id=1, source_target_pairs={{0,1},{1,2},{2,3},{3,0},{4,5},{5,6},{6,7},{7,4},{8,9},{9,10},{10,1... | collective-permute-start | bytes 98312 | tf_op jit(solution)/shard_map/ppermute | solution.py:134
  20.1 0.1 broadcast_in_dim.39
  20.2 0.1 broadcast_in_dim.40
  20.3 1.1 %collective-permute-done.5 = bf16[2,64,128]{2,1,0:T(8,128)(2,1)S(1)} collective-permute-done((bf16[2,64,128]{2,1,0:T(8,128)(2,1)S(1)}, bf16[2,64,128]{2,1,0:T(8,128)(2,1)S(1)}, u32[]{:S(2)}, u32[]{:S(2)}) %collective-permute-start.5) | collective-permute-done | bytes 32800 | tf_op jit(solution)/shard_map/ppermute | solution.py:134
  21.4 1.6 %collective-permute-done.4 = bf16[2,64,128]{2,1,0:T(8,128)(2,1)S(1)} collective-permute-done((bf16[2,64,128]{2,1,0:T(8,128)(2,1)S(1)}, bf16[2,64,128]{2,1,0:T(8,128)(2,1)S(1)}, u32[]{:S(2)}, u32[]{:S(2)}) %collective-permute-start.4) | collective-permute-done | bytes 32800 | tf_op jit(solution)/shard_map/ppermute | solution.py:134
  23.0 0.8 collective-permute-done.3
  23.8 0.6 gather_fusion
  24.4 0.1 copy_select_fusion
  24.5 0.2 convolution_convert_fusion.1
  24.7 0.8 all_to_all.14
  25.5 13.7 %all-to-all-start = ((bf16[64,2,1024]{2,1,0:T(2,128)(2,1)}), bf16[64,2,1024]{2,1,0:T(2,128)(2,1)S(1)}, u32[]{:S(2)}, u32[]{:S(2)}) async-start(bf16[64,2,1024]{2,1,0:T(2,128)(2,1)} %all_to_all.14), calls=%async_computation | async-start | bytes 524288 | tf_op jit(solution)/shard_map/all_to_all | solution.py:154
  39.2 0.0 copy-done
  39.2 4.7 %subtract_convert_fusion = (bf16[128,1536]{1,0:T(8,128)(2,1)}, bf16[128,1536]{1,0:T(8,128)(2,1)}) fusion(bf16[2048,1536]{1,0:T(8,128)(2,1)} %param.9, bf16[1,128,2048]{2,1,0:T(8,128)(2,1)S(1)} %copy-done), kind=kOutput, calls=%fused_computation.13 | convolution fusion | flops 806092800 | bytes 7602176 | tf_op jit(solution)/shard_map/dot_general | solution.py:156
  43.9 7.3 %all-to-all-done = bf16[64,2,1024]{2,1,0:T(2,128)(2,1)S(1)} async-done(((bf16[64,2,1024]{2,1,0:T(2,128)(2,1)}), bf16[64,2,1024]{2,1,0:T(2,128)(2,1)S(1)}, u32[]{:S(2)}, u32[]{:S(2)}) %all-to-all-start) | async-done | bytes 262176 | tf_op jit(solution)/shard_map/all_to_all | solution.py:154
  51.2 0.9 reshape.100.rows_ref
  52.1 6.4 %shard_map.55 = bf16[1024,320]{1,0:T(8,128)(2,1)} custom-call(bf16[1024,128]{1,0:T(8,128)(2,1)} %reshape.100.rows_ref, bf16[128,1536]{1,0:T(8,128)(2,1)} %get-tuple-element.8.hi_ref, bf16[128,1536]{1,0:T(8,128)(2,1)} %get-tuple-element.7.lo_ref), custom_call_target="tpu_custom_call" | custom-call | tf_op jit(solution)/shard_map/pallas_call | solution.py:79
  58.5 2.4 %all_to_all.16 = bf16[64,2,2560]{2,1,0:T(2,128)(2,1)S(1)} reshape(bf16[1024,320]{1,0:T(8,128)(2,1)} %shard_map.55) | data formatting | bytes 1310720 | tf_op jit(solution)/shard_map/all_to_all | solution.py:161
  60.9 25.9 %all_to_all.21 = bf16[64,2,2560]{2,1,0:T(2,128)(2,1)S(1)} all-to-all(bf16[64,2,2560]{2,1,0:T(2,128)(2,1)S(1)} %all_to_all.16), channel_id=1, replica_groups=mesh['wide'=64,'seq'=4] {'wide'}, dimensions={0} | all-to-all | bytes 1310720 | tf_op jit(solution)/shard_map/all_to_all | solution.py:161
  86.9 0.2 all_to_all.18
  87.1 0.3 convolution_convert_fusion
  87.4 0.3 reshape.101
  87.7 0.5 copy.11
  88.2 1.4 %bitcast_convert_fusion = bf16[64,2,128,4,8]{2,4,3,1,0:T(8,128)(2,1)} fusion(bf16[64,2,8,32]{2,3,1,0:T(8,128)(2,1)S(1)} %bitcast.42, bf16[64,8,320]{2,1,0:T(8,128)(2,1)S(1)} %reshape.101), kind=kOutput, calls=%fused_computation.11 | convolution fusion | flops 8912896 | bytes 2359296
  (5 shorter events, 0.1 us)
Async XLA Ops:
  0.0 39.2 %copy-start = (bf16[1,128,2048]{2,1,0:T(8,128)(2,1)S(1)}, bf16[1,128,2048]{2,1,0:T(8,128)(2,1)}, u32[]{:S(2)}) copy-start(bf16[1,128,2048]{2,1,0:T(8,128)(2,1)} %param.8) | copy-start | bytes 1572868
  0.0 16.6 %copy-start.1 = (bf16[40,32768]{1,0:T(8,128)(2,1)S(1)}, bf16[40,32768]{1,0:T(8,128)(2,1)}, u32[]{:S(2)}) copy-start(bf16[40,32768]{1,0:T(8,128)(2,1)} %param.5) | copy-start | bytes 7864324
  2.6 8.1 %collective-permute-start.2 = (f32[32768]{0:T(1024)S(1)}, f32[32768]{0:T(1024)S(1)}, u32[]{:S(2)}, u32[]{:S(2)}) collective-permute-start(f32[32768]{0:T(1024)S(1)} %fusion), channel_id=1, source_target_pairs={{0,3},{1,0},{2,1},{3,2},{4,7},{5,4},{6,5},{7,6},{8,11},{9,8},{10,9... | collective-permute-start | bytes 393224 | tf_op jit(solution)/shard_map/ppermute | solution.py:118
  6.0 5.4 %collective-permute-start.1 = (f32[32768]{0:T(1024)S(1)}, f32[32768]{0:T(1024)S(1)}, u32[]{:S(2)}, u32[]{:S(2)}) collective-permute-start(f32[32768]{0:T(1024)S(1)} %fusion), channel_id=1, source_target_pairs={{0,2},{1,3},{2,0},{3,1},{4,6},{5,7},{6,4},{7,5},{8,10},{9,11},{10,... | collective-permute-start | bytes 393224 | tf_op jit(solution)/shard_map/ppermute | solution.py:118
  6.5 9.2 %collective-permute-start = (f32[32768]{0:T(1024)S(1)}, f32[32768]{0:T(1024)}, u32[]{:S(2)}, u32[]{:S(2)}) collective-permute-start(f32[32768]{0:T(1024)S(1)} %fusion), channel_id=1, source_target_pairs={{0,1},{1,2},{2,3},{3,0},{4,5},{5,6},{6,7},{7,4},{8,9},{9,10},{10,1... | collective-permute-start | bytes 393224 | tf_op jit(solution)/shard_map/ppermute | solution.py:118
  18.5 2.8 %collective-permute-start.5 = (bf16[2,64,128]{2,1,0:T(8,128)(2,1)S(1)}, bf16[2,64,128]{2,1,0:T(8,128)(2,1)S(1)}, u32[]{:S(2)}, u32[]{:S(2)}) collective-permute-start(bf16[2,64,128]{2,1,0:T(8,128)(2,1)S(1)} %get-tuple-element.10), channel_id=1, source_target_pairs={{0,3},{1,0},{2,1},{3,2},{4,7},{5,4},{6,5},{7,6},{8,11},{9,8},{10,9... | collective-permute-start | bytes 98312 | tf_op jit(solution)/shard_map/ppermute | solution.py:134
  18.6 4.4 %collective-permute-start.4 = (bf16[2,64,128]{2,1,0:T(8,128)(2,1)S(1)}, bf16[2,64,128]{2,1,0:T(8,128)(2,1)S(1)}, u32[]{:S(2)}, u32[]{:S(2)}) collective-permute-start(bf16[2,64,128]{2,1,0:T(8,128)(2,1)S(1)} %get-tuple-element.11), channel_id=1, source_target_pairs={{0,2},{1,3},{2,0},{3,1},{4,6},{5,7},{6,4},{7,5},{8,10},{9,11},{10,... | collective-permute-start | bytes 98312 | tf_op jit(solution)/shard_map/ppermute | solution.py:134
  18.9 4.9 %collective-permute-start.3 = (bf16[2,64,128]{2,1,0:T(8,128)(2,1)S(1)}, bf16[2,64,128]{2,1,0:T(8,128)(2,1)S(1)}, u32[]{:S(2)}, u32[]{:S(2)}) collective-permute-start(bf16[2,64,128]{2,1,0:T(8,128)(2,1)S(1)} %get-tuple-element.12), channel_id=1, source_target_pairs={{0,1},{1,2},{2,3},{3,0},{4,5},{5,6},{6,7},{7,4},{8,9},{9,10},{10,1... | collective-permute-start | bytes 98312 | tf_op jit(solution)/shard_map/ppermute | solution.py:134
  25.5 25.7 %all-to-all-start = ((bf16[64,2,1024]{2,1,0:T(2,128)(2,1)}), bf16[64,2,1024]{2,1,0:T(2,128)(2,1)S(1)}, u32[]{:S(2)}, u32[]{:S(2)}) async-start(bf16[64,2,1024]{2,1,0:T(2,128)(2,1)} %all_to_all.14), calls=%async_computation | async-start | bytes 524288 | tf_op jit(solution)/shard_map/all_to_all | solution.py:154

commit v18 on v17

--- a/solution.py
+++ b/solution.py
@@ -13,7 +13,7 @@
 CAP = 2
 BINS = 8
 ROWS = 512
-SUB = 8
+SUB = 16
 
 
 def _owner_kernel(rows_ref, hi_ref, lo_ref, o_ref, w_ref):

time: 90 us -> 90.9 us (1.010)
  Pallas kernels: 6.43 us -> 7.38 us
    pallas_call x1, Pallas kernels: 6.43 us -> 7.38 us  [owner_payload(): pl.pallas_call(_owner_kernel, out_shape=jax.ShapeDtypeStruct((total, KVH...]
where the time goes in v18:
time: 90.9 us; the launch traced here: 90.5 us
  blocking collectives  25.9 us (28%)
  starting transfers between devices  19.8 us (22%)
  waiting for transfers between devices  15.8 us (17%)
  other arithmetic  8.32 us (9%)
  Pallas kernels  7.38 us (8%)
  local copies, waits for them, and re-layouts  6.64 us (7%)
  matrix products  6.55 us (7%)
    all_to_all x1, blocking collectives, body(): lax.all_to_all(payload, 'wide', split_axis=0, concat_axis=0, tiled=True)  25.9 us
    all_to_all x1, starting transfers between devices, body(): lax.all_to_all(outgoing, 'wide', split_axis=0, concat_axis=0, tiled=True)  13.7 us
    pallas_call x1, Pallas kernels, owner_payload(): pl.pallas_call(_owner_kernel, out_shape=jax.ShapeDtypeStruct((total, KVH...  7.38 us
    all_to_all x1, waiting for transfers between devices, body(): lax.all_to_all(outgoing, 'wide', split_axis=0, concat_axis=0, tiled=True)  7.29 us
    ppermute x3, waiting for transfers between devices, body(): received.append(lax.ppermute(partial, 'seq', pairs))  4.99 us
    dot_general x1, matrix products, body(): jnp.dot(weight_block, qkv_weight, preferred_element_type=jnp.float32)  4.66 us
    ppermute x3, starting transfers between devices, body(): received.append(lax.ppermute(partial, 'seq', pairs))  4.5 us
    ppermute x3, waiting for transfers between devices, body(): received.append(lax.ppermute(piece, 'seq', pairs))  3.51 us
  transfers between devices with their start and end apart: 7, of which 6 were waited for; matrix products, arithmetic and copies ran while one was open for 9% of the time, Pallas kernels for 0%

profile of v18, /device:TPU:1, one launch (start us, length us, event | category | flops | bytes accessed | tf_op | source)
XLA Modules:
  0.0 90.5 jit_solution(5452473119083698825)
XLA Ops:
  0.0 0.0 copy-start
  0.0 0.0 copy-start.1
  0.0 2.6 %fusion = f32[32768]{0:T(1024)S(1)} fusion(bf16[40,32768]{1,0:T(8,128)(2,1)} %param.5), kind=kLoop, calls=%fused_computation.3 | loop fusion | flops 3899392 | bytes 2752512 | tf_op jit(solution)/shard_map/reduce_sum | solution.py:114
  2.6 3.4 %collective-permute-start.2 = (f32[32768]{0:T(1024)S(1)}, f32[32768]{0:T(1024)S(1)}, u32[]{:S(2)}, u32[]{:S(2)}) collective-permute-start(f32[32768]{0:T(1024)S(1)} %fusion), channel_id=1, source_target_pairs={{0,3},{1,0},{2,1},{3,2},{4,7},{5,4},{6,5},{7,6},{8,11},{9,8},{10,9... | collective-permute-start | bytes 393224 | tf_op jit(solution)/shard_map/ppermute | solution.py:118
  6.0 0.5 collective-permute-start.1
  6.5 0.6 collective-permute-start
  7.1 0.8 dynamic_slice.10
  7.9 0.2 convert_reduce_fusion
  8.1 0.8 multiply_add_fusion
  8.8 0.7 subtract_compare_fusion
  9.5 0.5 fusion.17
  10.0 0.7 pad_clamp_fusion
  10.7 0.0 collective-permute-done.2
  10.7 0.7 collective-permute-done.1
  11.4 4.3 %collective-permute-done = f32[32768]{0:T(1024)} collective-permute-done((f32[32768]{0:T(1024)S(1)}, f32[32768]{0:T(1024)}, u32[]{:S(2)}, u32[]{:S(2)}) %collective-permute-start) | collective-permute-done | bytes 131104 | tf_op jit(solution)/shard_map/ppermute | solution.py:118
  15.7 1.0 %add_rsqrt_fusion = f32[32768]{0:T(1024)S(1)} fusion(f32[32768]{0:T(1024)S(1)} %collective-permute-done.2, f32[32768]{0:T(1024)S(1)} %collective-permute-done.1, f32[32768]{0:T(1024)S(1)} %fusion, f32[32768]{0:T(1024)} %collective-permute-done), kind=kLoop, calls=%fused_computation.23 | loop fusion | flops 163840 | bytes 655360 | tf_op jit(solution)/shard_map/sqrt | solution.py:122
  16.6 0.0 copy-done.1
  16.6 1.8 %fusion.5 = (f32[32768]{0:T(1024)S(1)}, f32[32768]{0:T(1024)S(1)}) fusion(bf16[40,32768]{1,0:T(8,128)(2,1)S(1)} %copy-done.1, f32[32768]{0:T(1024)S(1)} %add_rsqrt_fusion, pred[40]{0:T(512)(128)(4,1)S(1)} %get-tuple-element.14, pred[40]{0:T(512)(128)(4,1)S(1)} %get-tuple-element.13), kind=kLoop, calls=%fused_computation.8 | loop fusion | flops 10420224 | bytes 3014736 | tf_op jit(solution)/shard_map/reduce_sum | solution.py:126
  18.5 0.1 collective-permute-start.5
  18.6 0.2 collective-permute-start.4
  18.9 1.2 %collective-permute-start.3 = (bf16[2,64,128]{2,1,0:T(8,128)(2,1)S(1)}, bf16[2,64,128]{2,1,0:T(8,128)(2,1)S(1)}, u32[]{:S(2)}, u32[]{:S(2)}) collective-permute-start(bf16[2,64,128]{2,1,0:T(8,128)(2,1)S(1)} %get-tuple-element.12), channel_id=1, source_target_pairs={{0,1},{1,2},{2,3},{3,0},{4,5},{5,6},{6,7},{7,4},{8,9},{9,10},{10,1... | collective-permute-start | bytes 98312 | tf_op jit(solution)/shard_map/ppermute | solution.py:134
  20.1 0.1 broadcast_in_dim.39
  20.2 0.1 broadcast_in_dim.40
  20.3 1.1 %collective-permute-done.5 = bf16[2,64,128]{2,1,0:T(8,128)(2,1)S(1)} collective-permute-done((bf16[2,64,128]{2,1,0:T(8,128)(2,1)S(1)}, bf16[2,64,128]{2,1,0:T(8,128)(2,1)S(1)}, u32[]{:S(2)}, u32[]{:S(2)}) %collective-permute-start.5) | collective-permute-done | bytes 32800 | tf_op jit(solution)/shard_map/ppermute | solution.py:134
  21.4 1.6 %collective-permute-done.4 = bf16[2,64,128]{2,1,0:T(8,128)(2,1)S(1)} collective-permute-done((bf16[2,64,128]{2,1,0:T(8,128)(2,1)S(1)}, bf16[2,64,128]{2,1,0:T(8,128)(2,1)S(1)}, u32[]{:S(2)}, u32[]{:S(2)}) %collective-permute-start.4) | collective-permute-done | bytes 32800 | tf_op jit(solution)/shard_map/ppermute | solution.py:134
  23.0 0.8 collective-permute-done.3
  23.8 0.6 gather_fusion
  24.4 0.1 copy_select_fusion
  24.5 0.2 convolution_convert_fusion.1
  24.7 0.8 all_to_all.14
  25.5 13.7 %all-to-all-start = ((bf16[64,2,1024]{2,1,0:T(2,128)(2,1)}), bf16[64,2,1024]{2,1,0:T(2,128)(2,1)S(1)}, u32[]{:S(2)}, u32[]{:S(2)}) async-start(bf16[64,2,1024]{2,1,0:T(2,128)(2,1)} %all_to_all.14), calls=%async_computation | async-start | bytes 524288 | tf_op jit(solution)/shard_map/all_to_all | solution.py:154
  39.2 0.0 copy-done
  39.2 4.7 %subtract_convert_fusion = (bf16[128,1536]{1,0:T(8,128)(2,1)}, bf16[128,1536]{1,0:T(8,128)(2,1)}) fusion(bf16[2048,1536]{1,0:T(8,128)(2,1)} %param.9, bf16[1,128,2048]{2,1,0:T(8,128)(2,1)S(1)} %copy-done), kind=kOutput, calls=%fused_computation.13 | convolution fusion | flops 806092800 | bytes 7602176 | tf_op jit(solution)/shard_map/dot_general | solution.py:156
  43.9 7.3 %all-to-all-done = bf16[64,2,1024]{2,1,0:T(2,128)(2,1)S(1)} async-done(((bf16[64,2,1024]{2,1,0:T(2,128)(2,1)}), bf16[64,2,1024]{2,1,0:T(2,128)(2,1)S(1)}, u32[]{:S(2)}, u32[]{:S(2)}) %all-to-all-start) | async-done | bytes 262176 | tf_op jit(solution)/shard_map/all_to_all | solution.py:154
  51.2 0.9 reshape.100.rows_ref
  52.1 7.4 %shard_map.55 = bf16[1024,320]{1,0:T(8,128)(2,1)} custom-call(bf16[1024,128]{1,0:T(8,128)(2,1)} %reshape.100.rows_ref, bf16[128,1536]{1,0:T(8,128)(2,1)} %get-tuple-element.8.hi_ref, bf16[128,1536]{1,0:T(8,128)(2,1)} %get-tuple-element.7.lo_ref), custom_call_target="tpu_custom_call" | custom-call | tf_op jit(solution)/shard_map/pallas_call | solution.py:79
  59.4 2.4 %all_to_all.16 = bf16[64,2,2560]{2,1,0:T(2,128)(2,1)S(1)} reshape(bf16[1024,320]{1,0:T(8,128)(2,1)} %shard_map.55) | data formatting | bytes 1310720 | tf_op jit(solution)/shard_map/all_to_all | solution.py:161
  61.9 25.9 %all_to_all.21 = bf16[64,2,2560]{2,1,0:T(2,128)(2,1)S(1)} all-to-all(bf16[64,2,2560]{2,1,0:T(2,128)(2,1)S(1)} %all_to_all.16), channel_id=1, replica_groups=mesh['wide'=64,'seq'=4] {'wide'}, dimensions={0} | all-to-all | bytes 1310720 | tf_op jit(solution)/shard_map/all_to_all | solution.py:161
  87.8 0.2 all_to_all.18
  88.1 0.3 convolution_convert_fusion
  88.4 0.3 reshape.101
  88.7 0.5 copy.11
  89.2 1.4 %bitcast_convert_fusion = bf16[64,2,128,4,8]{2,4,3,1,0:T(8,128)(2,1)} fusion(bf16[64,2,8,32]{2,3,1,0:T(8,128)(2,1)S(1)} %bitcast.42, bf16[64,8,320]{2,1,0:T(8,128)(2,1)S(1)} %reshape.101), kind=kOutput, calls=%fused_computation.11 | convolution fusion | flops 8912896 | bytes 2359296
  (5 shorter events, 0.1 us)
Async XLA Ops:
  0.0 39.2 %copy-start = (bf16[1,128,2048]{2,1,0:T(8,128)(2,1)S(1)}, bf16[1,128,2048]{2,1,0:T(8,128)(2,1)}, u32[]{:S(2)}) copy-start(bf16[1,128,2048]{2,1,0:T(8,128)(2,1)} %param.8) | copy-start | bytes 1572868
  0.0 16.6 %copy-start.1 = (bf16[40,32768]{1,0:T(8,128)(2,1)S(1)}, bf16[40,32768]{1,0:T(8,128)(2,1)}, u32[]{:S(2)}) copy-start(bf16[40,32768]{1,0:T(8,128)(2,1)} %param.5) | copy-start | bytes 7864324
  2.6 8.1 %collective-permute-start.2 = (f32[32768]{0:T(1024)S(1)}, f32[32768]{0:T(1024)S(1)}, u32[]{:S(2)}, u32[]{:S(2)}) collective-permute-start(f32[32768]{0:T(1024)S(1)} %fusion), channel_id=1, source_target_pairs={{0,3},{1,0},{2,1},{3,2},{4,7},{5,4},{6,5},{7,6},{8,11},{9,8},{10,9... | collective-permute-start | bytes 393224 | tf_op jit(solution)/shard_map/ppermute | solution.py:118
  6.0 5.4 %collective-permute-start.1 = (f32[32768]{0:T(1024)S(1)}, f32[32768]{0:T(1024)S(1)}, u32[]{:S(2)}, u32[]{:S(2)}) collective-permute-start(f32[32768]{0:T(1024)S(1)} %fusion), channel_id=1, source_target_pairs={{0,2},{1,3},{2,0},{3,1},{4,6},{5,7},{6,4},{7,5},{8,10},{9,11},{10,... | collective-permute-start | bytes 393224 | tf_op jit(solution)/shard_map/ppermute | solution.py:118
  6.5 9.2 %collective-permute-start = (f32[32768]{0:T(1024)S(1)}, f32[32768]{0:T(1024)}, u32[]{:S(2)}, u32[]{:S(2)}) collective-permute-start(f32[32768]{0:T(1024)S(1)} %fusion), channel_id=1, source_target_pairs={{0,1},{1,2},{2,3},{3,0},{4,5},{5,6},{6,7},{7,4},{8,9},{9,10},{10,1... | collective-permute-start | bytes 393224 | tf_op jit(solution)/shard_map/ppermute | solution.py:118
  18.5 2.8 %collective-permute-start.5 = (bf16[2,64,128]{2,1,0:T(8,128)(2,1)S(1)}, bf16[2,64,128]{2,1,0:T(8,128)(2,1)S(1)}, u32[]{:S(2)}, u32[]{:S(2)}) collective-permute-start(bf16[2,64,128]{2,1,0:T(8,128)(2,1)S(1)} %get-tuple-element.10), channel_id=1, source_target_pairs={{0,3},{1,0},{2,1},{3,2},{4,7},{5,4},{6,5},{7,6},{8,11},{9,8},{10,9... | collective-permute-start | bytes 98312 | tf_op jit(solution)/shard_map/ppermute | solution.py:134
  18.6 4.4 %collective-permute-start.4 = (bf16[2,64,128]{2,1,0:T(8,128)(2,1)S(1)}, bf16[2,64,128]{2,1,0:T(8,128)(2,1)S(1)}, u32[]{:S(2)}, u32[]{:S(2)}) collective-permute-start(bf16[2,64,128]{2,1,0:T(8,128)(2,1)S(1)} %get-tuple-element.11), channel_id=1, source_target_pairs={{0,2},{1,3},{2,0},{3,1},{4,6},{5,7},{6,4},{7,5},{8,10},{9,11},{10,... | collective-permute-start | bytes 98312 | tf_op jit(solution)/shard_map/ppermute | solution.py:134
  18.9 4.9 %collective-permute-start.3 = (bf16[2,64,128]{2,1,0:T(8,128)(2,1)S(1)}, bf16[2,64,128]{2,1,0:T(8,128)(2,1)S(1)}, u32[]{:S(2)}, u32[]{:S(2)}) collective-permute-start(bf16[2,64,128]{2,1,0:T(8,128)(2,1)S(1)} %get-tuple-element.12), channel_id=1, source_target_pairs={{0,1},{1,2},{2,3},{3,0},{4,5},{5,6},{6,7},{7,4},{8,9},{9,10},{10,1... | collective-permute-start | bytes 98312 | tf_op jit(solution)/shard_map/ppermute | solution.py:134
  25.5 25.7 %all-to-all-start = ((bf16[64,2,1024]{2,1,0:T(2,128)(2,1)}), bf16[64,2,1024]{2,1,0:T(2,128)(2,1)S(1)}, u32[]{:S(2)}, u32[]{:S(2)}) async-start(bf16[64,2,1024]{2,1,0:T(2,128)(2,1)} %all_to_all.14), calls=%async_computation | async-start | bytes 524288 | tf_op jit(solution)/shard_map/all_to_all | solution.py:154

commit v19 on v17

--- a/solution.py
+++ b/solution.py
@@ -132,8 +132,10 @@
         pairs = [(i, (i + shift) % seq_count) for i in range(seq_count)]
         piece = lax.dynamic_index_in_dim(binned, (seq_index + shift) % seq_count, 0, keepdims=False)
         received.append(lax.ppermute(piece, "seq", pairs))
-    order = (seq_index - jnp.arange(seq_count, dtype=jnp.int32)) % seq_count
-    binned = jnp.take(jnp.stack(received), order, axis=0)
+    flipped = jnp.stack(received[::-1])
+    doubled = jnp.concatenate([flipped, flipped], axis=0)
+    start = (seq_count - 1 - seq_index) % seq_count
+    binned = lax.dynamic_slice_in_dim(doubled, start, seq_count, axis=0)
     block_rows = binned.reshape(all_bins, quarter, CH).transpose(1, 0, 2).reshape(
         quarter, all_bins * CH
     )

time: 90 us -> 91.6 us (1.018)
  waiting for transfers between devices: 15.8 us -> 18.4 us
  other arithmetic: 8.32 us -> 7.22 us
    ppermute x3, waiting for transfers between devices: 4.99 us -> 6.95 us  [body(): received.append(lax.ppermute(partial, 'seq', pairs))]
  transfers between devices with their start and end apart: 7 -> 7, of which waited for: 6 -> 6; matrix products, arithmetic and copies ran while one was open for 9% -> 8% of each run, Pallas kernels for 0% -> 0%
where the time goes in v19:
time: 91.6 us; the launch traced here: 91.3 us
  blocking collectives  25.9 us (28%)
  starting transfers between devices  20.1 us (22%)
  waiting for transfers between devices  18.4 us (20%)
  other arithmetic  7.22 us (8%)
  matrix products  6.55 us (7%)
  Pallas kernels  6.44 us (7%)
  local copies, waits for them, and re-layouts  6.43 us (7%)
    all_to_all x1, blocking collectives, body(): lax.all_to_all(payload, 'wide', split_axis=0, concat_axis=0, tiled=True)  25.9 us
    all_to_all x1, starting transfers between devices, body(): lax.all_to_all(outgoing, 'wide', split_axis=0, concat_axis=0, tiled=True)  13.9 us
    all_to_all x1, waiting for transfers between devices, body(): lax.all_to_all(outgoing, 'wide', split_axis=0, concat_axis=0, tiled=True)  7.29 us
    ppermute x3, waiting for transfers between devices, body(): received.append(lax.ppermute(partial, 'seq', pairs))  6.95 us
    pallas_call x1, Pallas kernels, owner_payload(): pl.pallas_call(_owner_kernel, out_shape=jax.ShapeDtypeStruct((total, KVH...  6.44 us
    dot_general x1, matrix products, body(): jnp.dot(weight_block, qkv_weight, preferred_element_type=jnp.float32)  4.66 us
    ppermute x3, starting transfers between devices, body(): received.append(lax.ppermute(partial, 'seq', pairs))  4.5 us
    ppermute x3, waiting for transfers between devices, body(): received.append(lax.ppermute(piece, 'seq', pairs))  4.19 us
  transfers between devices with their start and end apart: 7, of which 6 were waited for; matrix products, arithmetic and copies ran while one was open for 8% of the time, Pallas kernels for 0%

profile of v19, /device:TPU:1, one launch (start us, length us, event | category | flops | bytes accessed | tf_op | source)
XLA Modules:
  0.0 91.3 jit_solution(823960264572481893)
XLA Ops:
  0.0 0.0 copy-start
  0.0 0.0 copy-start.1
  0.0 2.6 %fusion = f32[32768]{0:T(1024)S(1)} fusion(bf16[40,32768]{1,0:T(8,128)(2,1)} %param.5), kind=kLoop, calls=%fused_computation.2 | loop fusion | flops 3899392 | bytes 2752512 | tf_op jit(solution)/shard_map/reduce_sum | solution.py:114
  2.6 3.4 %collective-permute-start.2 = (f32[32768]{0:T(1024)S(1)}, f32[32768]{0:T(1024)S(1)}, u32[]{:S(2)}, u32[]{:S(2)}) collective-permute-start(f32[32768]{0:T(1024)S(1)} %fusion), channel_id=1, source_target_pairs={{0,3},{1,0},{2,1},{3,2},{4,7},{5,4},{6,5},{7,6},{8,11},{9,8},{10,9... | collective-permute-start | bytes 393224 | tf_op jit(solution)/shard_map/ppermute | solution.py:118
  6.0 0.5 collective-permute-start.1
  6.5 0.6 collective-permute-start
  7.1 0.7 subtract_compare_fusion
  7.8 0.8 dynamic_slice.13
  8.5 0.2 convert_reduce_fusion
  8.7 0.9 collective-permute-done.2
  9.6 1.8 %collective-permute-done.1 = f32[32768]{0:T(1024)S(1)} collective-permute-done((f32[32768]{0:T(1024)S(1)}, f32[32768]{0:T(1024)S(1)}, u32[]{:S(2)}, u32[]{:S(2)}) %collective-permute-start.1) | collective-permute-done | bytes 131104 | tf_op jit(solution)/shard_map/ppermute | solution.py:118
  11.4 4.3 %collective-permute-done = f32[32768]{0:T(1024)} collective-permute-done((f32[32768]{0:T(1024)S(1)}, f32[32768]{0:T(1024)}, u32[]{:S(2)}, u32[]{:S(2)}) %collective-permute-start) | collective-permute-done | bytes 131104 | tf_op jit(solution)/shard_map/ppermute | solution.py:118
  15.7 0.9 %add_rsqrt_fusion = f32[32768]{0:T(1024)S(1)} fusion(f32[32768]{0:T(1024)S(1)} %collective-permute-done.2, f32[32768]{0:T(1024)S(1)} %collective-permute-done.1, f32[32768]{0:T(1024)S(1)} %fusion, f32[32768]{0:T(1024)} %collective-permute-done), kind=kLoop, calls=%fused_computation.20 | loop fusion | flops 163840 | bytes 655360 | tf_op jit(solution)/shard_map/sqrt | solution.py:122
  16.6 0.0 copy-done.1
  16.6 1.8 %fusion.5 = (f32[32768]{0:T(1024)S(1)}, f32[32768]{0:T(1024)S(1)}) fusion(bf16[40,32768]{1,0:T(8,128)(2,1)S(1)} %copy-done.1, f32[32768]{0:T(1024)S(1)} %add_rsqrt_fusion, pred[40]{0:T(512)(128)(4,1)S(1)} %get-tuple-element.13, pred[40]{0:T(512)(128)(4,1)S(1)} %get-tuple-element.12), kind=kLoop, calls=%fused_computation.7 | loop fusion | flops 10420224 | bytes 3014736 | tf_op jit(solution)/shard_map/reduce_sum | solution.py:126
  18.4 0.3 fusion.9
  18.7 0.1 dynamic-slice_bitcast_fusion
  18.8 0.1 collective-permute-start.3
  18.9 0.8 multiply_add_fusion
  19.6 1.4 %collective-permute-start.5 = (bf16[2,64,128]{2,0,1:T(2,128)(2,1)S(1)}, bf16[2,64,128]{2,0,1:T(2,128)(2,1)S(1)}, u32[]{:S(2)}, u32[]{:S(2)}) collective-permute-start(bf16[2,64,128]{2,0,1:T(2,128)(2,1)S(1)} %get-tuple-element.9), channel_id=1, source_target_pairs={{0,1},{1,2},{2,3},{3,0},{4,5},{5,6},{6,7},{7,4},{8,9},{9,10},{10,1... | collective-permute-start | bytes 98312 | tf_op jit(solution)/shard_map/ppermute | solution.py:134
  21.1 0.2 collective-permute-start.4
  21.2 0.4 collective-permute-done.3
  21.7 3.8 %collective-permute-done.4 = bf16[2,64,128]{2,0,1:T(2,128)(2,1)S(1)} collective-permute-done((bf16[2,64,128]{2,0,1:T(2,128)(2,1)S(1)}, bf16[2,64,128]{2,0,1:T(2,128)(2,1)S(1)}, u32[]{:S(2)}, u32[]{:S(2)}) %collective-permute-start.4) | collective-permute-done | bytes 32800 | tf_op jit(solution)/shard_map/ppermute | solution.py:134
  25.5 0.0 collective-permute-done.5
  25.6 0.1 bitcast_dynamic-update-slice_fusion
  25.8 0.1 bitcast_dynamic-update-slice_fusion.1
  25.9 0.1 constant_dynamic-slice_fusion
  26.0 0.2 convolution_convert_fusion.1
  26.2 0.8 all_to_all.14
  27.0 13.9 %all-to-all-start = ((bf16[64,2,1024]{2,1,0:T(2,128)(2,1)}), bf16[64,2,1024]{2,1,0:T(2,128)(2,1)S(1)}, u32[]{:S(2)}, u32[]{:S(2)}) async-start(bf16[64,2,1024]{2,1,0:T(2,128)(2,1)} %all_to_all.14), calls=%async_computation | async-start | bytes 524288 | tf_op jit(solution)/shard_map/all_to_all | solution.py:156
  40.9 0.0 copy-done
  40.9 4.7 %subtract_convert_fusion = (bf16[128,1536]{1,0:T(8,128)(2,1)}, bf16[128,1536]{1,0:T(8,128)(2,1)}) fusion(bf16[2048,1536]{1,0:T(8,128)(2,1)} %param.9, bf16[1,128,2048]{2,1,0:T(8,128)(2,1)S(1)} %copy-done), kind=kOutput, calls=%fused_computation.12 | convolution fusion | flops 806092800 | bytes 7602176 | tf_op jit(solution)/shard_map/dot_general | solution.py:158
  45.6 7.3 %all-to-all-done = bf16[64,2,1024]{2,1,0:T(2,128)(2,1)S(1)} async-done(((bf16[64,2,1024]{2,1,0:T(2,128)(2,1)}), bf16[64,2,1024]{2,1,0:T(2,128)(2,1)S(1)}, u32[]{:S(2)}, u32[]{:S(2)}) %all-to-all-start) | async-done | bytes 262176 | tf_op jit(solution)/shard_map/all_to_all | solution.py:156
  52.9 0.9 reshape.47.rows_ref
  53.8 6.4 %shard_map.55 = bf16[1024,320]{1,0:T(8,128)(2,1)} custom-call(bf16[1024,128]{1,0:T(8,128)(2,1)} %reshape.47.rows_ref, bf16[128,1536]{1,0:T(8,128)(2,1)} %get-tuple-element.8.hi_ref, bf16[128,1536]{1,0:T(8,128)(2,1)} %get-tuple-element.7.lo_ref), custom_call_target="tpu_custom_call" | custom-call | tf_op jit(solution)/shard_map/pallas_call | solution.py:79
  60.2 2.4 %all_to_all.16 = bf16[64,2,2560]{2,1,0:T(2,128)(2,1)S(1)} reshape(bf16[1024,320]{1,0:T(8,128)(2,1)} %shard_map.55) | data formatting | bytes 1310720 | tf_op jit(solution)/shard_map/all_to_all | solution.py:163
  62.6 25.9 %all_to_all.21 = bf16[64,2,2560]{2,1,0:T(2,128)(2,1)S(1)} all-to-all(bf16[64,2,2560]{2,1,0:T(2,128)(2,1)S(1)} %all_to_all.16), channel_id=1, replica_groups=mesh['wide'=64,'seq'=4] {'wide'}, dimensions={0} | all-to-all | bytes 1310720 | tf_op jit(solution)/shard_map/all_to_all | solution.py:163
  88.5 0.2 all_to_all.18
  88.8 0.3 convolution_convert_fusion
  89.1 0.3 reshape.48
  89.4 0.5 copy.8
  89.9 1.4 %bitcast_convert_fusion = bf16[64,2,128,4,8]{2,4,3,1,0:T(8,128)(2,1)} fusion(bf16[64,2,8,32]{2,3,1,0:T(8,128)(2,1)S(1)} %bitcast.48, bf16[64,8,320]{2,1,0:T(8,128)(2,1)S(1)} %reshape.48), kind=kOutput, calls=%fused_computation.10 | convolution fusion | flops 8912896 | bytes 2359296
  (7 shorter events, 0.3 us)
Async XLA Ops:
  0.0 40.9 %copy-start = (bf16[1,128,2048]{2,1,0:T(8,128)(2,1)S(1)}, bf16[1,128,2048]{2,1,0:T(8,128)(2,1)}, u32[]{:S(2)}) copy-start(bf16[1,128,2048]{2,1,0:T(8,128)(2,1)} %param.8) | copy-start | bytes 1572868
  0.0 16.6 %copy-start.1 = (bf16[40,32768]{1,0:T(8,128)(2,1)S(1)}, bf16[40,32768]{1,0:T(8,128)(2,1)}, u32[]{:S(2)}) copy-start(bf16[40,32768]{1,0:T(8,128)(2,1)} %param.5) | copy-start | bytes 7864324
  2.6 7.0 %collective-permute-start.2 = (f32[32768]{0:T(1024)S(1)}, f32[32768]{0:T(1024)S(1)}, u32[]{:S(2)}, u32[]{:S(2)}) collective-permute-start(f32[32768]{0:T(1024)S(1)} %fusion), channel_id=1, source_target_pairs={{0,3},{1,0},{2,1},{3,2},{4,7},{5,4},{6,5},{7,6},{8,11},{9,8},{10,9... | collective-permute-start | bytes 393224 | tf_op jit(solution)/shard_map/ppermute | solution.py:118
  6.0 5.4 %collective-permute-start.1 = (f32[32768]{0:T(1024)S(1)}, f32[32768]{0:T(1024)S(1)}, u32[]{:S(2)}, u32[]{:S(2)}) collective-permute-start(f32[32768]{0:T(1024)S(1)} %fusion), channel_id=1, source_target_pairs={{0,2},{1,3},{2,0},{3,1},{4,6},{5,7},{6,4},{7,5},{8,10},{9,11},{10,... | collective-permute-start | bytes 393224 | tf_op jit(solution)/shard_map/ppermute | solution.py:118
  6.5 9.2 %collective-permute-start = (f32[32768]{0:T(1024)S(1)}, f32[32768]{0:T(1024)}, u32[]{:S(2)}, u32[]{:S(2)}) collective-permute-start(f32[32768]{0:T(1024)S(1)} %fusion), channel_id=1, source_target_pairs={{0,1},{1,2},{2,3},{3,0},{4,5},{5,6},{6,7},{7,4},{8,9},{9,10},{10,1... | collective-permute-start | bytes 393224 | tf_op jit(solution)/shard_map/ppermute | solution.py:118
  18.8 2.8 %collective-permute-start.3 = (bf16[2,64,128]{2,0,1:T(2,128)(2,1)S(1)}, bf16[2,64,128]{2,0,1:T(2,128)(2,1)S(1)}, u32[]{:S(2)}, u32[]{:S(2)}) collective-permute-start(bf16[2,64,128]{2,0,1:T(2,128)(2,1)S(1)} %get-tuple-element.11), channel_id=1, source_target_pairs={{0,3},{1,0},{2,1},{3,2},{4,7},{5,4},{6,5},{7,6},{8,11},{9,8},{10,9... | collective-permute-start | bytes 98312 | tf_op jit(solution)/shard_map/ppermute | solution.py:134
  19.6 5.9 %collective-permute-start.5 = (bf16[2,64,128]{2,0,1:T(2,128)(2,1)S(1)}, bf16[2,64,128]{2,0,1:T(2,128)(2,1)S(1)}, u32[]{:S(2)}, u32[]{:S(2)}) collective-permute-start(bf16[2,64,128]{2,0,1:T(2,128)(2,1)S(1)} %get-tuple-element.9), channel_id=1, source_target_pairs={{0,1},{1,2},{2,3},{3,0},{4,5},{5,6},{6,7},{7,4},{8,9},{9,10},{10,1... | collective-permute-start | bytes 98312 | tf_op jit(solution)/shard_map/ppermute | solution.py:134
  21.1 4.4 %collective-permute-start.4 = (bf16[2,64,128]{2,0,1:T(2,128)(2,1)S(1)}, bf16[2,64,128]{2,0,1:T(2,128)(2,1)S(1)}, u32[]{:S(2)}, u32[]{:S(2)}) collective-permute-start(bf16[2,64,128]{2,0,1:T(2,128)(2,1)S(1)} %get-tuple-element.10), channel_id=1, source_target_pairs={{0,2},{1,3},{2,0},{3,1},{4,6},{5,7},{6,4},{7,5},{8,10},{9,11},{10,... | collective-permute-start | bytes 98312 | tf_op jit(solution)/shard_map/ppermute | solution.py:134
  27.0 25.9 %all-to-all-start = ((bf16[64,2,1024]{2,1,0:T(2,128)(2,1)}), bf16[64,2,1024]{2,1,0:T(2,128)(2,1)S(1)}, u32[]{:S(2)}, u32[]{:S(2)}) async-start(bf16[64,2,1024]{2,1,0:T(2,128)(2,1)} %all_to_all.14), calls=%async_computation | async-start | bytes 524288 | tf_op jit(solution)/shard_map/all_to_all | solution.py:156
